TPU v7x, 128 devices: a whole 4x4x4 slice. The times are simulated.
128 devices in a mesh: row: 8 (over x, z_lo), col: 16 (over y, z_hi, core).
Axes of the slice: x: 4, y: 4, z: 4 (z_hi: 2, z_lo: 2; z = z_hi * 2 + z_lo), core: 2. Of those that a mesh axis runs over, the one named last changes fastest.
Arguments:
- points: float32 [65536, 64], P(('row', 'col')), may hold values from -6 to 6
- feature_scales: float32 [64], replicated, may hold values from 0.06 to 0.25
- amplitude: float32 [1], replicated, may hold values from 1 to 3
- ridge: float32 [1], replicated, may hold values from 0.5 to 2
Outputs:
- factored: float32 [6, 16, 16, 8, 8192], P(None, 'col', None, 'row')
All inputs are finite; a program needn't handle non-finite values.
Results may differ from a plain program's by a relative error of at most 0.0009.
The roundings to bfloat16 on the way count: a program that leaves them out, or rounds other values in their place, can miss the bound.
Values may be sent and summed in bfloat16 or wider, within the bound.
No kernel may reach another device: no remote copies, remote signals or barrier semaphores. Data moves between devices by JAX's collectives and lax.ppermute only.
A program may use at most 128 MiB of HBM per device.

v0:
```python
import jax
import jax.numpy as jnp
from jax import lax
from jax.sharding import PartitionSpec as P

FEAT = 64
SLAB = 1536
PANEL = 256
BLK = 16

HIGHEST = lax.Precision.HIGHEST


def kernel_block(left, left_norms, right, right_norms, signal):
    cross = jnp.dot(left, right.T, precision=HIGHEST, preferred_element_type=jnp.float32)
    return signal * jnp.exp(-0.5 * (left_norms[:, None] + right_norms[None, :] - 2.0 * cross))


def lower_inverse(block):
    factor = jnp.linalg.cholesky(block)
    identity = jnp.eye(block.shape[0], dtype=jnp.float32)
    return lax.linalg.triangular_solve(factor, identity, left_side=True, lower=True)


def ridge_where(row_ids, col_ids, jitter):
    return jnp.where(row_ids[:, None] == col_ids[None, :], jitter, jnp.float32(0.0))


def gather_by_all_to_all(piece, axis_name):
    count = lax.axis_size(axis_name)
    copies = jnp.broadcast_to(piece[None], (count,) + piece.shape)
    return lax.all_to_all(copies, axis_name, 0, 0, tiled=True)


def on_device(points, feature_scales, amplitude, ridge):
    row_count = lax.axis_size("row")
    col_count = lax.axis_size("col")
    row = lax.axis_index("row")
    column = lax.axis_index("col")
    rows_one = points.shape[0]
    block_rows = rows_one // row_count
    col_blocks = SLAB // (BLK * col_count)
    panel_blocks = PANEL // (BLK * col_count)
    center_sources = SLAB // rows_one
    signal = amplitude[0]
    jitter = ridge[0]

    blocks = points.reshape(row_count, block_rows, FEAT)
    moved = lax.all_to_all(blocks, "row", 0, 0, tiled=True)

    first_slot = gather_by_all_to_all(moved[0], "col")[:center_sources]
    center_grid = gather_by_all_to_all(first_slot, "row")
    centers = center_grid.transpose(1, 0, 2, 3).reshape(SLAB, FEAT)

    moved, centers = lax.optimization_barrier((moved, centers))
    gathered = lax.all_gather(moved, "col", axis=0, tiled=False)
    row_points = gathered.transpose(1, 0, 2, 3).reshape(-1, FEAT)
    grid_rows = row_points.shape[0]

    center_scaled = centers * feature_scales
    center_norms = jnp.sum(center_scaled * center_scaled, axis=1)
    point_scaled = row_points * feature_scales
    point_norms = jnp.sum(point_scaled * point_scaled, axis=1)

    point_ids = (
        lax.broadcasted_iota(jnp.int32, (grid_rows // block_rows, block_rows), 0) * row_count
        + row
    ) * block_rows + lax.broadcasted_iota(jnp.int32, (grid_rows // block_rows, block_rows), 1)
    point_ids = point_ids.reshape(grid_rows)

    own_ids = (
        (
            lax.broadcasted_iota(jnp.int32, (col_blocks, BLK), 0) * col_count + column
        )
        * BLK
        + lax.broadcasted_iota(jnp.int32, (col_blocks, BLK), 1)
    )[2 * panel_blocks :].reshape(-1)
    own_scaled = jnp.take(center_scaled, own_ids, axis=0)
    own_norms = jnp.take(center_norms, own_ids, axis=0)

    lead_ids = jnp.arange(PANEL, dtype=jnp.int32)
    k11 = kernel_block(
        center_scaled[:PANEL], center_norms[:PANEL], center_scaled[:PANEL], center_norms[:PANEL], signal
    ) + ridge_where(lead_ids, lead_ids, jitter)
    first_inverse = lower_inverse(k11)
    used_ids = jnp.concatenate([jnp.arange(PANEL, 2 * PANEL, dtype=jnp.int32), own_ids])
    used_scaled = jnp.concatenate([center_scaled[PANEL : 2 * PANEL], own_scaled])
    used_norms = jnp.concatenate([center_norms[PANEL : 2 * PANEL], own_norms])
    used_kernel = kernel_block(
        used_scaled, used_norms, center_scaled[: 2 * PANEL], center_norms[: 2 * PANEL], signal
    ) + ridge_where(used_ids, jnp.arange(2 * PANEL, dtype=jnp.int32), jitter)
    center_first = jnp.dot(
        used_kernel[:, :PANEL], first_inverse.T, precision=HIGHEST, preferred_element_type=jnp.float32
    ).astype(jnp.bfloat16)
    first_mid = center_first[:PANEL]
    center_second = used_kernel[:, PANEL:] - jnp.dot(
        center_first, first_mid.T, preferred_element_type=jnp.float32
    )
    second_inverse = lower_inverse(center_second[:PANEL])
    second_own = jnp.dot(
        center_second[PANEL:], second_inverse.T, precision=HIGHEST, preferred_element_type=jnp.float32
    ).astype(jnp.bfloat16)
    own_panels = jnp.concatenate([center_first[PANEL:], second_own], axis=1)

    panel_kernel = kernel_block(
        center_scaled[: 2 * PANEL], center_norms[: 2 * PANEL], point_scaled, point_norms, signal
    ) + ridge_where(jnp.arange(2 * PANEL, dtype=jnp.int32), point_ids, jitter)
    first_panel = jnp.dot(
        first_inverse, panel_kernel[:PANEL], precision=HIGHEST, preferred_element_type=jnp.float32
    ).astype(jnp.bfloat16)
    reduced = panel_kernel[PANEL:] - jnp.dot(first_mid, first_panel, preferred_element_type=jnp.float32)
    second_panel = jnp.dot(
        second_inverse, reduced, precision=HIGHEST, preferred_element_type=jnp.float32
    ).astype(jnp.bfloat16)
    panels = jnp.concatenate([first_panel, second_panel], axis=0)

    own_kernel = kernel_block(own_scaled, own_norms, point_scaled, point_norms, signal) + ridge_where(
        own_ids, point_ids, jitter
    )
    trailing = own_kernel - jnp.dot(own_panels, panels, preferred_element_type=jnp.float32)

    own_first = lax.dynamic_slice_in_dim(first_panel, column * BLK, BLK, 0)
    own_second = lax.dynamic_slice_in_dim(second_panel, column * BLK, BLK, 0)
    finished = jnp.concatenate(
        [own_first.astype(jnp.float32), own_second.astype(jnp.float32), trailing], axis=0
    )
    return finished.reshape(col_blocks, 1, BLK, 1, grid_rows)


def solution(mesh):
    placed = (P(("row", "col"), None), P(), P(), P())
    return jax.shard_map(
        on_device,
        mesh=mesh,
        in_specs=placed,
        out_specs=P(None, "col", None, "row", None),
        check_vma=False,
    )
```

profile of v0, /device:TPU:1, one launch (start us, length us, event | category | flops | bytes accessed | tf_op | source)
XLA Modules:
  0.0 252.0 jit_solution(7890708759829238661)
XLA Ops:
  6.5 1.0 copy.40
  7.6 0.8 reshape.168
  8.4 6.2 %all-to-all-start = ((f32[8,1,4096]{2,1,0:T(1,128)}), f32[8,1,4096]{2,1,0:T(1,128)S(1)}, u32[]{:S(2)}, u32[]{:S(2)}) async-start(f32[8,1,4096]{2,1,0:T(1,128)} %reshape.168), calls=%async_computation | async-start | bytes 262144 | tf_op jit(solution)/shard_map/all_to_all | solution.py:49
  14.8 5.1 %all-to-all-done = f32[8,1,4096]{2,1,0:T(1,128)S(1)} async-done(((f32[8,1,4096]{2,1,0:T(1,128)}), f32[8,1,4096]{2,1,0:T(1,128)S(1)}, u32[]{:S(2)}, u32[]{:S(2)}) %all-to-all-start) | async-done | bytes 131104 | tf_op jit(solution)/shard_map/all_to_all | solution.py:49
  19.9 0.5 broadcast.191
  20.4 0.9 reduce.9
  21.5 1.0 reshape.170
  22.6 9.6 %all-to-all-start.1 = ((f32[16,1,4096]{2,1,0:T(1,128)}), f32[16,1,4096]{2,1,0:T(1,128)S(1)}, u32[]{:S(2)}, u32[]{:S(2)}) async-start(f32[16,1,4096]{2,1,0:T(1,128)} %reshape.170), calls=%async_computation.1 | async-start | bytes 524288 | tf_op jit(solution)/shard_map/all_to_all | solution.py:32
  32.3 8.8 %all-to-all-done.1 = f32[16,1,4096]{2,1,0:T(1,128)S(1)} async-done(((f32[16,1,4096]{2,1,0:T(1,128)}), f32[16,1,4096]{2,1,0:T(1,128)S(1)}, u32[]{:S(2)}, u32[]{:S(2)}) %all-to-all-start.1) | async-done | bytes 262176 | tf_op jit(solution)/shard_map/all_to_all | solution.py:32
  41.1 1.2 reduce.10
  42.3 0.2 reshape.171
  42.6 1.2 reshape.172
  43.9 3.5 %all-to-all-start.2 = ((f32[8,1,12288]{2,1,0:T(1,128)}), f32[8,1,12288]{2,1,0:T(1,128)S(1)}, u32[]{:S(2)}, u32[]{:S(2)}) async-start(f32[8,1,12288]{2,1,0:T(1,128)} %reshape.172), calls=%async_computation.2 | async-start | bytes 786432 | tf_op jit(solution)/shard_map/all_to_all | solution.py:32
  49.1 6.2 %all-to-all-done.2 = f32[8,1,12288]{2,1,0:T(1,128)S(1)} async-done(((f32[8,1,12288]{2,1,0:T(1,128)}), f32[8,1,12288]{2,1,0:T(1,128)S(1)}, u32[]{:S(2)}, u32[]{:S(2)}) %all-to-all-start.2) | async-done | bytes 393248 | tf_op jit(solution)/shard_map/all_to_all | solution.py:32
  55.3 1.6 reduce.11
  56.9 0.3 reshape.173
  57.3 0.3 multiply_reduce_fusion.1
  57.6 0.8 gather_fusion
  58.4 0.6 gather_fusion.1
  59.1 0.4 fusion.20
  59.7 11.7 %cholesky.130 = f32[128,128]{1,0:T(8,128)S(1)} custom-call(f32[128,128]{1,0:T(8,128)S(1)} %cholesky.194), custom_call_target="Cholesky" | custom-call | tf_op jit(solution)/shard_map/jit(cholesky)/cholesky | solution.py:20
  71.4 9.8 %custom-call.13 = f32[1,128,128]{1,2,0:T(8,128)S(1)} custom-call(f32[1,128,128]{2,1,0:T(8,128)S(1)} %get-tuple-element.58), custom_call_target="InvertDiagBlocksLowerTriangular" | custom-call | tf_op jit(solution)/shard_map/jit(cholesky)/cholesky | solution.py:20
  81.5 0.3 convolution_subtract_fusion.6
  81.8 11.9 %cholesky.147 = f32[128,128]{1,0:T(8,128)S(1)} custom-call(f32[128,128]{1,0:T(8,128)S(1)} %convolution_subtract_fusion.6), custom_call_target="Cholesky" | custom-call | tf_op jit(solution)/shard_map/jit(cholesky)/cholesky | solution.py:20
  93.7 0.7 compare_reduce_fusion.2
  95.8 4.0 %while.4 = (s32[]{:T(128)}, f32[256,256]{1,0:T(8,128)S(1)}, s32[2,2]{1,0:T(2,128)S(1)}, f32[2,128,128]{2,1,0:T(8,128)S(1)}, s32[]{:T(128)}) while((s32[]{:T(128)}, f32[256,256]{1,0:T(8,128)S(1)}, s32[2,2]{1,0:T(2,128)S(1)}, f32[2,128,128]{2,1,0:T(8,128)S(1)}, s32[]{:T(128)}) %tuple.48), condition=%wide.while_cond, body=%wide.while_body.sunk | while | flops 2 | bytes 131189 | solution.py:22
  95.9 0.6 fusion.77
  96.5 1.4 bitcast_dynamic-update-slice_fusion.4
  97.8 0.6 fusion.77
  98.4 1.4 bitcast_dynamic-update-slice_fusion.4
  99.8 19.7 %custom-call.14 = f32[2,128,128]{1,2,0:T(8,128)S(1)} custom-call(f32[2,128,128]{2,1,0:T(8,128)S(1)} %get-tuple-element.25), custom_call_target="InvertDiagBlocksLowerTriangular" | custom-call | tf_op jit(solution)/shard_map/triangular_solve/custom-call.0 | solution.py:22
  119.5 0.3 fusion.36
  119.8 0.4 convolution_subtract_fusion.4
  120.2 0.3 fusion.45
  120.6 1.0 fusion.15
  121.6 0.8 convolution_convert_fusion.2
  122.5 0.2 convolution_subtract_fusion.2
  122.9 11.7 %cholesky.164 = f32[128,128]{1,0:T(8,128)S(1)} custom-call(f32[128,128]{1,0:T(8,128)S(1)} %cholesky.197), custom_call_target="Cholesky" | custom-call | tf_op jit(solution)/shard_map/jit(cholesky)/cholesky | solution.py:20
  134.7 9.8 %custom-call.15 = f32[1,128,128]{1,2,0:T(8,128)S(1)} custom-call(f32[1,128,128]{2,1,0:T(8,128)S(1)} %get-tuple-element.54), custom_call_target="InvertDiagBlocksLowerTriangular" | custom-call | tf_op jit(solution)/shard_map/jit(cholesky)/cholesky | solution.py:20
  144.7 0.3 convolution_subtract_fusion.5
  145.0 12.1 %cholesky.181 = f32[128,128]{1,0:T(8,128)S(1)} custom-call(f32[128,128]{1,0:T(8,128)S(1)} %convolution_subtract_fusion.5), custom_call_target="Cholesky" | custom-call | tf_op jit(solution)/shard_map/jit(cholesky)/cholesky | solution.py:20
  157.1 0.6 compare_reduce_fusion.1
  157.8 0.6 compare_reduce_fusion
  159.6 3.6 %while.5 = (s32[]{:T(128)}, f32[256,256]{1,0:T(8,128)S(1)}, s32[2,2]{1,0:T(2,128)S(1)}, f32[2,128,128]{2,1,0:T(8,128)S(1)}, s32[]{:T(128)}) while((s32[]{:T(128)}, f32[256,256]{1,0:T(8,128)S(1)}, s32[2,2]{1,0:T(2,128)S(1)}, f32[2,128,128]{2,1,0:T(8,128)S(1)}, s32[]{:T(128)}) %tuple.56), condition=%wide.while_cond.clone, body=%wide.while_body.clone.sunk | while | flops 2 | bytes 131189 | solution.py:22
  159.6 0.6 fusion.78
  160.2 1.2 bitcast_dynamic-update-slice_fusion.5
  161.4 0.6 fusion.78
  162.0 1.2 bitcast_dynamic-update-slice_fusion.5
  163.2 19.7 %custom-call.16 = f32[2,128,128]{1,2,0:T(8,128)S(1)} custom-call(f32[2,128,128]{2,1,0:T(8,128)S(1)} %get-tuple-element.26), custom_call_target="InvertDiagBlocksLowerTriangular" | custom-call | tf_op jit(solution)/shard_map/triangular_solve/custom-call.0 | solution.py:22
  182.9 0.3 fusion.34
  183.2 0.4 convolution_subtract_fusion.3
  183.6 0.3 fusion.41
  183.9 1.0 convolution_convert_fusion.3
  184.9 3.3 %multiply_reduce_fusion = f32[8,16,64]{2,0,1:T(8,128)S(1)} fusion(f32[8,16,64,64]{3,2,0,1:T(8,128)} %bitcast.91, f32[64]{0:T(128)S(1)} %copy-done.6), kind=kLoop, calls=%fused_computation.22 | loop fusion | flops 1564672 | bytes 2130176 | tf_op jit(solution)/shard_map/reduce_sum | solution.py:63
  188.3 5.7 %copy.46 = f32[8,16,64,64]{2,1,0,3:T(8,128)} copy(f32[8,16,64,64]{3,2,0,1:T(8,128)} %bitcast.92) | data formatting | bytes 4194304 | tf_op jit(solution)/shard_map/transpose | solution.py:57
  194.0 3.7 %reshape.119 = f32[8192,64]{0,1:T(8,128)S(1)} reshape(f32[8,16,64,64]{2,1,0,3:T(8,128)} %copy.46) | data formatting | bytes 4194304 | tf_op jit(solution)/shard_map/reshape | solution.py:57
  197.8 20.1 %select_add_fusion = f32[512,8192]{1,0:T(8,128)S(1)} fusion(f32[]{:T(128)} %bitcast.88, s32[8192]{0:T(1024)S(1)} %add.164, f32[8192]{0:T(1024)S(1)} %add.158, f32[512]{0:T(512)S(1)} %copy-done.8, f32[]{:T(128)} %bitcast.84, f32[8192,64]{0,1:T(8,128)S(1)} %reshape.119, f32[64]{0:T(128)S(1)} %copy-done.6, f32[1536,64]{1,0:T(8,128)} %copy-done.1), kind=kOutput, calls=%fused_computation.6 | convolution fusion | flops 3255304192 | bytes 19205376 | tf_op jit(solution)/shard_map/dot_general | solution.py:15
  217.9 8.1 %convolution_convert_fusion.1 = bf16[256,8192]{1,0:T(8,128)(2,1)S(1)} fusion(f32[512,8192]{1,0:T(8,128)S(1)} %select_add_fusion, f32[128,256]{1,0:T(8,128)S(1)} %copy-done.4, f32[128,256]{1,0:T(8,128)S(1)} %fusion.36), kind=kOutput, calls=%fused_computation.10 | convolution fusion | flops 6444613632 | bytes 12845056 | tf_op jit(solution)/shard_map/dot_general | solution.py:108
  225.9 1.3 convolution_subtract_fusion
  227.2 7.8 %convolution_convert_fusion = bf16[256,8192]{1,0:T(8,128)(2,1)S(1)} fusion(f32[256,8192]{1,0:T(8,128)S(1)} %convolution_subtract_fusion, f32[128,256]{1,0:T(8,128)S(1)} %fusion.41, f32[128,256]{1,0:T(8,128)S(1)} %fusion.34), kind=kOutput, calls=%fused_computation.9 | convolution fusion | flops 6444613632 | bytes 12845056 | tf_op jit(solution)/shard_map/dot_general | solution.py:112
  235.2 2.5 %fusion.4 = f32[64,8192]{1,0:T(8,128)S(1)} fusion(f32[64,64]{1,0:T(8,128)S(1)} %broadcast_select_fusion, f32[8192,64]{0,1:T(8,128)S(1)} %reshape.119, f32[]{:T(128)} %bitcast.90, s32[8192]{0:T(1024)S(1)} %add.164, f32[8192]{0:T(1024)S(1)} %add.158, f32[64]{0:T(128)S(1)} %copy-done.10, f32[]{:T(128)} %bitcast.86, f32[64]{0:T(128)S(1)} %copy-done.6, ...), kind=kOutput, calls=%fused_computation.17 | convolution fusion | flops 407371776 | bytes 4277000 | tf_op jit(solution)/shard_map/dot_general | solution.py:15
  237.7 1.6 convolution_subtract_fusion.1
  239.3 0.2 pad_maximum_fusion
  239.5 5.2 %copy.51 = f32[6,1,16,1,8192]{4,3,2,1,0:T(1,128)} copy(f32[6,1,16,1,8192]{4,2,0,3,1:T(8,128)S(1)} %bitcast.93) | data formatting | bytes 6291456 | tf_op jit(solution)/shard_map/reshape | solution.py:127
  (81 shorter events, 2.4 us)
Async XLA Ops:
  8.4 11.5 %all-to-all-start = ((f32[8,1,4096]{2,1,0:T(1,128)}), f32[8,1,4096]{2,1,0:T(1,128)S(1)}, u32[]{:S(2)}, u32[]{:S(2)}) async-start(f32[8,1,4096]{2,1,0:T(1,128)} %reshape.168), calls=%async_computation | async-start | bytes 262144 | tf_op jit(solution)/shard_map/all_to_all | solution.py:49
  21.5 35.8 %copy-start.2 = (f32[8,64,64]{2,1,0:T(8,128)}, f32[8,64,64]{2,1,0:T(8,128)S(1)}, u32[]{:S(2)}) copy-start(f32[8,64,64]{2,1,0:T(8,128)S(1)} %reshape.169) | copy-start | bytes 393220
  22.6 18.5 %all-to-all-start.1 = ((f32[16,1,4096]{2,1,0:T(1,128)}), f32[16,1,4096]{2,1,0:T(1,128)S(1)}, u32[]{:S(2)}, u32[]{:S(2)}) async-start(f32[16,1,4096]{2,1,0:T(1,128)} %reshape.170), calls=%async_computation.1 | async-start | bytes 524288 | tf_op jit(solution)/shard_map/all_to_all | solution.py:32
  32.2 25.1 %copy-start.6 = (f32[64]{0:T(128)S(1)}, f32[64]{0:T(128)}, u32[]{:S(2)}) copy-start(f32[64]{0:T(128)} %param.8) | copy-start | bytes 772
  43.9 11.4 %all-to-all-start.2 = ((f32[8,1,12288]{2,1,0:T(1,128)}), f32[8,1,12288]{2,1,0:T(1,128)S(1)}, u32[]{:S(2)}, u32[]{:S(2)}) async-start(f32[8,1,12288]{2,1,0:T(1,128)} %reshape.172), calls=%async_computation.2 | async-start | bytes 786432 | tf_op jit(solution)/shard_map/all_to_all | solution.py:32
  47.3 137.6 %all-gather.3.cloned.1.call-start = ((), (), s32[]{:S(2)}) async-start(), calls=%async_computation.3 | async-start | bytes 4456448 | tf_op jit(solution)/shard_map/all_gather | solution.py:56
  57.6 64.0 %copy-start.1 = (f32[1536,64]{1,0:T(8,128)}, f32[1536,64]{1,0:T(8,128)S(1)}, u32[]{:S(2)}) copy-start(f32[1536,64]{1,0:T(8,128)S(1)} %get-tuple-element.46) | copy-start | bytes 1179652
  57.6 64.0 %copy-start.7 = (f32[512]{0:T(512)}, f32[512]{0:T(512)S(1)}, u32[]{:S(2)}) copy-start(f32[512]{0:T(512)S(1)} %slice.151) | copy-start | bytes 6148
  59.1 63.4 %copy-start.9 = (f32[64]{0:T(128)}, f32[64]{0:T(128)S(1)}, u32[]{:S(2)}) copy-start(f32[64]{0:T(128)S(1)} %get-tuple-element.43) | copy-start | bytes 772
  120.5 39.0 %copy-start.3 = (f32[128,256]{1,0:T(8,128)}, f32[128,256]{1,0:T(8,128)S(1)}, u32[]{:S(2)}) copy-start(f32[128,256]{1,0:T(8,128)S(1)} %fusion.45) | copy-start | bytes 393220
  122.4 103.5 %copy-start = (bf16[320,256]{1,0:T(8,128)(2,1)}, bf16[320,256]{1,0:T(8,128)(2,1)S(1)}, u32[]{:S(2)}) copy-start(bf16[320,256]{1,0:T(8,128)(2,1)S(1)} %convolution_convert_fusion.2) | copy-start | bytes 491524
  194.0 3.8 %copy-start.8 = (f32[512]{0:T(512)S(1)}, f32[512]{0:T(512)}, u32[]{:S(2)}) copy-start(f32[512]{0:T(512)} %copy-done.7) | copy-start | bytes 6148
  197.8 20.1 %copy-start.4 = (f32[128,256]{1,0:T(8,128)S(1)}, f32[128,256]{1,0:T(8,128)}, u32[]{:S(2)}) copy-start(f32[128,256]{1,0:T(8,128)} %copy-done.3) | copy-start | bytes 393220
  227.2 8.0 %copy-start.10 = (f32[64]{0:T(128)S(1)}, f32[64]{0:T(128)}, u32[]{:S(2)}) copy-start(f32[64]{0:T(128)} %copy-done.9) | copy-start | bytes 772
  235.1 2.7 %slice-start = ((bf16[320,256]{1,0:T(8,128)(2,1)}), bf16[64,256]{1,0:T(8,128)(2,1)S(1)}, s32[]{:S(2)}) async-start(bf16[320,256]{1,0:T(8,128)(2,1)} %copy-done), calls=%async_computation.4 | async-start | bytes 65536 | tf_op jit(solution)/shard_map/slice | solution.py:103
  235.1 2.7 %copy-start.5 = (bf16[64,256]{1,0:T(8,128)(2,1)S(1)}, bf16[64,256]{1,0:T(8,128)(2,1)}, u32[]{:S(2)}) copy-start(bf16[64,256]{1,0:T(8,128)(2,1)} %convolution_convert_fusion.3) | copy-start | bytes 98308
Sparse Core Ops, SparseCore 0:
  59.2 53.3 all-gather.2
where the time goes:
time: 255 us; the launch traced here: 252 us
  other arithmetic  117 us (46%)
  matrix products  47.8 us (19%)
  local copies, waits for them, and re-layouts  29.7 us (12%)
  waiting for transfers between devices  20.1 us (8%)
  starting transfers between devices  19.5 us (8%)
  between operations  18.2 us (7%)
    another operation x13, other arithmetic, lower_inverse(): factor = jnp.linalg.cholesky(block)  69.2 us
    another operation x5, other arithmetic, lower_inverse(): lax.linalg.triangular_solve(factor, identity, left_side=True, lower=True)  39.4 us
    dot_general x4, matrix products, kernel_block(): jnp.dot(left, right.T, precision=HIGHEST, preferred_element_type=jnp.floa...  24 us
    all_to_all x2, waiting for transfers between devices, gather_by_all_to_all(): return lax.all_to_all(copies, axis_name, 0, 0, tiled=True)  15 us
    all_to_all x2, starting transfers between devices, gather_by_all_to_all(): return lax.all_to_all(copies, axis_name, 0, 0, tiled=True)  13.1 us
    dot_general x1, matrix products, on_device(): jnp.dot(first_inverse, panel_kernel[:PANEL], precision=HIGHEST, preferred...  8.06 us
    dot_general x1, matrix products, on_device(): jnp.dot(second_inverse, reduced, precision=HIGHEST, preferred_element_typ...  7.8 us
    another operation x15, local copies, waits for them, and re-layouts, lower_inverse(): lax.linalg.triangular_solve(factor, identity, left_side=True, lower=True)  7.55 us
  transfers between devices with their start and end apart: 4, of which 3 were waited for; matrix products, arithmetic and copies ran while one was open for 49% of the time, Pallas kernels for 0%

commit v1 on v0

--- a/solution.py
+++ b/solution.py
@@ -2,6 +2,8 @@
 import jax.numpy as jnp
 from jax import lax
 from jax.sharding import PartitionSpec as P
+from jax.experimental import pallas as pl
+from jax.experimental.pallas import tpu as pltpu
 
 FEAT = 64
 SLAB = 1536
@@ -16,10 +18,119 @@
     return signal * jnp.exp(-0.5 * (left_norms[:, None] + right_norms[None, :] - 2.0 * cross))
 
 
+def _nt(left, right):
+    return lax.dot_general(
+        left, right, (((1,), (1,)), ((), ())), precision=HIGHEST, preferred_element_type=jnp.float32
+    )
+
+
+def lower_inverse_kernel(a_ref, o_ref, s_ref, x_ref):
+    half = a_ref.shape[0] // 2
+    lanes = lax.broadcasted_iota(jnp.int32, (half, half), 1)
+    rows = lax.broadcasted_iota(jnp.int32, (half, 1), 0)
+    lane_row = lax.broadcasted_iota(jnp.int32, (1, half), 1)
+    eye = jnp.where(lax.broadcasted_iota(jnp.int32, (half, half), 0) == lanes, 1.0, 0.0)
+
+    def step(k, carry):
+        s = s_ref[...]
+        x = x_ref[...]
+        row = s_ref[pl.ds(k, 1), :]
+        col = jnp.sum(jnp.where(lanes == k, s, 0.0), axis=1, keepdims=True)
+        root = jnp.sqrt(jnp.sum(jnp.where(lane_row == k, row, 0.0), axis=1, keepdims=True))
+        col = jnp.where(rows >= k, col / root, 0.0)
+        row = jnp.where(lane_row >= k, row / root, 0.0)
+        s_ref[...] = s - col * row
+        xk = x_ref[pl.ds(k, 1), :] / root
+        x_ref[...] = jnp.where(rows == k, xk, x - jnp.where(rows > k, col, 0.0) * xk)
+        return carry
+
+    def base(block):
+        s_ref[...] = block
+        x_ref[...] = eye.astype(jnp.float32)
+        lax.fori_loop(0, half, step, 0)
+        return x_ref[...]
+
+    first = base(a_ref[:half, :half])
+    lower = _nt(a_ref[half:, :half], first)
+    schur = a_ref[half:, half:] - _nt(lower, lower)
+    second = base((schur + schur.T) * 0.5)
+    below = -jnp.dot(
+        second,
+        jnp.dot(lower, first, precision=HIGHEST, preferred_element_type=jnp.float32),
+        precision=HIGHEST,
+        preferred_element_type=jnp.float32,
+    )
+    o_ref[:half, :half] = first
+    o_ref[:half, half:] = jnp.zeros((half, half), jnp.float32)
+    o_ref[half:, :half] = below
+    o_ref[half:, half:] = second
+
+
 def lower_inverse(block):
-    factor = jnp.linalg.cholesky(block)
-    identity = jnp.eye(block.shape[0], dtype=jnp.float32)
-    return lax.linalg.triangular_solve(factor, identity, left_side=True, lower=True)
+    size = block.shape[0]
+    half = size // 2
+    block = (block + block.T) * 0.5
+    return pl.pallas_call(
+        lower_inverse_kernel,
+        out_shape=jax.ShapeDtypeStruct((size, size), jnp.float32),
+        scratch_shapes=[pltpu.VMEM((half, half), jnp.float32), pltpu.VMEM((half, half), jnp.float32)],
+    )(block)
+
+
+def panel_kernel(
+    consts_ref, pts_ref, pnorm_ref, pid_ref, scales_ref, cs_ref, cn_ref, own_cs_ref, own_cn_ref,
+    own_ids_ref, finv_ref, sinv_ref, mid_ref, own_panels_ref, sel_ref, out_ref,
+):
+    signal = consts_ref[0]
+    jitter = consts_ref[1]
+    tile = pts_ref.shape[0] * pts_ref.shape[2]
+    scaled = pts_ref[...].reshape(tile, FEAT) * scales_ref[...]
+    pnorm = pnorm_ref[...]
+    pid = pid_ref[...]
+    cross = _nt(cs_ref[...], scaled)
+    values = signal * jnp.exp(-0.5 * (cn_ref[...] + pnorm - 2.0 * cross))
+    lead = lax.broadcasted_iota(jnp.int32, values.shape, 0)
+    values = values + jnp.where(lead == pid, jitter, jnp.float32(0.0))
+    first = jnp.dot(
+        finv_ref[...], values[:PANEL], precision=HIGHEST, preferred_element_type=jnp.float32
+    ).astype(jnp.bfloat16)
+    reduced = values[PANEL:] - jnp.dot(mid_ref[...], first, preferred_element_type=jnp.float32)
+    second = jnp.dot(
+        sinv_ref[...], reduced, precision=HIGHEST, preferred_element_type=jnp.float32
+    ).astype(jnp.bfloat16)
+    own_cross = _nt(own_cs_ref[...], scaled)
+    own = signal * jnp.exp(-0.5 * (own_cn_ref[...] + pnorm - 2.0 * own_cross))
+    own = own + jnp.where(own_ids_ref[...] == pid, jitter, jnp.float32(0.0))
+    both = jnp.concatenate([first, second], axis=0)
+    trailing = own - jnp.dot(own_panels_ref[...], both, preferred_element_type=jnp.float32)
+    sel = sel_ref[...]
+    out_ref[:BLK] = jnp.dot(sel, first, preferred_element_type=jnp.float32)
+    out_ref[BLK : 2 * BLK] = jnp.dot(sel, second, preferred_element_type=jnp.float32)
+    out_ref[2 * BLK :] = trailing
+
+
+def panel_stage(consts, gathered, pnorm, pid, scales, cs, cn, own_cs, own_cn, own_ids, finv, sinv, mid, own_panels, sel):
+    col_count, row_count, block_rows, _ = gathered.shape
+    tile = col_count * block_rows
+    grid_rows = tile * row_count
+    out_rows = 2 * BLK + own_cs.shape[0]
+
+    def whole(array):
+        return pl.BlockSpec(array.shape, lambda i: (0,) * array.ndim)
+
+    return pl.pallas_call(
+        panel_kernel,
+        grid=(row_count,),
+        in_specs=[
+            pl.BlockSpec(memory_space=pltpu.SMEM),
+            pl.BlockSpec((col_count, 1, block_rows, FEAT), lambda i: (0, i, 0, 0)),
+            pl.BlockSpec((1, tile), lambda i: (0, i)),
+            pl.BlockSpec((1, tile), lambda i: (0, i)),
+        ]
+        + [whole(a) for a in (scales, cs, cn, own_cs, own_cn, own_ids, finv, sinv, mid, own_panels, sel)],
+        out_specs=pl.BlockSpec((out_rows, tile), lambda i: (0, i)),
+        out_shape=jax.ShapeDtypeStruct((out_rows, grid_rows), jnp.float32),
+    )(consts, gathered, pnorm, pid, scales, cs, cn, own_cs, own_cn, own_ids, finv, sinv, mid, own_panels, sel)
 
 
 def ridge_where(row_ids, col_ids, jitter):
@@ -54,19 +165,18 @@
 
     moved, centers = lax.optimization_barrier((moved, centers))
     gathered = lax.all_gather(moved, "col", axis=0, tiled=False)
-    row_points = gathered.transpose(1, 0, 2, 3).reshape(-1, FEAT)
-    grid_rows = row_points.shape[0]
+    grid_rows = gathered.shape[0] * gathered.shape[1] * block_rows
 
     center_scaled = centers * feature_scales
     center_norms = jnp.sum(center_scaled * center_scaled, axis=1)
-    point_scaled = row_points * feature_scales
-    point_norms = jnp.sum(point_scaled * point_scaled, axis=1)
+    gathered_scaled = gathered * feature_scales
+    point_norms = jnp.sum(gathered_scaled * gathered_scaled, axis=3).transpose(1, 0, 2).reshape(1, grid_rows)
 
     point_ids = (
         lax.broadcasted_iota(jnp.int32, (grid_rows // block_rows, block_rows), 0) * row_count
         + row
     ) * block_rows + lax.broadcasted_iota(jnp.int32, (grid_rows // block_rows, block_rows), 1)
-    point_ids = point_ids.reshape(grid_rows)
+    point_ids = point_ids.reshape(1, grid_rows)
 
     own_ids = (
         (
@@ -102,27 +212,29 @@
     ).astype(jnp.bfloat16)
     own_panels = jnp.concatenate([center_first[PANEL:], second_own], axis=1)
 
-    panel_kernel = kernel_block(
-        center_scaled[: 2 * PANEL], center_norms[: 2 * PANEL], point_scaled, point_norms, signal
-    ) + ridge_where(jnp.arange(2 * PANEL, dtype=jnp.int32), point_ids, jitter)
-    first_panel = jnp.dot(
-        first_inverse, panel_kernel[:PANEL], precision=HIGHEST, preferred_element_type=jnp.float32
-    ).astype(jnp.bfloat16)
-    reduced = panel_kernel[PANEL:] - jnp.dot(first_mid, first_panel, preferred_element_type=jnp.float32)
-    second_panel = jnp.dot(
-        second_inverse, reduced, precision=HIGHEST, preferred_element_type=jnp.float32
-    ).astype(jnp.bfloat16)
-    panels = jnp.concatenate([first_panel, second_panel], axis=0)
-
-    own_kernel = kernel_block(own_scaled, own_norms, point_scaled, point_norms, signal) + ridge_where(
-        own_ids, point_ids, jitter
-    )
-    trailing = own_kernel - jnp.dot(own_panels, panels, preferred_element_type=jnp.float32)
-
-    own_first = lax.dynamic_slice_in_dim(first_panel, column * BLK, BLK, 0)
-    own_second = lax.dynamic_slice_in_dim(second_panel, column * BLK, BLK, 0)
-    finished = jnp.concatenate(
-        [own_first.astype(jnp.float32), own_second.astype(jnp.float32), trailing], axis=0
+    select = jnp.where(
+        lax.broadcasted_iota(jnp.int32, (BLK, PANEL), 1)
+        == column * BLK + lax.broadcasted_iota(jnp.int32, (BLK, PANEL), 0),
+        1.0,
+        0.0,
+    ).astype(jnp.bfloat16)
+    consts = jnp.stack([signal, jitter])
+    finished = panel_stage(
+        consts,
+        gathered,
+        point_norms,
+        point_ids,
+        feature_scales.reshape(1, FEAT),
+        center_scaled[: 2 * PANEL],
+        center_norms[: 2 * PANEL].reshape(-1, 1),
+        own_scaled,
+        own_norms.reshape(-1, 1),
+        own_ids.reshape(-1, 1),
+        first_inverse,
+        second_inverse,
+        first_mid,
+        own_panels,
+        select,
     )
     return finished.reshape(col_blocks, 1, BLK, 1, grid_rows)
 

time: 255 us -> 200 us (0.78)
  Pallas kernels: 0 us -> 109 us
  other arithmetic: 117 us -> 12 us
  matrix products: 47.8 us -> 4.68 us
  local copies, waits for them, and re-layouts: 29.7 us -> 17.4 us
  blocking collectives: 0 us -> 11.3 us
  starting transfers between devices: 19.5 us -> 13.1 us
  waiting for transfers between devices: 20.1 us -> 16.7 us
  between operations: 18.2 us -> 15 us
    pallas_call x0 -> x3, Pallas kernels: none -> 109 us  [the longest x2 69.1 us: lower_inverse(): pl.pallas_call(lower_inverse_kernel, out_shape=jax.ShapeDtypeStruct((size...]
    another operation x18 -> x1, other arithmetic: 109 us -> 0.61 us  [on_device(): consts = jnp.stack([signal, jitter])]
    dot_general x4 -> x2, matrix products: 24 us -> 1.37 us  [kernel_block(): jnp.dot(left, right.T, precision=HIGHEST, preferred_element_type=jnp.floa...]
    dot_general x4 -> x0, matrix products: 18.7 us -> none  [the longest x1 8.06 us: on_device(): jnp.dot(first_inverse, panel_kernel[:PANEL], precision=HIGHEST, preferred...]
    all_to_all x0 -> x1, blocking collectives: none -> 11.3 us  [on_device(): moved = lax.all_to_all(blocks, 'row', 0, 0, tiled=True)]
    another operation x19 -> x0, local copies, waits for them, and re-layouts: 7.6 us -> none  [the longest x15 7.55 us: lower_inverse(): lax.linalg.triangular_solve(factor, identity, left_side=True, lower=True)]
    all_to_all x1 -> x0, starting transfers between devices: 6.2 us -> none  [on_device(): moved = lax.all_to_all(blocks, 'row', 0, 0, tiled=True)]
    transpose x1, local copies, waits for them, and re-layouts: 5.69 us -> 0.01 us  [on_device(): jnp.sum(gathered_scaled * gathered_scaled, axis=3).transpose(1, 0, 2)]
  transfers between devices with their start and end apart: 4 -> 3, of which waited for: 3 -> 2; matrix products, arithmetic and copies ran while one was open for 49% -> 7% of each run, Pallas kernels for 0% -> 35%
where the time goes in v1:
time: 200 us; the launch traced here: 199 us
  Pallas kernels  109 us (54%)
  local copies, waits for them, and re-layouts  17.4 us (9%)
  waiting for transfers between devices  16.7 us (8%)
  between operations  15 us (8%)
  starting transfers between devices  13.1 us (7%)
  other arithmetic  12 us (6%)
  blocking collectives  11.3 us (6%)
  matrix products  4.68 us (2%)
    pallas_call x2, Pallas kernels, lower_inverse(): pl.pallas_call(lower_inverse_kernel, out_shape=jax.ShapeDtypeStruct((size...  69.1 us
    pallas_call x1, Pallas kernels, panel_stage(): pl.pallas_call(panel_kernel, grid=(row_count,), in_specs=[pl.BlockSpec(me...  40.3 us
    all_to_all x2, waiting for transfers between devices, gather_by_all_to_all(): return lax.all_to_all(copies, axis_name, 0, 0, tiled=True)  16.6 us
    all_to_all x2, starting transfers between devices, gather_by_all_to_all(): return lax.all_to_all(copies, axis_name, 0, 0, tiled=True)  13.1 us
    all_to_all x1, blocking collectives, on_device(): moved = lax.all_to_all(blocks, 'row', 0, 0, tiled=True)  11.3 us
    reshape x1, local copies, waits for them, and re-layouts, on_device(): return finished.reshape(col_blocks, 1, BLK, 1, grid_rows)  6.82 us
    unnamed x14, local copies, waits for them, and re-layouts  4.01 us
  transfers between devices with their start and end apart: 3, of which 2 were waited for; matrix products, arithmetic and copies ran while one was open for 7% of the time, Pallas kernels for 35%

profile of v1, /device:TPU:1, one launch (start us, length us, event | category | flops | bytes accessed | tf_op | source)
XLA Modules:
  0.0 199.5 jit_solution(1438032756155513401)
XLA Ops:
  6.5 1.0 copy.32
  7.6 0.2 reshape.152
  7.8 11.3 %all_to_all.15 = f32[8,1,4096]{2,1,0:T(1,128)S(1)} all-to-all(f32[8,1,4096]{2,1,0:T(1,128)S(1)} %reshape.152), channel_id=1, replica_groups=mesh['row'=8,'col'=16] {'row'}, dimensions={0} | all-to-all | bytes 262144 | tf_op jit(solution)/shard_map/all_to_all | solution.py:160
  19.0 0.6 broadcast.127
  19.6 1.0 reduce.2
  20.6 0.1 reshape.153
  20.7 0.0 copy-start
  20.8 1.0 reshape.154
  21.8 9.6 %all-to-all-start.1 = ((f32[16,1,4096]{2,1,0:T(1,128)}), f32[16,1,4096]{2,1,0:T(1,128)S(1)}, u32[]{:S(2)}, u32[]{:S(2)}) async-start(f32[16,1,4096]{2,1,0:T(1,128)} %reshape.154), calls=%async_computation.1 | async-start | bytes 524288 | tf_op jit(solution)/shard_map/all_to_all | solution.py:143
  31.4 0.0 copy-start.3
  31.4 8.9 %all-to-all-done.1 = f32[16,1,4096]{2,1,0:T(1,128)S(1)} async-done(((f32[16,1,4096]{2,1,0:T(1,128)}), f32[16,1,4096]{2,1,0:T(1,128)S(1)}, u32[]{:S(2)}, u32[]{:S(2)}) %all-to-all-start.1) | async-done | bytes 262176 | tf_op jit(solution)/shard_map/all_to_all | solution.py:143
  40.3 1.3 reduce.3
  41.6 0.2 reshape.155
  41.9 0.1 broadcast_in_dim.67
  42.0 1.2 reshape.156
  43.2 3.5 %all-to-all-start.2 = ((f32[8,1,12288]{2,1,0:T(1,128)}), f32[8,1,12288]{2,1,0:T(1,128)S(1)}, u32[]{:S(2)}, u32[]{:S(2)}) async-start(f32[8,1,12288]{2,1,0:T(1,128)} %reshape.156), calls=%async_computation.2 | async-start | bytes 786432 | tf_op jit(solution)/shard_map/all_to_all | solution.py:143
  46.7 0.0 all-gather.3.cloned.1.call-start
  46.7 0.1 iota_add_fusion.1
  46.8 0.1 iota_add_fusion
  46.9 7.7 %all-to-all-done.2 = f32[8,1,12288]{2,1,0:T(1,128)S(1)} async-done(((f32[8,1,12288]{2,1,0:T(1,128)}), f32[8,1,12288]{2,1,0:T(1,128)S(1)}, u32[]{:S(2)}, u32[]{:S(2)}) %all-to-all-start.2) | async-done | bytes 393248 | tf_op jit(solution)/shard_map/all_to_all | solution.py:143
  54.6 1.6 reduce.4
  56.2 0.3 reshape.157
  56.6 0.1 copy.33
  56.6 0.0 copy-done
  56.7 0.0 all-gather.3.cloned.1.call-update
  56.7 0.1 reshape.130
  56.8 0.1 reshape.150.own_ids_ref
  56.9 0.0 copy-start.1
  58.2 0.7 add.125.pid_ref
  58.9 0.6 pad_maximum_fusion.2.consts_ref
  59.5 0.1 fusion.19
  59.6 0.7 select_convert_fusion.sel_ref
  60.3 0.0 copy-done.3
  60.3 0.3 multiply_reduce_fusion.1
  60.6 0.8 gather_fusion.1
  61.4 0.6 gather_fusion
  62.0 0.7 slice.70.cs_ref
  62.7 0.4 fusion.18
  63.1 0.1 copy.40
  63.2 0.1 copy.41
  63.4 0.8 fusion.12.a_ref
  64.2 34.6 %shard_map.46.finv_ref = f32[256,256]{1,0:T(8,128)} custom-call(f32[256,256]{1,0:T(8,128)} %fusion.12.a_ref), custom_call_target="tpu_custom_call" | custom-call | tf_op jit(solution)/shard_map/pallas_call | solution.py:73
  98.8 0.1 broadcast_select_fusion.own_cs_ref
  98.9 0.0 copy-start.2
  98.9 1.0 fusion.4
  99.9 1.7 convolution_convert_fusion
  101.7 0.7 slice.78.mid_ref
  102.3 0.1 copy.38
  102.4 0.8 copy.45.cn_ref
  103.3 0.2 convolution_subtract_fusion
  103.5 0.1 copy.44
  103.7 0.7 fusion.6.a_ref
  104.4 34.5 %shard_map.47.sinv_ref = f32[256,256]{1,0:T(8,128)} custom-call(f32[256,256]{1,0:T(8,128)} %fusion.6.a_ref), custom_call_target="tpu_custom_call" | custom-call | tf_op jit(solution)/shard_map/pallas_call | solution.py:73
  138.9 1.3 convolution_convert_fusion.1
  140.2 0.6 pad_maximum_fusion.own_panels_ref
  140.8 0.0 copy-done.1
  140.8 0.6 and_select_fusion.own_cn_ref
  141.5 0.0 all-gather.3.cloned.1.call-done
  141.5 3.3 %multiply_reduce_fusion = f32[16,8,64]{2,1,0:T(8,128)S(1)} fusion(f32[16,8,64,64]{3,2,1,0:T(8,128)} %bitcast.38, f32[64]{0:T(128)S(1)} %copy-done.3), kind=kLoop, calls=%fused_computation.2 | loop fusion | flops 1564672 | bytes 2130176 | tf_op jit(solution)/shard_map/reduce_sum | solution.py:173
  144.8 0.0 copy-done.2
  144.9 0.7 reshape.127.pnorm_ref
  145.6 40.3 %shard_map.48 = f32[96,8192]{1,0:T(8,128)} custom-call(f32[2]{0:T(128)} %pad_maximum_fusion.2.consts_ref, f32[16,8,64,64]{3,2,1,0:T(8,128)} %bitcast.39, f32[1,8192]{1,0:T(1,128)} %reshape.127.pnorm_ref, s32[1,8192]{1,0:T(1,128)} %add.125.pid_ref, f32[1,64]{1,0:T(1,128)} %bitcast.47, f32[512,64]{1,0:T(8,128)} %slice.70.cs_ref, f32[512,1]{1,0:T(8,128)} %copy.45.cn_ref, ...), custom_call_target="tpu_custom_call" | custom-call | tf_op jit(solution)/shard_map/pallas_call | solution.py:121
  185.8 6.8 %copy.47 = f32[6,1,16,1,8192]{4,3,2,1,0:T(1,128)} copy(f32[6,1,16,1,8192]{4,2,0,3,1:T(8,128)} %bitcast.40) | data formatting | bytes 6291456 | tf_op jit(solution)/shard_map/reshape | solution.py:239
  (18 shorter events, 0.2 us)
Async XLA Ops:
  20.7 35.9 %copy-start = (f32[8,64,64]{2,1,0:T(8,128)}, f32[8,64,64]{2,1,0:T(8,128)S(1)}, u32[]{:S(2)}) copy-start(f32[8,64,64]{2,1,0:T(8,128)S(1)} %reshape.153) | copy-start | bytes 393220
  21.8 18.5 %all-to-all-start.1 = ((f32[16,1,4096]{2,1,0:T(1,128)}), f32[16,1,4096]{2,1,0:T(1,128)S(1)}, u32[]{:S(2)}, u32[]{:S(2)}) async-start(f32[16,1,4096]{2,1,0:T(1,128)} %reshape.154), calls=%async_computation.1 | async-start | bytes 524288 | tf_op jit(solution)/shard_map/all_to_all | solution.py:143
  31.4 28.9 %copy-start.3 = (f32[64]{0:T(128)S(1)}, f32[64]{0:T(128)}, u32[]{:S(2)}) copy-start(f32[64]{0:T(128)} %param.5) | copy-start | bytes 772
  43.2 11.4 %all-to-all-start.2 = ((f32[8,1,12288]{2,1,0:T(1,128)}), f32[8,1,12288]{2,1,0:T(1,128)S(1)}, u32[]{:S(2)}, u32[]{:S(2)}) async-start(f32[8,1,12288]{2,1,0:T(1,128)} %reshape.156), calls=%async_computation.2 | async-start | bytes 786432 | tf_op jit(solution)/shard_map/all_to_all | solution.py:143
  46.7 94.8 %all-gather.3.cloned.1.call-start = ((), (), s32[]{:S(2)}) async-start(), calls=%async_computation.3 | async-start | bytes 4456448 | tf_op jit(solution)/shard_map/all_gather | solution.py:167
  56.9 84.0 %copy-start.1 = (s32[64,1]{1,0:T(8,128)}, s32[64,1]{1,0:T(8,128)S(1)}, u32[]{:S(2)}) copy-start(s32[64,1]{1,0:T(8,128)S(1)} %reshape.150.own_ids_ref) | copy-start | bytes 772
  98.9 45.9 %copy-start.2 = (f32[64,64]{1,0:T(8,128)}, f32[64,64]{1,0:T(8,128)S(1)}, u32[]{:S(2)}) copy-start(f32[64,64]{1,0:T(8,128)S(1)} %broadcast_select_fusion.own_cs_ref) | copy-start | bytes 49156
Sparse Core Ops, SparseCore 0:
  56.8 53.0 all-gather.2

commit v2 on v1

--- a/solution.py
+++ b/solution.py
@@ -47,7 +47,7 @@
     def base(block):
         s_ref[...] = block
         x_ref[...] = eye.astype(jnp.float32)
-        lax.fori_loop(0, half, step, 0)
+        lax.fori_loop(0, half, step, 0, unroll=2)
         return x_ref[...]
 
     first = base(a_ref[:half, :half])
@@ -75,6 +75,19 @@
         out_shape=jax.ShapeDtypeStruct((size, size), jnp.float32),
         scratch_shapes=[pltpu.VMEM((half, half), jnp.float32), pltpu.VMEM((half, half), jnp.float32)],
     )(block)
+
+
+def lower_times(lower_ref, right):
+    half = lower_ref.shape[0] // 2
+    top = jnp.dot(
+        lower_ref[:half, :half], right[:half], precision=HIGHEST, preferred_element_type=jnp.float32
+    )
+    bottom = jnp.dot(
+        lower_ref[half:, :half], right[:half], precision=HIGHEST, preferred_element_type=jnp.float32
+    ) + jnp.dot(
+        lower_ref[half:, half:], right[half:], precision=HIGHEST, preferred_element_type=jnp.float32
+    )
+    return jnp.concatenate([top, bottom], axis=0)
 
 
 def panel_kernel(
@@ -91,13 +104,9 @@
     values = signal * jnp.exp(-0.5 * (cn_ref[...] + pnorm - 2.0 * cross))
     lead = lax.broadcasted_iota(jnp.int32, values.shape, 0)
     values = values + jnp.where(lead == pid, jitter, jnp.float32(0.0))
-    first = jnp.dot(
-        finv_ref[...], values[:PANEL], precision=HIGHEST, preferred_element_type=jnp.float32
-    ).astype(jnp.bfloat16)
+    first = lower_times(finv_ref, values[:PANEL]).astype(jnp.bfloat16)
     reduced = values[PANEL:] - jnp.dot(mid_ref[...], first, preferred_element_type=jnp.float32)
-    second = jnp.dot(
-        sinv_ref[...], reduced, precision=HIGHEST, preferred_element_type=jnp.float32
-    ).astype(jnp.bfloat16)
+    second = lower_times(sinv_ref, reduced).astype(jnp.bfloat16)
     own_cross = _nt(own_cs_ref[...], scaled)
     own = signal * jnp.exp(-0.5 * (own_cn_ref[...] + pnorm - 2.0 * own_cross))
     own = own + jnp.where(own_ids_ref[...] == pid, jitter, jnp.float32(0.0))

time: 200 us -> 206 us (1.030)
  Pallas kernels: 109 us -> 115 us
    pallas_call x1, Pallas kernels: 40.3 us -> 46.6 us  [panel_stage(): pl.pallas_call(panel_kernel, grid=(row_count,), in_specs=[pl.BlockSpec(me...]
  transfers between devices with their start and end apart: 3 -> 3, of which waited for: 2 -> 2; matrix products, arithmetic and copies ran while one was open for 7% -> 7% of each run, Pallas kernels for 35% -> 33%
where the time goes in v2:
time: 206 us
  Pallas kernels  115 us (56%)
  local copies, waits for them, and re-layouts  17.4 us (8%)
  waiting for transfers between devices  16.7 us (8%)
  between operations  15 us (7%)
  starting transfers between devices  13.1 us (6%)
  other arithmetic  12 us (6%)
  blocking collectives  11.3 us (5%)
  matrix products  4.68 us (2%)
    pallas_call x2, Pallas kernels, lower_inverse(): pl.pallas_call(lower_inverse_kernel, out_shape=jax.ShapeDtypeStruct((size...  68.8 us
    pallas_call x1, Pallas kernels, panel_stage(): pl.pallas_call(panel_kernel, grid=(row_count,), in_specs=[pl.BlockSpec(me...  46.6 us
    all_to_all x2, waiting for transfers between devices, gather_by_all_to_all(): return lax.all_to_all(copies, axis_name, 0, 0, tiled=True)  16.6 us
    all_to_all x2, starting transfers between devices, gather_by_all_to_all(): return lax.all_to_all(copies, axis_name, 0, 0, tiled=True)  13.1 us
    all_to_all x1, blocking collectives, on_device(): moved = lax.all_to_all(blocks, 'row', 0, 0, tiled=True)  11.3 us
    reshape x1, local copies, waits for them, and re-layouts, on_device(): return finished.reshape(col_blocks, 1, BLK, 1, grid_rows)  6.82 us
  transfers between devices with their start and end apart: 3, of which 2 were waited for; matrix products, arithmetic and copies ran while one was open for 7% of the time, Pallas kernels for 33%

profile of v2, /device:TPU:1, one launch (start us, length us, event | category | flops | bytes accessed | tf_op | source)
XLA Modules:
  0.0 205.6 jit_solution(12087805766577586310)
XLA Ops:
  6.5 1.0 copy.32
  7.6 0.2 reshape.152
  7.8 11.3 %all_to_all.15 = f32[8,1,4096]{2,1,0:T(1,128)S(1)} all-to-all(f32[8,1,4096]{2,1,0:T(1,128)S(1)} %reshape.152), channel_id=1, replica_groups=mesh['row'=8,'col'=16] {'row'}, dimensions={0} | all-to-all | bytes 262144 | tf_op jit(solution)/shard_map/all_to_all | solution.py:169
  19.0 0.6 broadcast.127
  19.6 1.0 reduce.2
  20.6 0.1 reshape.153
  20.7 0.0 copy-start
  20.8 1.0 reshape.154
  21.8 9.6 %all-to-all-start.1 = ((f32[16,1,4096]{2,1,0:T(1,128)}), f32[16,1,4096]{2,1,0:T(1,128)S(1)}, u32[]{:S(2)}, u32[]{:S(2)}) async-start(f32[16,1,4096]{2,1,0:T(1,128)} %reshape.154), calls=%async_computation.1 | async-start | bytes 524288 | tf_op jit(solution)/shard_map/all_to_all | solution.py:152
  31.4 0.0 copy-start.3
  31.4 8.9 %all-to-all-done.1 = f32[16,1,4096]{2,1,0:T(1,128)S(1)} async-done(((f32[16,1,4096]{2,1,0:T(1,128)}), f32[16,1,4096]{2,1,0:T(1,128)S(1)}, u32[]{:S(2)}, u32[]{:S(2)}) %all-to-all-start.1) | async-done | bytes 262176 | tf_op jit(solution)/shard_map/all_to_all | solution.py:152
  40.3 1.3 reduce.3
  41.6 0.2 reshape.155
  41.9 0.1 broadcast_in_dim.67
  42.0 1.2 reshape.156
  43.2 3.5 %all-to-all-start.2 = ((f32[8,1,12288]{2,1,0:T(1,128)}), f32[8,1,12288]{2,1,0:T(1,128)S(1)}, u32[]{:S(2)}, u32[]{:S(2)}) async-start(f32[8,1,12288]{2,1,0:T(1,128)} %reshape.156), calls=%async_computation.2 | async-start | bytes 786432 | tf_op jit(solution)/shard_map/all_to_all | solution.py:152
  46.7 0.0 all-gather.3.cloned.1.call-start
  46.7 0.1 iota_add_fusion.1
  46.8 0.1 iota_add_fusion
  46.9 7.7 %all-to-all-done.2 = f32[8,1,12288]{2,1,0:T(1,128)S(1)} async-done(((f32[8,1,12288]{2,1,0:T(1,128)}), f32[8,1,12288]{2,1,0:T(1,128)S(1)}, u32[]{:S(2)}, u32[]{:S(2)}) %all-to-all-start.2) | async-done | bytes 393248 | tf_op jit(solution)/shard_map/all_to_all | solution.py:152
  54.6 1.6 reduce.4
  56.2 0.3 reshape.157
  56.6 0.1 copy.33
  56.6 0.0 copy-done
  56.7 0.0 all-gather.3.cloned.1.call-update
  56.7 0.1 reshape.130
  56.8 0.1 reshape.150.own_ids_ref
  56.9 0.0 copy-start.1
  58.2 0.7 add.125.pid_ref
  58.9 0.6 pad_maximum_fusion.2.consts_ref
  59.5 0.1 fusion.19
  59.6 0.7 select_convert_fusion.sel_ref
  60.3 0.0 copy-done.3
  60.3 0.3 multiply_reduce_fusion.1
  60.6 0.8 gather_fusion.1
  61.4 0.6 gather_fusion
  62.0 0.7 slice.70.cs_ref
  62.7 0.4 fusion.18
  63.1 0.1 copy.40
  63.2 0.1 copy.41
  63.4 0.8 fusion.12.a_ref
  64.2 34.5 %shard_map.46.finv_ref = f32[256,256]{1,0:T(8,128)} custom-call(f32[256,256]{1,0:T(8,128)} %fusion.12.a_ref), custom_call_target="tpu_custom_call" | custom-call | tf_op jit(solution)/shard_map/pallas_call | solution.py:73
  98.7 0.1 broadcast_select_fusion.own_cs_ref
  98.8 0.0 copy-start.2
  98.8 1.0 fusion.4
  99.8 1.7 convolution_convert_fusion
  101.5 0.7 slice.78.mid_ref
  102.2 0.1 copy.38
  102.3 0.8 copy.45.cn_ref
  103.1 0.2 convolution_subtract_fusion
  103.4 0.1 copy.44
  103.5 0.7 fusion.6.a_ref
  104.3 34.4 %shard_map.47.sinv_ref = f32[256,256]{1,0:T(8,128)} custom-call(f32[256,256]{1,0:T(8,128)} %fusion.6.a_ref), custom_call_target="tpu_custom_call" | custom-call | tf_op jit(solution)/shard_map/pallas_call | solution.py:73
  138.6 1.3 convolution_convert_fusion.1
  140.0 0.6 pad_maximum_fusion.own_panels_ref
  140.6 0.0 copy-done.1
  140.6 0.6 and_select_fusion.own_cn_ref
  141.2 0.0 all-gather.3.cloned.1.call-done
  141.2 3.3 %multiply_reduce_fusion = f32[16,8,64]{2,1,0:T(8,128)S(1)} fusion(f32[16,8,64,64]{3,2,1,0:T(8,128)} %bitcast.38, f32[64]{0:T(128)S(1)} %copy-done.3), kind=kLoop, calls=%fused_computation.2 | loop fusion | flops 1564672 | bytes 2130176 | tf_op jit(solution)/shard_map/reduce_sum | solution.py:182
  144.6 0.0 copy-done.2
  144.6 0.7 reshape.127.pnorm_ref
  145.3 46.6 %shard_map.48 = f32[96,8192]{1,0:T(8,128)} custom-call(f32[2]{0:T(128)} %pad_maximum_fusion.2.consts_ref, f32[16,8,64,64]{3,2,1,0:T(8,128)} %bitcast.39, f32[1,8192]{1,0:T(1,128)} %reshape.127.pnorm_ref, s32[1,8192]{1,0:T(1,128)} %add.125.pid_ref, f32[1,64]{1,0:T(1,128)} %bitcast.47, f32[512,64]{1,0:T(8,128)} %slice.70.cs_ref, f32[512,1]{1,0:T(8,128)} %copy.45.cn_ref, ...), custom_call_target="tpu_custom_call" | custom-call | tf_op jit(solution)/shard_map/pallas_call | solution.py:130
  191.9 6.8 %copy.47 = f32[6,1,16,1,8192]{4,3,2,1,0:T(1,128)} copy(f32[6,1,16,1,8192]{4,2,0,3,1:T(8,128)} %bitcast.40) | data formatting | bytes 6291456 | tf_op jit(solution)/shard_map/reshape | solution.py:248
  (18 shorter events, 0.2 us)
Async XLA Ops:
  20.7 35.9 %copy-start = (f32[8,64,64]{2,1,0:T(8,128)}, f32[8,64,64]{2,1,0:T(8,128)S(1)}, u32[]{:S(2)}) copy-start(f32[8,64,64]{2,1,0:T(8,128)S(1)} %reshape.153) | copy-start | bytes 393220
  21.8 18.5 %all-to-all-start.1 = ((f32[16,1,4096]{2,1,0:T(1,128)}), f32[16,1,4096]{2,1,0:T(1,128)S(1)}, u32[]{:S(2)}, u32[]{:S(2)}) async-start(f32[16,1,4096]{2,1,0:T(1,128)} %reshape.154), calls=%async_computation.1 | async-start | bytes 524288 | tf_op jit(solution)/shard_map/all_to_all | solution.py:152
  31.4 28.9 %copy-start.3 = (f32[64]{0:T(128)S(1)}, f32[64]{0:T(128)}, u32[]{:S(2)}) copy-start(f32[64]{0:T(128)} %param.5) | copy-start | bytes 772
  43.2 11.4 %all-to-all-start.2 = ((f32[8,1,12288]{2,1,0:T(1,128)}), f32[8,1,12288]{2,1,0:T(1,128)S(1)}, u32[]{:S(2)}, u32[]{:S(2)}) async-start(f32[8,1,12288]{2,1,0:T(1,128)} %reshape.156), calls=%async_computation.2 | async-start | bytes 786432 | tf_op jit(solution)/shard_map/all_to_all | solution.py:152
  46.7 94.6 %all-gather.3.cloned.1.call-start = ((), (), s32[]{:S(2)}) async-start(), calls=%async_computation.3 | async-start | bytes 4456448 | tf_op jit(solution)/shard_map/all_gather | solution.py:176
  56.9 83.7 %copy-start.1 = (s32[64,1]{1,0:T(8,128)}, s32[64,1]{1,0:T(8,128)S(1)}, u32[]{:S(2)}) copy-start(s32[64,1]{1,0:T(8,128)S(1)} %reshape.150.own_ids_ref) | copy-start | bytes 772
  98.8 45.8 %copy-start.2 = (f32[64,64]{1,0:T(8,128)}, f32[64,64]{1,0:T(8,128)S(1)}, u32[]{:S(2)}) copy-start(f32[64,64]{1,0:T(8,128)S(1)} %broadcast_select_fusion.own_cs_ref) | copy-start | bytes 49156
Sparse Core Ops, SparseCore 0:
  56.8 53.0 all-gather.2

commit v3 on v1

--- a/solution.py
+++ b/solution.py
@@ -77,6 +77,23 @@
     )(block)
 
 
+def split_three(values):
+    high = values.astype(jnp.bfloat16)
+    rest = values - high.astype(jnp.float32)
+    middle = rest.astype(jnp.bfloat16)
+    low = (rest - middle.astype(jnp.float32)).astype(jnp.bfloat16)
+    return high, middle, low
+
+
+def pack_left(values):
+    high = lax.reduce_precision(values, exponent_bits=8, mantissa_bits=7)
+    rest = values - high
+    middle = lax.reduce_precision(rest, exponent_bits=8, mantissa_bits=7)
+    low = rest - middle
+    high, middle, low = (piece.astype(jnp.bfloat16) for piece in (high, middle, low))
+    return jnp.concatenate([high, high, middle, high, low, middle], axis=1)
+
+
 def panel_kernel(
     consts_ref, pts_ref, pnorm_ref, pid_ref, scales_ref, cs_ref, cn_ref, own_cs_ref, own_cn_ref,
     own_ids_ref, finv_ref, sinv_ref, mid_ref, own_panels_ref, sel_ref, out_ref,
@@ -84,10 +101,12 @@
     signal = consts_ref[0]
     jitter = consts_ref[1]
     tile = pts_ref.shape[0] * pts_ref.shape[2]
-    scaled = pts_ref[...].reshape(tile, FEAT) * scales_ref[...]
+    scaled = (pts_ref[...].reshape(tile, FEAT) * scales_ref[...]).T
+    high, middle, low = split_three(scaled)
+    packed = jnp.concatenate([high, middle, high, low, high, middle], axis=0)
     pnorm = pnorm_ref[...]
     pid = pid_ref[...]
-    cross = _nt(cs_ref[...], scaled)
+    cross = jnp.dot(cs_ref[...], packed, preferred_element_type=jnp.float32)
     values = signal * jnp.exp(-0.5 * (cn_ref[...] + pnorm - 2.0 * cross))
     lead = lax.broadcasted_iota(jnp.int32, values.shape, 0)
     values = values + jnp.where(lead == pid, jitter, jnp.float32(0.0))
@@ -98,7 +117,7 @@
     second = jnp.dot(
         sinv_ref[...], reduced, precision=HIGHEST, preferred_element_type=jnp.float32
     ).astype(jnp.bfloat16)
-    own_cross = _nt(own_cs_ref[...], scaled)
+    own_cross = jnp.dot(own_cs_ref[...], packed, preferred_element_type=jnp.float32)
     own = signal * jnp.exp(-0.5 * (own_cn_ref[...] + pnorm - 2.0 * own_cross))
     own = own + jnp.where(own_ids_ref[...] == pid, jitter, jnp.float32(0.0))
     both = jnp.concatenate([first, second], axis=0)
@@ -225,9 +244,9 @@
         point_norms,
         point_ids,
         feature_scales.reshape(1, FEAT),
-        center_scaled[: 2 * PANEL],
+        pack_left(center_scaled[: 2 * PANEL]),
         center_norms[: 2 * PANEL].reshape(-1, 1),
-        own_scaled,
+        pack_left(own_scaled),
         own_norms.reshape(-1, 1),
         own_ids.reshape(-1, 1),
         first_inverse,

time: 200 us -> 190 us (0.950)
  blocking collectives: 11.3 us -> 0 us
  Pallas kernels: 109 us -> 98.7 us
  starting transfers between devices: 13.1 us -> 19.3 us
  waiting for transfers between devices: 16.7 us -> 20.3 us
    all_to_all x1 -> x0, blocking collectives: 11.3 us -> none  [on_device(): moved = lax.all_to_all(blocks, 'row', 0, 0, tiled=True)]
    pallas_call x1, Pallas kernels: 40.3 us -> 29.6 us  [panel_stage(): pl.pallas_call(panel_kernel, grid=(row_count,), in_specs=[pl.BlockSpec(me...]
    all_to_all x0 -> x1, starting transfers between devices: none -> 6.2 us  [on_device(): moved = lax.all_to_all(blocks, 'row', 0, 0, tiled=True)]
    all_to_all x0 -> x1, waiting for transfers between devices: none -> 5.18 us  [on_device(): moved = lax.all_to_all(blocks, 'row', 0, 0, tiled=True)]
    unnamed x14 -> x12, local copies, waits for them, and re-layouts: 4.01 us -> 4.67 us
  transfers between devices with their start and end apart: 3 -> 4, of which waited for: 2 -> 3; matrix products, arithmetic and copies ran while one was open for 7% -> 8% of each run, Pallas kernels for 35% -> 37%
where the time goes in v3:
time: 190 us; the launch traced here: 189 us
  Pallas kernels  98.7 us (52%)
  waiting for transfers between devices  20.3 us (11%)
  starting transfers between devices  19.3 us (10%)
  local copies, waits for them, and re-layouts  19.1 us (10%)
  between operations  15 us (8%)
  other arithmetic  12 us (6%)
  matrix products  4.7 us (2%)
    pallas_call x2, Pallas kernels, lower_inverse(): pl.pallas_call(lower_inverse_kernel, out_shape=jax.ShapeDtypeStruct((size...  69.1 us
    pallas_call x1, Pallas kernels, panel_stage(): pl.pallas_call(panel_kernel, grid=(row_count,), in_specs=[pl.BlockSpec(me...  29.6 us
    all_to_all x2, waiting for transfers between devices, gather_by_all_to_all(): return lax.all_to_all(copies, axis_name, 0, 0, tiled=True)  15.1 us
    all_to_all x2, starting transfers between devices, gather_by_all_to_all(): return lax.all_to_all(copies, axis_name, 0, 0, tiled=True)  13.1 us
    reshape x1, local copies, waits for them, and re-layouts, on_device(): return finished.reshape(col_blocks, 1, BLK, 1, grid_rows)  6.82 us
    all_to_all x1, starting transfers between devices, on_device(): moved = lax.all_to_all(blocks, 'row', 0, 0, tiled=True)  6.2 us
    all_to_all x1, waiting for transfers between devices, on_device(): moved = lax.all_to_all(blocks, 'row', 0, 0, tiled=True)  5.18 us
    unnamed x12, local copies, waits for them, and re-layouts  4.67 us
  transfers between devices with their start and end apart: 4, of which 3 were waited for; matrix products, arithmetic and copies ran while one was open for 8% of the time, Pallas kernels for 37%

profile of v3, /device:TPU:1, one launch (start us, length us, event | category | flops | bytes accessed | tf_op | source)
XLA Modules:
  0.0 189.0 jit_solution(10717002555497824037)
XLA Ops:
  6.5 1.0 copy.48
  7.6 0.8 reshape.152
  8.4 6.2 %all-to-all-start = ((f32[8,1,4096]{2,1,0:T(1,128)}), f32[8,1,4096]{2,1,0:T(1,128)S(1)}, u32[]{:S(2)}, u32[]{:S(2)}) async-start(f32[8,1,4096]{2,1,0:T(1,128)} %reshape.152), calls=%async_computation | async-start | bytes 262144 | tf_op jit(solution)/shard_map/all_to_all | solution.py:179
  14.6 0.1 iota_add_fusion.1
  14.7 5.2 %all-to-all-done = f32[8,1,4096]{2,1,0:T(1,128)S(1)} async-done(((f32[8,1,4096]{2,1,0:T(1,128)}), f32[8,1,4096]{2,1,0:T(1,128)S(1)}, u32[]{:S(2)}, u32[]{:S(2)}) %all-to-all-start) | async-done | bytes 131104 | tf_op jit(solution)/shard_map/all_to_all | solution.py:179
  19.9 0.5 broadcast.127
  20.4 0.9 reduce.2
  21.3 0.1 reshape.153
  21.4 0.0 copy-start
  21.5 1.0 reshape.154
  22.5 9.6 %all-to-all-start.1 = ((f32[16,1,4096]{2,1,0:T(1,128)}), f32[16,1,4096]{2,1,0:T(1,128)S(1)}, u32[]{:S(2)}, u32[]{:S(2)}) async-start(f32[16,1,4096]{2,1,0:T(1,128)} %reshape.154), calls=%async_computation.1 | async-start | bytes 524288 | tf_op jit(solution)/shard_map/all_to_all | solution.py:162
  32.2 0.1 reshape.130
  32.3 0.0 copy-start.2
  32.3 8.8 %all-to-all-done.1 = f32[16,1,4096]{2,1,0:T(1,128)S(1)} async-done(((f32[16,1,4096]{2,1,0:T(1,128)}), f32[16,1,4096]{2,1,0:T(1,128)S(1)}, u32[]{:S(2)}, u32[]{:S(2)}) %all-to-all-start.1) | async-done | bytes 262176 | tf_op jit(solution)/shard_map/all_to_all | solution.py:162
  41.0 1.2 reduce.3
  42.3 0.2 reshape.155
  42.5 0.1 broadcast_in_dim.67
  42.6 1.2 reshape.156
  43.8 3.5 %all-to-all-start.2 = ((f32[8,1,12288]{2,1,0:T(1,128)}), f32[8,1,12288]{2,1,0:T(1,128)S(1)}, u32[]{:S(2)}, u32[]{:S(2)}) async-start(f32[8,1,12288]{2,1,0:T(1,128)} %reshape.156), calls=%async_computation.2 | async-start | bytes 786432 | tf_op jit(solution)/shard_map/all_to_all | solution.py:162
  47.3 0.0 all-gather.3.cloned.1.call-start
  47.4 0.1 reshape.150.own_ids_ref
  47.5 0.0 copy-start.1
  48.8 0.1 fusion.22
  48.9 0.1 iota_add_fusion
  49.0 6.3 %all-to-all-done.2 = f32[8,1,12288]{2,1,0:T(1,128)S(1)} async-done(((f32[8,1,12288]{2,1,0:T(1,128)}), f32[8,1,12288]{2,1,0:T(1,128)S(1)}, u32[]{:S(2)}, u32[]{:S(2)}) %all-to-all-start.2) | async-done | bytes 393248 | tf_op jit(solution)/shard_map/all_to_all | solution.py:162
  55.3 1.5 reduce.4
  56.8 0.3 reshape.157
  57.1 0.0 copy-done
  57.1 0.1 copy.49
  57.2 0.0 all-gather.3.cloned.1.call-update
  57.2 0.7 pad_maximum_fusion.2.consts_ref
  57.9 0.7 add.125.pid_ref
  58.6 0.7 select_convert_fusion.sel_ref
  59.3 0.0 copy-done.2
  59.3 0.3 multiply_reduce_fusion.1
  59.6 0.8 gather_fusion.1
  60.3 0.6 gather_fusion
  61.0 0.4 fusion.20
  61.4 0.1 copy.56
  61.5 0.1 copy.57
  61.6 0.8 fusion.13.a_ref
  62.5 34.6 %shard_map.46.finv_ref = f32[256,256]{1,0:T(8,128)} custom-call(f32[256,256]{1,0:T(8,128)} %fusion.13.a_ref), custom_call_target="tpu_custom_call" | custom-call | tf_op jit(solution)/shard_map/pallas_call | solution.py:73
  97.1 0.1 fusion.21
  97.2 1.0 fusion.4
  98.2 1.7 convolution_convert_fusion
  99.9 0.7 slice.78.mid_ref
  100.6 0.1 copy.54
  100.7 0.9 copy.61.cn_ref
  101.5 0.2 convolution_subtract_fusion
  101.8 0.1 copy.60
  102.0 0.7 fusion.7.a_ref
  102.7 34.4 %shard_map.47.sinv_ref = f32[256,256]{1,0:T(8,128)} custom-call(f32[256,256]{1,0:T(8,128)} %fusion.7.a_ref), custom_call_target="tpu_custom_call" | custom-call | tf_op jit(solution)/shard_map/pallas_call | solution.py:73
  137.1 0.7 concatenate.19.own_cs_ref
  137.9 0.1 fusion.6
  137.9 1.1 concatenate.18.cs_ref
  139.0 1.3 convolution_convert_fusion.1
  140.3 0.6 pad_maximum_fusion.own_panels_ref
  141.0 0.0 copy-done.1
  141.0 0.6 and_select_fusion.own_cn_ref
  141.6 0.0 all-gather.3.cloned.1.call-done
  141.6 3.3 %multiply_reduce_fusion = f32[16,8,64]{2,1,0:T(8,128)S(1)} fusion(f32[16,8,64,64]{3,2,1,0:T(8,128)} %bitcast.38, f32[64]{0:T(128)S(1)} %copy-done.2), kind=kLoop, calls=%fused_computation.2 | loop fusion | flops 1564672 | bytes 2130176 | tf_op jit(solution)/shard_map/reduce_sum | solution.py:192
  145.0 0.7 reshape.127.pnorm_ref
  145.7 29.6 %shard_map.48 = f32[96,8192]{1,0:T(8,128)} custom-call(f32[2]{0:T(128)} %pad_maximum_fusion.2.consts_ref, f32[16,8,64,64]{3,2,1,0:T(8,128)} %bitcast.39, f32[1,8192]{1,0:T(1,128)} %reshape.127.pnorm_ref, s32[1,8192]{1,0:T(1,128)} %add.125.pid_ref, f32[1,64]{1,0:T(1,128)} %bitcast.46, bf16[512,384]{1,0:T(8,128)(2,1)} %concatenate.18.cs_ref, ...), custom_call_target="tpu_custom_call" | custom-call | tf_op jit(solution)/shard_map/pallas_call | solution.py:140
  175.3 6.8 %copy.63 = f32[6,1,16,1,8192]{4,3,2,1,0:T(1,128)} copy(f32[6,1,16,1,8192]{4,2,0,3,1:T(8,128)} %bitcast.40) | data formatting | bytes 6291456 | tf_op jit(solution)/shard_map/reshape | solution.py:258
  (19 shorter events, 0.2 us)
Async XLA Ops:
  8.4 11.5 %all-to-all-start = ((f32[8,1,4096]{2,1,0:T(1,128)}), f32[8,1,4096]{2,1,0:T(1,128)S(1)}, u32[]{:S(2)}, u32[]{:S(2)}) async-start(f32[8,1,4096]{2,1,0:T(1,128)} %reshape.152), calls=%async_computation | async-start | bytes 262144 | tf_op jit(solution)/shard_map/all_to_all | solution.py:179
  21.4 35.7 %copy-start = (f32[8,64,64]{2,1,0:T(8,128)}, f32[8,64,64]{2,1,0:T(8,128)S(1)}, u32[]{:S(2)}) copy-start(f32[8,64,64]{2,1,0:T(8,128)S(1)} %reshape.153) | copy-start | bytes 393220
  22.5 18.5 %all-to-all-start.1 = ((f32[16,1,4096]{2,1,0:T(1,128)}), f32[16,1,4096]{2,1,0:T(1,128)S(1)}, u32[]{:S(2)}, u32[]{:S(2)}) async-start(f32[16,1,4096]{2,1,0:T(1,128)} %reshape.154), calls=%async_computation.1 | async-start | bytes 524288 | tf_op jit(solution)/shard_map/all_to_all | solution.py:162
  32.3 27.0 %copy-start.2 = (f32[64]{0:T(128)S(1)}, f32[64]{0:T(128)}, u32[]{:S(2)}) copy-start(f32[64]{0:T(128)} %param.5) | copy-start | bytes 772
  43.8 11.4 %all-to-all-start.2 = ((f32[8,1,12288]{2,1,0:T(1,128)}), f32[8,1,12288]{2,1,0:T(1,128)S(1)}, u32[]{:S(2)}, u32[]{:S(2)}) async-start(f32[8,1,12288]{2,1,0:T(1,128)} %reshape.156), calls=%async_computation.2 | async-start | bytes 786432 | tf_op jit(solution)/shard_map/all_to_all | solution.py:162
  47.3 94.3 %all-gather.3.cloned.1.call-start = ((), (), s32[]{:S(2)}) async-start(), calls=%async_computation.3 | async-start | bytes 4456448 | tf_op jit(solution)/shard_map/all_gather | solution.py:186
  47.5 93.5 %copy-start.1 = (s32[64,1]{1,0:T(8,128)}, s32[64,1]{1,0:T(8,128)S(1)}, u32[]{:S(2)}) copy-start(s32[64,1]{1,0:T(8,128)S(1)} %reshape.150.own_ids_ref) | copy-start | bytes 772
Sparse Core Ops, SparseCore 0:
  57.4 53.0 all-gather.2

commit v4 on v3

--- a/solution.py
+++ b/solution.py
@@ -31,23 +31,35 @@
     lane_row = lax.broadcasted_iota(jnp.int32, (1, half), 1)
     eye = jnp.where(lax.broadcasted_iota(jnp.int32, (half, half), 0) == lanes, 1.0, 0.0)
 
-    def step(k, carry):
+    def pick(values, index):
+        return jnp.sum(jnp.where(lane_row == index, values, 0.0), axis=1, keepdims=True)
+
+    def step(j, carry):
+        k = 2 * j
         s = s_ref[...]
         x = x_ref[...]
-        row = s_ref[pl.ds(k, 1), :]
-        col = jnp.sum(jnp.where(lanes == k, s, 0.0), axis=1, keepdims=True)
-        root = jnp.sqrt(jnp.sum(jnp.where(lane_row == k, row, 0.0), axis=1, keepdims=True))
-        col = jnp.where(rows >= k, col / root, 0.0)
-        row = jnp.where(lane_row >= k, row / root, 0.0)
-        s_ref[...] = s - col * row
-        xk = x_ref[pl.ds(k, 1), :] / root
-        x_ref[...] = jnp.where(rows == k, xk, x - jnp.where(rows > k, col, 0.0) * xk)
+        row0 = s_ref[pl.ds(k, 1), :]
+        row1 = s_ref[pl.ds(k + 1, 1), :]
+        col0 = jnp.sum(jnp.where(lanes == k, s, 0.0), axis=1, keepdims=True)
+        col1 = jnp.sum(jnp.where(lanes == k + 1, s, 0.0), axis=1, keepdims=True)
+        root0 = jnp.sqrt(pick(row0, k))
+        cross = pick(row1, k) / root0
+        root1 = jnp.sqrt(pick(row1, k + 1) - cross * cross)
+        col0 = jnp.where(rows >= k, col0 / root0, 0.0)
+        row0 = jnp.where(lane_row >= k, row0 / root0, 0.0)
+        col1 = jnp.where(rows >= k + 1, (col1 - col0 * cross) / root1, 0.0)
+        row1 = jnp.where(lane_row >= k + 1, (row1 - cross * row0) / root1, 0.0)
+        s_ref[...] = s - col0 * row0 - col1 * row1
+        x0 = x_ref[pl.ds(k, 1), :] / root0
+        x1 = (x_ref[pl.ds(k + 1, 1), :] - cross * x0) / root1
+        rest = x - jnp.where(rows > k, col0, 0.0) * x0 - jnp.where(rows > k + 1, col1, 0.0) * x1
+        x_ref[...] = jnp.where(rows == k, x0, jnp.where(rows == k + 1, x1, rest))
         return carry
 
     def base(block):
         s_ref[...] = block
         x_ref[...] = eye.astype(jnp.float32)
-        lax.fori_loop(0, half, step, 0)
+        lax.fori_loop(0, half // 2, step, 0)
         return x_ref[...]
 
     first = base(a_ref[:half, :half])

time: 190 us -> 168 us (0.88)
  Pallas kernels: 98.7 us -> 76.7 us
    pallas_call x2, Pallas kernels: 69.1 us -> 47 us  [lower_inverse(): pl.pallas_call(lower_inverse_kernel, out_shape=jax.ShapeDtypeStruct((size...]
  transfers between devices with their start and end apart: 4 -> 4, of which waited for: 3 -> 3; matrix products, arithmetic and copies ran while one was open for 8% -> 9% of each run, Pallas kernels for 37% -> 28%
where the time goes in v4:
time: 168 us; the launch traced here: 167 us
  Pallas kernels  76.7 us (46%)
  waiting for transfers between devices  20.1 us (12%)
  starting transfers between devices  19.5 us (12%)
  local copies, waits for them, and re-layouts  19.1 us (11%)
  between operations  15 us (9%)
  other arithmetic  12 us (7%)
  matrix products  4.7 us (3%)
    pallas_call x2, Pallas kernels, lower_inverse(): pl.pallas_call(lower_inverse_kernel, out_shape=jax.ShapeDtypeStruct((size...  47 us
    pallas_call x1, Pallas kernels, panel_stage(): pl.pallas_call(panel_kernel, grid=(row_count,), in_specs=[pl.BlockSpec(me...  29.6 us
    all_to_all x2, waiting for transfers between devices, gather_by_all_to_all(): return lax.all_to_all(copies, axis_name, 0, 0, tiled=True)  14.9 us
    all_to_all x2, starting transfers between devices, gather_by_all_to_all(): return lax.all_to_all(copies, axis_name, 0, 0, tiled=True)  13.1 us
    reshape x1, local copies, waits for them, and re-layouts, on_device(): return finished.reshape(col_blocks, 1, BLK, 1, grid_rows)  6.82 us
    all_to_all x1, starting transfers between devices, on_device(): moved = lax.all_to_all(blocks, 'row', 0, 0, tiled=True)  6.2 us
    all_to_all x1, waiting for transfers between devices, on_device(): moved = lax.all_to_all(blocks, 'row', 0, 0, tiled=True)  5.18 us
    unnamed x12, local copies, waits for them, and re-layouts  4.67 us
  transfers between devices with their start and end apart: 4, of which 3 were waited for; matrix products, arithmetic and copies ran while one was open for 9% of the time, Pallas kernels for 28%

profile of v4, /device:TPU:1, one launch (start us, length us, event | category | flops | bytes accessed | tf_op | source)
XLA Modules:
  0.0 167.0 jit_solution(10125282742723126253)
XLA Ops:
  6.5 1.0 copy.48
  7.6 0.8 reshape.152
  8.4 6.2 %all-to-all-start = ((f32[8,1,4096]{2,1,0:T(1,128)}), f32[8,1,4096]{2,1,0:T(1,128)S(1)}, u32[]{:S(2)}, u32[]{:S(2)}) async-start(f32[8,1,4096]{2,1,0:T(1,128)} %reshape.152), calls=%async_computation | async-start | bytes 262144 | tf_op jit(solution)/shard_map/all_to_all | solution.py:191
  14.6 0.1 iota_add_fusion.1
  14.7 5.2 %all-to-all-done = f32[8,1,4096]{2,1,0:T(1,128)S(1)} async-done(((f32[8,1,4096]{2,1,0:T(1,128)}), f32[8,1,4096]{2,1,0:T(1,128)S(1)}, u32[]{:S(2)}, u32[]{:S(2)}) %all-to-all-start) | async-done | bytes 131104 | tf_op jit(solution)/shard_map/all_to_all | solution.py:191
  19.9 0.5 broadcast.127
  20.4 0.9 reduce.2
  21.3 0.1 reshape.153
  21.4 0.0 copy-start
  21.5 1.0 reshape.154
  22.5 9.6 %all-to-all-start.1 = ((f32[16,1,4096]{2,1,0:T(1,128)}), f32[16,1,4096]{2,1,0:T(1,128)S(1)}, u32[]{:S(2)}, u32[]{:S(2)}) async-start(f32[16,1,4096]{2,1,0:T(1,128)} %reshape.154), calls=%async_computation.1 | async-start | bytes 524288 | tf_op jit(solution)/shard_map/all_to_all | solution.py:174
  32.2 0.1 reshape.130
  32.3 0.0 copy-start.2
  32.3 8.8 %all-to-all-done.1 = f32[16,1,4096]{2,1,0:T(1,128)S(1)} async-done(((f32[16,1,4096]{2,1,0:T(1,128)}), f32[16,1,4096]{2,1,0:T(1,128)S(1)}, u32[]{:S(2)}, u32[]{:S(2)}) %all-to-all-start.1) | async-done | bytes 262176 | tf_op jit(solution)/shard_map/all_to_all | solution.py:174
  41.0 1.2 reduce.3
  42.3 0.2 reshape.155
  42.5 0.1 broadcast_in_dim.67
  42.6 1.2 reshape.156
  43.8 3.5 %all-to-all-start.2 = ((f32[8,1,12288]{2,1,0:T(1,128)}), f32[8,1,12288]{2,1,0:T(1,128)S(1)}, u32[]{:S(2)}, u32[]{:S(2)}) async-start(f32[8,1,12288]{2,1,0:T(1,128)} %reshape.156), calls=%async_computation.2 | async-start | bytes 786432 | tf_op jit(solution)/shard_map/all_to_all | solution.py:174
  47.3 0.2 all-gather.3.cloned.1.call-start
  47.6 0.1 reshape.150.own_ids_ref
  47.6 0.0 copy-start.1
  49.0 0.1 fusion.22
  49.1 0.1 iota_add_fusion
  49.2 6.1 %all-to-all-done.2 = f32[8,1,12288]{2,1,0:T(1,128)S(1)} async-done(((f32[8,1,12288]{2,1,0:T(1,128)}), f32[8,1,12288]{2,1,0:T(1,128)S(1)}, u32[]{:S(2)}, u32[]{:S(2)}) %all-to-all-start.2) | async-done | bytes 393248 | tf_op jit(solution)/shard_map/all_to_all | solution.py:174
  55.3 1.5 reduce.4
  56.8 0.3 reshape.157
  57.1 0.0 copy-done
  57.1 0.1 copy.49
  57.2 0.0 all-gather.3.cloned.1.call-update
  57.2 0.7 pad_maximum_fusion.2.consts_ref
  57.9 0.7 add.125.pid_ref
  58.6 0.7 select_convert_fusion.sel_ref
  59.3 0.0 copy-done.2
  59.3 0.3 multiply_reduce_fusion.1
  59.6 0.8 gather_fusion.1
  60.3 0.6 gather_fusion
  61.0 0.4 fusion.20
  61.4 0.1 copy.56
  61.5 0.1 copy.57
  61.6 0.8 fusion.13.a_ref
  62.5 23.5 %shard_map.46.finv_ref = f32[256,256]{1,0:T(8,128)} custom-call(f32[256,256]{1,0:T(8,128)} %fusion.13.a_ref), custom_call_target="tpu_custom_call" | custom-call | tf_op jit(solution)/shard_map/pallas_call | solution.py:85
  86.0 0.1 fusion.21
  86.1 1.0 fusion.4
  87.1 1.7 %convolution_convert_fusion = bf16[320,256]{1,0:T(8,128)(2,1)S(1)} fusion(f32[256,256]{1,0:T(8,128)} %shard_map.46.finv_ref, f32[320,512]{0,1:T(8,128)S(1)} %fusion.4), kind=kOutput, calls=%fused_computation.11 | convolution fusion | flops 251740160 | bytes 819200 | tf_op jit(solution)/shard_map/dot_general | solution.py:233
  88.8 0.7 slice.78.mid_ref
  89.5 0.1 copy.54
  89.6 0.9 copy.61.cn_ref
  90.4 0.2 convolution_subtract_fusion
  90.7 0.1 copy.60
  90.9 0.7 fusion.7.a_ref
  91.6 23.5 %shard_map.47.sinv_ref = f32[256,256]{1,0:T(8,128)} custom-call(f32[256,256]{1,0:T(8,128)} %fusion.7.a_ref), custom_call_target="tpu_custom_call" | custom-call | tf_op jit(solution)/shard_map/pallas_call | solution.py:85
  115.1 0.7 concatenate.19.own_cs_ref
  115.9 0.1 fusion.6
  115.9 1.1 concatenate.18.cs_ref
  117.0 1.3 convolution_convert_fusion.1
  118.3 0.6 pad_maximum_fusion.own_panels_ref
  119.0 0.0 copy-done.1
  119.0 0.6 and_select_fusion.own_cn_ref
  119.6 0.0 all-gather.3.cloned.1.call-done
  119.6 3.3 %multiply_reduce_fusion = f32[16,8,64]{2,1,0:T(8,128)S(1)} fusion(f32[16,8,64,64]{3,2,1,0:T(8,128)} %bitcast.38, f32[64]{0:T(128)S(1)} %copy-done.2), kind=kLoop, calls=%fused_computation.2 | loop fusion | flops 1564672 | bytes 2130176 | tf_op jit(solution)/shard_map/reduce_sum | solution.py:204
  123.0 0.7 reshape.127.pnorm_ref
  123.7 29.6 %shard_map.48 = f32[96,8192]{1,0:T(8,128)} custom-call(f32[2]{0:T(128)} %pad_maximum_fusion.2.consts_ref, f32[16,8,64,64]{3,2,1,0:T(8,128)} %bitcast.39, f32[1,8192]{1,0:T(1,128)} %reshape.127.pnorm_ref, s32[1,8192]{1,0:T(1,128)} %add.125.pid_ref, f32[1,64]{1,0:T(1,128)} %bitcast.46, bf16[512,384]{1,0:T(8,128)(2,1)} %concatenate.18.cs_ref, ...), custom_call_target="tpu_custom_call" | custom-call | tf_op jit(solution)/shard_map/pallas_call | solution.py:152
  153.3 6.8 %copy.63 = f32[6,1,16,1,8192]{4,3,2,1,0:T(1,128)} copy(f32[6,1,16,1,8192]{4,2,0,3,1:T(8,128)} %bitcast.40) | data formatting | bytes 6291456 | tf_op jit(solution)/shard_map/reshape | solution.py:270
  (19 shorter events, 0.2 us)
Async XLA Ops:
  8.4 11.5 %all-to-all-start = ((f32[8,1,4096]{2,1,0:T(1,128)}), f32[8,1,4096]{2,1,0:T(1,128)S(1)}, u32[]{:S(2)}, u32[]{:S(2)}) async-start(f32[8,1,4096]{2,1,0:T(1,128)} %reshape.152), calls=%async_computation | async-start | bytes 262144 | tf_op jit(solution)/shard_map/all_to_all | solution.py:191
  21.4 35.7 %copy-start = (f32[8,64,64]{2,1,0:T(8,128)}, f32[8,64,64]{2,1,0:T(8,128)S(1)}, u32[]{:S(2)}) copy-start(f32[8,64,64]{2,1,0:T(8,128)S(1)} %reshape.153) | copy-start | bytes 393220
  22.5 18.5 %all-to-all-start.1 = ((f32[16,1,4096]{2,1,0:T(1,128)}), f32[16,1,4096]{2,1,0:T(1,128)S(1)}, u32[]{:S(2)}, u32[]{:S(2)}) async-start(f32[16,1,4096]{2,1,0:T(1,128)} %reshape.154), calls=%async_computation.1 | async-start | bytes 524288 | tf_op jit(solution)/shard_map/all_to_all | solution.py:174
  32.3 27.0 %copy-start.2 = (f32[64]{0:T(128)S(1)}, f32[64]{0:T(128)}, u32[]{:S(2)}) copy-start(f32[64]{0:T(128)} %param.5) | copy-start | bytes 772
  43.8 11.4 %all-to-all-start.2 = ((f32[8,1,12288]{2,1,0:T(1,128)}), f32[8,1,12288]{2,1,0:T(1,128)S(1)}, u32[]{:S(2)}, u32[]{:S(2)}) async-start(f32[8,1,12288]{2,1,0:T(1,128)} %reshape.156), calls=%async_computation.2 | async-start | bytes 786432 | tf_op jit(solution)/shard_map/all_to_all | solution.py:174
  47.3 72.3 %all-gather.3.cloned.1.call-start = ((), (), s32[]{:S(2)}) async-start(), calls=%async_computation.3 | async-start | bytes 4456448 | tf_op jit(solution)/shard_map/all_gather | solution.py:198
  47.6 71.3 %copy-start.1 = (s32[64,1]{1,0:T(8,128)}, s32[64,1]{1,0:T(8,128)S(1)}, u32[]{:S(2)}) copy-start(s32[64,1]{1,0:T(8,128)S(1)} %reshape.150.own_ids_ref) | copy-start | bytes 772
Sparse Core Ops, SparseCore 0:
  57.4 52.9 all-gather.2

commit v5 on v3

--- a/solution.py
+++ b/solution.py
@@ -11,6 +11,7 @@
 BLK = 16
 
 HIGHEST = lax.Precision.HIGHEST
+WIDTH = 4
 
 
 def kernel_block(left, left_norms, right, right_norms, signal):
@@ -31,23 +32,44 @@
     lane_row = lax.broadcasted_iota(jnp.int32, (1, half), 1)
     eye = jnp.where(lax.broadcasted_iota(jnp.int32, (half, half), 0) == lanes, 1.0, 0.0)
 
-    def step(k, carry):
+    def pick(values, index):
+        return jnp.sum(jnp.where(lane_row == index, values, 0.0), axis=1, keepdims=True)
+
+    def step(j, carry):
+        k = WIDTH * j
         s = s_ref[...]
         x = x_ref[...]
-        row = s_ref[pl.ds(k, 1), :]
-        col = jnp.sum(jnp.where(lanes == k, s, 0.0), axis=1, keepdims=True)
-        root = jnp.sqrt(jnp.sum(jnp.where(lane_row == k, row, 0.0), axis=1, keepdims=True))
-        col = jnp.where(rows >= k, col / root, 0.0)
-        row = jnp.where(lane_row >= k, row / root, 0.0)
-        s_ref[...] = s - col * row
-        xk = x_ref[pl.ds(k, 1), :] / root
-        x_ref[...] = jnp.where(rows == k, xk, x - jnp.where(rows > k, col, 0.0) * xk)
+        cols, rows_out, xs = [], [], []
+        update = s
+        rest = x
+        for m in range(WIDTH):
+            col = jnp.sum(jnp.where(lanes == k + m, s, 0.0), axis=1, keepdims=True)
+            row = s_ref[pl.ds(k + m, 1), :]
+            xm = x_ref[pl.ds(k + m, 1), :]
+            for p in range(m):
+                factor = pick(rows_out[p], k + m)
+                col = col - cols[p] * factor
+                row = row - factor * rows_out[p]
+                xm = xm - factor * xs[p]
+            root = jnp.sqrt(pick(row, k + m))
+            col = jnp.where(rows >= k + m, col / root, 0.0)
+            row = jnp.where(lane_row >= k + m, row / root, 0.0)
+            xm = xm / root
+            cols.append(col)
+            rows_out.append(row)
+            xs.append(xm)
+            update = update - col * row
+            rest = rest - jnp.where(rows > k + m, col, 0.0) * xm
+        s_ref[...] = update
+        for m in range(WIDTH):
+            rest = jnp.where(rows == k + m, xs[m], rest)
+        x_ref[...] = rest
         return carry
 
     def base(block):
         s_ref[...] = block
         x_ref[...] = eye.astype(jnp.float32)
-        lax.fori_loop(0, half, step, 0)
+        lax.fori_loop(0, half // WIDTH, step, 0)
         return x_ref[...]
 
     first = base(a_ref[:half, :half])

time: 190 us -> 212 us (1.12)
  Pallas kernels: 98.7 us -> 121 us
    pallas_call x2, Pallas kernels: 69.1 us -> 91.1 us  [lower_inverse(): pl.pallas_call(lower_inverse_kernel, out_shape=jax.ShapeDtypeStruct((size...]
  transfers between devices with their start and end apart: 4 -> 4, of which waited for: 3 -> 3; matrix products, arithmetic and copies ran while one was open for 8% -> 7% of each run, Pallas kernels for 37% -> 43%
where the time goes in v5:
time: 212 us; the launch traced here: 211 us
  Pallas kernels  121 us (57%)
  waiting for transfers between devices  20.3 us (10%)
  starting transfers between devices  19.3 us (9%)
  local copies, waits for them, and re-layouts  19.1 us (9%)
  between operations  15 us (7%)
  other arithmetic  12 us (6%)
  matrix products  4.7 us (2%)
    pallas_call x2, Pallas kernels, lower_inverse(): pl.pallas_call(lower_inverse_kernel, out_shape=jax.ShapeDtypeStruct((size...  91.1 us
    pallas_call x1, Pallas kernels, panel_stage(): pl.pallas_call(panel_kernel, grid=(row_count,), in_specs=[pl.BlockSpec(me...  29.6 us
    all_to_all x2, waiting for transfers between devices, gather_by_all_to_all(): return lax.all_to_all(copies, axis_name, 0, 0, tiled=True)  15.1 us
    all_to_all x2, starting transfers between devices, gather_by_all_to_all(): return lax.all_to_all(copies, axis_name, 0, 0, tiled=True)  13.1 us
    reshape x1, local copies, waits for them, and re-layouts, on_device(): return finished.reshape(col_blocks, 1, BLK, 1, grid_rows)  6.82 us
    all_to_all x1, starting transfers between devices, on_device(): moved = lax.all_to_all(blocks, 'row', 0, 0, tiled=True)  6.2 us
    all_to_all x1, waiting for transfers between devices, on_device(): moved = lax.all_to_all(blocks, 'row', 0, 0, tiled=True)  5.18 us
    unnamed x12, local copies, waits for them, and re-layouts  4.67 us
  transfers between devices with their start and end apart: 4, of which 3 were waited for; matrix products, arithmetic and copies ran while one was open for 7% of the time, Pallas kernels for 43%

profile of v5, /device:TPU:1, one launch (start us, length us, event | category | flops | bytes accessed | tf_op | source)
XLA Modules:
  0.0 211.0 jit_solution(5864999745463908276)
XLA Ops:
  6.5 1.0 copy.48
  7.6 0.8 reshape.152
  8.4 6.2 %all-to-all-start = ((f32[8,1,4096]{2,1,0:T(1,128)}), f32[8,1,4096]{2,1,0:T(1,128)S(1)}, u32[]{:S(2)}, u32[]{:S(2)}) async-start(f32[8,1,4096]{2,1,0:T(1,128)} %reshape.152), calls=%async_computation | async-start | bytes 262144 | tf_op jit(solution)/shard_map/all_to_all | solution.py:201
  14.6 0.1 iota_add_fusion.1
  14.7 5.2 %all-to-all-done = f32[8,1,4096]{2,1,0:T(1,128)S(1)} async-done(((f32[8,1,4096]{2,1,0:T(1,128)}), f32[8,1,4096]{2,1,0:T(1,128)S(1)}, u32[]{:S(2)}, u32[]{:S(2)}) %all-to-all-start) | async-done | bytes 131104 | tf_op jit(solution)/shard_map/all_to_all | solution.py:201
  19.9 0.5 broadcast.127
  20.4 0.9 reduce.2
  21.3 0.1 reshape.153
  21.4 0.0 copy-start
  21.5 1.0 reshape.154
  22.5 9.6 %all-to-all-start.1 = ((f32[16,1,4096]{2,1,0:T(1,128)}), f32[16,1,4096]{2,1,0:T(1,128)S(1)}, u32[]{:S(2)}, u32[]{:S(2)}) async-start(f32[16,1,4096]{2,1,0:T(1,128)} %reshape.154), calls=%async_computation.1 | async-start | bytes 524288 | tf_op jit(solution)/shard_map/all_to_all | solution.py:184
  32.2 0.1 reshape.130
  32.3 0.0 copy-start.2
  32.3 8.8 %all-to-all-done.1 = f32[16,1,4096]{2,1,0:T(1,128)S(1)} async-done(((f32[16,1,4096]{2,1,0:T(1,128)}), f32[16,1,4096]{2,1,0:T(1,128)S(1)}, u32[]{:S(2)}, u32[]{:S(2)}) %all-to-all-start.1) | async-done | bytes 262176 | tf_op jit(solution)/shard_map/all_to_all | solution.py:184
  41.0 1.2 reduce.3
  42.3 0.2 reshape.155
  42.5 0.1 broadcast_in_dim.67
  42.6 1.2 reshape.156
  43.8 3.5 %all-to-all-start.2 = ((f32[8,1,12288]{2,1,0:T(1,128)}), f32[8,1,12288]{2,1,0:T(1,128)S(1)}, u32[]{:S(2)}, u32[]{:S(2)}) async-start(f32[8,1,12288]{2,1,0:T(1,128)} %reshape.156), calls=%async_computation.2 | async-start | bytes 786432 | tf_op jit(solution)/shard_map/all_to_all | solution.py:184
  47.3 0.0 all-gather.3.cloned.1.call-start
  47.4 0.1 reshape.150.own_ids_ref
  47.5 0.0 copy-start.1
  48.8 0.1 fusion.22
  48.9 0.1 iota_add_fusion
  49.0 6.3 %all-to-all-done.2 = f32[8,1,12288]{2,1,0:T(1,128)S(1)} async-done(((f32[8,1,12288]{2,1,0:T(1,128)}), f32[8,1,12288]{2,1,0:T(1,128)S(1)}, u32[]{:S(2)}, u32[]{:S(2)}) %all-to-all-start.2) | async-done | bytes 393248 | tf_op jit(solution)/shard_map/all_to_all | solution.py:184
  55.3 1.5 reduce.4
  56.8 0.3 reshape.157
  57.1 0.0 copy-done
  57.1 0.1 copy.49
  57.2 0.0 all-gather.3.cloned.1.call-update
  57.2 0.7 pad_maximum_fusion.2.consts_ref
  57.9 0.7 add.125.pid_ref
  58.6 0.7 select_convert_fusion.sel_ref
  59.3 0.0 copy-done.2
  59.3 0.3 multiply_reduce_fusion.1
  59.6 0.8 gather_fusion.1
  60.3 0.6 gather_fusion
  61.0 0.4 fusion.20
  61.4 0.1 copy.56
  61.5 0.1 copy.57
  61.6 0.8 fusion.13.a_ref
  62.5 45.6 %shard_map.46.finv_ref = f32[256,256]{1,0:T(8,128)} custom-call(f32[256,256]{1,0:T(8,128)} %fusion.13.a_ref), custom_call_target="tpu_custom_call" | custom-call | tf_op jit(solution)/shard_map/pallas_call | solution.py:95
  108.1 0.1 fusion.21
  108.2 1.0 fusion.4
  109.2 1.7 convolution_convert_fusion
  110.9 0.7 slice.78.mid_ref
  111.6 0.1 copy.54
  111.7 0.9 copy.61.cn_ref
  112.5 0.2 convolution_subtract_fusion
  112.8 0.1 copy.60
  113.0 0.7 fusion.7.a_ref
  113.7 45.4 %shard_map.47.sinv_ref = f32[256,256]{1,0:T(8,128)} custom-call(f32[256,256]{1,0:T(8,128)} %fusion.7.a_ref), custom_call_target="tpu_custom_call" | custom-call | tf_op jit(solution)/shard_map/pallas_call | solution.py:95
  159.1 0.7 concatenate.19.own_cs_ref
  159.9 0.1 fusion.6
  159.9 1.1 concatenate.18.cs_ref
  161.0 1.3 convolution_convert_fusion.1
  162.3 0.6 pad_maximum_fusion.own_panels_ref
  163.0 0.0 copy-done.1
  163.0 0.6 and_select_fusion.own_cn_ref
  163.6 0.0 all-gather.3.cloned.1.call-done
  163.6 3.3 %multiply_reduce_fusion = f32[16,8,64]{2,1,0:T(8,128)S(1)} fusion(f32[16,8,64,64]{3,2,1,0:T(8,128)} %bitcast.38, f32[64]{0:T(128)S(1)} %copy-done.2), kind=kLoop, calls=%fused_computation.2 | loop fusion | flops 1564672 | bytes 2130176 | tf_op jit(solution)/shard_map/reduce_sum | solution.py:214
  167.0 0.7 reshape.127.pnorm_ref
  167.7 29.6 %shard_map.48 = f32[96,8192]{1,0:T(8,128)} custom-call(f32[2]{0:T(128)} %pad_maximum_fusion.2.consts_ref, f32[16,8,64,64]{3,2,1,0:T(8,128)} %bitcast.39, f32[1,8192]{1,0:T(1,128)} %reshape.127.pnorm_ref, s32[1,8192]{1,0:T(1,128)} %add.125.pid_ref, f32[1,64]{1,0:T(1,128)} %bitcast.46, bf16[512,384]{1,0:T(8,128)(2,1)} %concatenate.18.cs_ref, ...), custom_call_target="tpu_custom_call" | custom-call | tf_op jit(solution)/shard_map/pallas_call | solution.py:162
  197.3 6.8 %copy.63 = f32[6,1,16,1,8192]{4,3,2,1,0:T(1,128)} copy(f32[6,1,16,1,8192]{4,2,0,3,1:T(8,128)} %bitcast.40) | data formatting | bytes 6291456 | tf_op jit(solution)/shard_map/reshape | solution.py:280
  (19 shorter events, 0.2 us)
Async XLA Ops:
  8.4 11.5 %all-to-all-start = ((f32[8,1,4096]{2,1,0:T(1,128)}), f32[8,1,4096]{2,1,0:T(1,128)S(1)}, u32[]{:S(2)}, u32[]{:S(2)}) async-start(f32[8,1,4096]{2,1,0:T(1,128)} %reshape.152), calls=%async_computation | async-start | bytes 262144 | tf_op jit(solution)/shard_map/all_to_all | solution.py:201
  21.4 35.7 %copy-start = (f32[8,64,64]{2,1,0:T(8,128)}, f32[8,64,64]{2,1,0:T(8,128)S(1)}, u32[]{:S(2)}) copy-start(f32[8,64,64]{2,1,0:T(8,128)S(1)} %reshape.153) | copy-start | bytes 393220
  22.5 18.5 %all-to-all-start.1 = ((f32[16,1,4096]{2,1,0:T(1,128)}), f32[16,1,4096]{2,1,0:T(1,128)S(1)}, u32[]{:S(2)}, u32[]{:S(2)}) async-start(f32[16,1,4096]{2,1,0:T(1,128)} %reshape.154), calls=%async_computation.1 | async-start | bytes 524288 | tf_op jit(solution)/shard_map/all_to_all | solution.py:184
  32.3 27.0 %copy-start.2 = (f32[64]{0:T(128)S(1)}, f32[64]{0:T(128)}, u32[]{:S(2)}) copy-start(f32[64]{0:T(128)} %param.5) | copy-start | bytes 772
  43.8 11.4 %all-to-all-start.2 = ((f32[8,1,12288]{2,1,0:T(1,128)}), f32[8,1,12288]{2,1,0:T(1,128)S(1)}, u32[]{:S(2)}, u32[]{:S(2)}) async-start(f32[8,1,12288]{2,1,0:T(1,128)} %reshape.156), calls=%async_computation.2 | async-start | bytes 786432 | tf_op jit(solution)/shard_map/all_to_all | solution.py:184
  47.3 116.3 %all-gather.3.cloned.1.call-start = ((), (), s32[]{:S(2)}) async-start(), calls=%async_computation.3 | async-start | bytes 4456448 | tf_op jit(solution)/shard_map/all_gather | solution.py:208
  47.5 115.5 %copy-start.1 = (s32[64,1]{1,0:T(8,128)}, s32[64,1]{1,0:T(8,128)S(1)}, u32[]{:S(2)}) copy-start(s32[64,1]{1,0:T(8,128)S(1)} %reshape.150.own_ids_ref) | copy-start | bytes 772
Sparse Core Ops, SparseCore 0:
  57.4 53.1 all-gather.2

commit v6 on v4

--- a/solution.py
+++ b/solution.py
@@ -135,9 +135,17 @@
     both = jnp.concatenate([first, second], axis=0)
     trailing = own - jnp.dot(own_panels_ref[...], both, preferred_element_type=jnp.float32)
     sel = sel_ref[...]
-    out_ref[:BLK] = jnp.dot(sel, first, preferred_element_type=jnp.float32)
-    out_ref[BLK : 2 * BLK] = jnp.dot(sel, second, preferred_element_type=jnp.float32)
-    out_ref[2 * BLK :] = trailing
+    result = jnp.concatenate(
+        [
+            jnp.dot(sel, first, preferred_element_type=jnp.float32),
+            jnp.dot(sel, second, preferred_element_type=jnp.float32),
+            trailing,
+        ],
+        axis=0,
+    )
+    lanes = out_ref.shape[2]
+    for chunk in range(out_ref.shape[1]):
+        out_ref[:, chunk, :] = result[:, chunk * lanes : (chunk + 1) * lanes]
 
 
 def panel_stage(consts, gathered, pnorm, pid, scales, cs, cn, own_cs, own_cn, own_ids, finv, sinv, mid, own_panels, sel):
@@ -159,8 +167,8 @@
             pl.BlockSpec((1, tile), lambda i: (0, i)),
         ]
         + [whole(a) for a in (scales, cs, cn, own_cs, own_cn, own_ids, finv, sinv, mid, own_panels, sel)],
-        out_specs=pl.BlockSpec((out_rows, tile), lambda i: (0, i)),
-        out_shape=jax.ShapeDtypeStruct((out_rows, grid_rows), jnp.float32),
+        out_specs=pl.BlockSpec((out_rows, tile // 128, 128), lambda i: (0, i, 0)),
+        out_shape=jax.ShapeDtypeStruct((out_rows, grid_rows // 128, 128), jnp.float32),
     )(consts, gathered, pnorm, pid, scales, cs, cn, own_cs, own_cn, own_ids, finv, sinv, mid, own_panels, sel)
 
 

time: 168 us -> 162 us (0.964)
  local copies, waits for them, and re-layouts: 19.1 us -> 12.3 us
    reshape x1 -> x0, local copies, waits for them, and re-layouts: 6.82 us -> none  [on_device(): return finished.reshape(col_blocks, 1, BLK, 1, grid_rows)]
  transfers between devices with their start and end apart: 4 -> 4, of which waited for: 3 -> 3; matrix products, arithmetic and copies ran while one was open for 9% -> 10% of each run, Pallas kernels for 28% -> 29%
where the time goes in v6:
time: 162 us; the launch traced here: 161 us
  Pallas kernels  77.5 us (48%)
  waiting for transfers between devices  20.1 us (12%)
  starting transfers between devices  19.5 us (12%)
  between operations  15 us (9%)
  local copies, waits for them, and re-layouts  12.3 us (8%)
  other arithmetic  11.9 us (7%)
  matrix products  4.7 us (3%)
    pallas_call x2, Pallas kernels, lower_inverse(): pl.pallas_call(lower_inverse_kernel, out_shape=jax.ShapeDtypeStruct((size...  47.1 us
    pallas_call x1, Pallas kernels, panel_stage(): pl.pallas_call(panel_kernel, grid=(row_count,), in_specs=[pl.BlockSpec(me...  30.4 us
    all_to_all x2, waiting for transfers between devices, gather_by_all_to_all(): return lax.all_to_all(copies, axis_name, 0, 0, tiled=True)  14.9 us
    all_to_all x2, starting transfers between devices, gather_by_all_to_all(): return lax.all_to_all(copies, axis_name, 0, 0, tiled=True)  13.1 us
    all_to_all x1, starting transfers between devices, on_device(): moved = lax.all_to_all(blocks, 'row', 0, 0, tiled=True)  6.2 us
    all_to_all x1, waiting for transfers between devices, on_device(): moved = lax.all_to_all(blocks, 'row', 0, 0, tiled=True)  5.18 us
    unnamed x12, local copies, waits for them, and re-layouts  4.67 us
    reduce_sum x1, other arithmetic, on_device(): jnp.sum(gathered_scaled * gathered_scaled, axis=3).transpose(1, 0, 2)  3.34 us
  transfers between devices with their start and end apart: 4, of which 3 were waited for; matrix products, arithmetic and copies ran while one was open for 10% of the time, Pallas kernels for 29%

profile of v6, /device:TPU:1, one launch (start us, length us, event | category | flops | bytes accessed | tf_op | source)
XLA Modules:
  0.0 160.9 jit_solution(1251737990215386033)
XLA Ops:
  6.5 1.0 copy.48
  7.6 0.8 reshape.152
  8.4 6.2 %all-to-all-start = ((f32[8,1,4096]{2,1,0:T(1,128)}), f32[8,1,4096]{2,1,0:T(1,128)S(1)}, u32[]{:S(2)}, u32[]{:S(2)}) async-start(f32[8,1,4096]{2,1,0:T(1,128)} %reshape.152), calls=%async_computation | async-start | bytes 262144 | tf_op jit(solution)/shard_map/all_to_all | solution.py:199
  14.6 0.1 iota_add_fusion.1
  14.7 5.2 %all-to-all-done = f32[8,1,4096]{2,1,0:T(1,128)S(1)} async-done(((f32[8,1,4096]{2,1,0:T(1,128)}), f32[8,1,4096]{2,1,0:T(1,128)S(1)}, u32[]{:S(2)}, u32[]{:S(2)}) %all-to-all-start) | async-done | bytes 131104 | tf_op jit(solution)/shard_map/all_to_all | solution.py:199
  19.9 0.5 broadcast.127
  20.4 0.9 reduce.2
  21.3 0.1 reshape.153
  21.5 0.0 copy-start
  21.5 1.0 reshape.154
  22.6 9.6 %all-to-all-start.1 = ((f32[16,1,4096]{2,1,0:T(1,128)}), f32[16,1,4096]{2,1,0:T(1,128)S(1)}, u32[]{:S(2)}, u32[]{:S(2)}) async-start(f32[16,1,4096]{2,1,0:T(1,128)} %reshape.154), calls=%async_computation.1 | async-start | bytes 524288 | tf_op jit(solution)/shard_map/all_to_all | solution.py:182
  32.2 0.1 reshape.130
  32.3 0.0 copy-start.2
  32.3 8.8 %all-to-all-done.1 = f32[16,1,4096]{2,1,0:T(1,128)S(1)} async-done(((f32[16,1,4096]{2,1,0:T(1,128)}), f32[16,1,4096]{2,1,0:T(1,128)S(1)}, u32[]{:S(2)}, u32[]{:S(2)}) %all-to-all-start.1) | async-done | bytes 262176 | tf_op jit(solution)/shard_map/all_to_all | solution.py:182
  41.1 1.2 reduce.3
  42.3 0.2 reshape.155
  42.6 0.1 broadcast_in_dim.67
  42.6 1.2 reshape.156
  43.9 3.5 %all-to-all-start.2 = ((f32[8,1,12288]{2,1,0:T(1,128)}), f32[8,1,12288]{2,1,0:T(1,128)S(1)}, u32[]{:S(2)}, u32[]{:S(2)}) async-start(f32[8,1,12288]{2,1,0:T(1,128)} %reshape.156), calls=%async_computation.2 | async-start | bytes 786432 | tf_op jit(solution)/shard_map/all_to_all | solution.py:182
  47.3 0.2 all-gather.3.cloned.1.call-start
  47.6 0.1 reshape.150.own_ids_ref
  47.7 0.0 copy-start.1
  49.0 0.1 fusion.22
  49.1 0.1 iota_add_fusion
  49.2 6.1 %all-to-all-done.2 = f32[8,1,12288]{2,1,0:T(1,128)S(1)} async-done(((f32[8,1,12288]{2,1,0:T(1,128)}), f32[8,1,12288]{2,1,0:T(1,128)S(1)}, u32[]{:S(2)}, u32[]{:S(2)}) %all-to-all-start.2) | async-done | bytes 393248 | tf_op jit(solution)/shard_map/all_to_all | solution.py:182
  55.3 1.6 reduce.4
  56.9 0.3 reshape.157
  57.2 0.0 copy-done
  57.2 0.1 copy.49
  57.3 0.0 all-gather.3.cloned.1.call-update
  57.3 0.6 pad_maximum_fusion.2.consts_ref
  57.9 0.7 add.125.pid_ref
  58.6 0.7 select_convert_fusion.sel_ref
  59.3 0.0 copy-done.2
  59.3 0.3 multiply_reduce_fusion.1
  59.6 0.8 gather_fusion.1
  60.3 0.6 gather_fusion
  60.9 0.4 fusion.20
  61.3 0.1 copy.56
  61.5 0.1 copy.57
  61.6 0.8 fusion.13.a_ref
  62.4 23.5 %shard_map.46.finv_ref = f32[256,256]{1,0:T(8,128)} custom-call(f32[256,256]{1,0:T(8,128)} %fusion.13.a_ref), custom_call_target="tpu_custom_call" | custom-call | tf_op jit(solution)/shard_map/pallas_call | solution.py:85
  86.0 0.1 fusion.21
  86.1 1.0 fusion.4
  87.1 1.7 %convolution_convert_fusion = bf16[320,256]{1,0:T(8,128)(2,1)S(1)} fusion(f32[256,256]{1,0:T(8,128)} %shard_map.46.finv_ref, f32[320,512]{0,1:T(8,128)S(1)} %fusion.4), kind=kOutput, calls=%fused_computation.11 | convolution fusion | flops 251740160 | bytes 819200 | tf_op jit(solution)/shard_map/dot_general | solution.py:241
  88.8 0.7 slice.78.mid_ref
  89.5 0.1 copy.54
  89.6 0.8 copy.61.cn_ref
  90.4 0.2 convolution_subtract_fusion
  90.7 0.1 copy.60
  90.9 0.7 fusion.7.a_ref
  91.6 23.5 %shard_map.47.sinv_ref = f32[256,256]{1,0:T(8,128)} custom-call(f32[256,256]{1,0:T(8,128)} %fusion.7.a_ref), custom_call_target="tpu_custom_call" | custom-call | tf_op jit(solution)/shard_map/pallas_call | solution.py:85
  115.2 0.7 concatenate.19.own_cs_ref
  115.9 0.1 fusion.6
  116.0 1.1 concatenate.18.cs_ref
  117.0 1.3 convolution_convert_fusion.1
  118.4 0.6 pad_maximum_fusion.own_panels_ref
  119.0 0.0 copy-done.1
  119.0 0.6 and_select_fusion.own_cn_ref
  119.6 0.0 all-gather.3.cloned.1.call-done
  119.6 3.3 %multiply_reduce_fusion = f32[16,8,64]{2,1,0:T(8,128)S(1)} fusion(f32[16,8,64,64]{3,2,1,0:T(8,128)} %bitcast.38, f32[64]{0:T(128)S(1)} %copy-done.2), kind=kLoop, calls=%fused_computation.2 | loop fusion | flops 1564672 | bytes 2130176 | tf_op jit(solution)/shard_map/reduce_sum | solution.py:212
  123.0 0.7 reshape.127.pnorm_ref
  123.7 30.4 %shard_map.48 = f32[96,64,128]{2,1,0:T(8,128)} custom-call(f32[2]{0:T(128)} %pad_maximum_fusion.2.consts_ref, f32[16,8,64,64]{3,2,1,0:T(8,128)} %bitcast.39, f32[1,8192]{1,0:T(1,128)} %reshape.127.pnorm_ref, s32[1,8192]{1,0:T(1,128)} %add.125.pid_ref, f32[1,64]{1,0:T(1,128)} %bitcast.45, bf16[512,384]{1,0:T(8,128)(2,1)} %concatenate.18.cs_ref, ...), custom_call_target="tpu_custom_call" | custom-call | tf_op jit(solution)/shard_map/pallas_call | solution.py:160
  (19 shorter events, 0.2 us)
Async XLA Ops:
  8.4 11.5 %all-to-all-start = ((f32[8,1,4096]{2,1,0:T(1,128)}), f32[8,1,4096]{2,1,0:T(1,128)S(1)}, u32[]{:S(2)}, u32[]{:S(2)}) async-start(f32[8,1,4096]{2,1,0:T(1,128)} %reshape.152), calls=%async_computation | async-start | bytes 262144 | tf_op jit(solution)/shard_map/all_to_all | solution.py:199
  21.5 35.7 %copy-start = (f32[8,64,64]{2,1,0:T(8,128)}, f32[8,64,64]{2,1,0:T(8,128)S(1)}, u32[]{:S(2)}) copy-start(f32[8,64,64]{2,1,0:T(8,128)S(1)} %reshape.153) | copy-start | bytes 393220
  22.6 18.5 %all-to-all-start.1 = ((f32[16,1,4096]{2,1,0:T(1,128)}), f32[16,1,4096]{2,1,0:T(1,128)S(1)}, u32[]{:S(2)}, u32[]{:S(2)}) async-start(f32[16,1,4096]{2,1,0:T(1,128)} %reshape.154), calls=%async_computation.1 | async-start | bytes 524288 | tf_op jit(solution)/shard_map/all_to_all | solution.py:182
  32.3 27.0 %copy-start.2 = (f32[64]{0:T(128)S(1)}, f32[64]{0:T(128)}, u32[]{:S(2)}) copy-start(f32[64]{0:T(128)} %param.5) | copy-start | bytes 772
  43.9 11.4 %all-to-all-start.2 = ((f32[8,1,12288]{2,1,0:T(1,128)}), f32[8,1,12288]{2,1,0:T(1,128)S(1)}, u32[]{:S(2)}, u32[]{:S(2)}) async-start(f32[8,1,12288]{2,1,0:T(1,128)} %reshape.156), calls=%async_computation.2 | async-start | bytes 786432 | tf_op jit(solution)/shard_map/all_to_all | solution.py:182
  47.3 72.3 %all-gather.3.cloned.1.call-start = ((), (), s32[]{:S(2)}) async-start(), calls=%async_computation.3 | async-start | bytes 4456448 | tf_op jit(solution)/shard_map/all_gather | solution.py:206
  47.7 71.3 %copy-start.1 = (s32[64,1]{1,0:T(8,128)}, s32[64,1]{1,0:T(8,128)S(1)}, u32[]{:S(2)}) copy-start(s32[64,1]{1,0:T(8,128)S(1)} %reshape.150.own_ids_ref) | copy-start | bytes 772
Sparse Core Ops, SparseCore 0:
  57.4 52.9 all-gather.2

commit v7 on v6

--- a/solution.py
+++ b/solution.py
@@ -11,6 +11,7 @@
 BLK = 16
 
 HIGHEST = lax.Precision.HIGHEST
+PHASES = 4
 
 
 def kernel_block(left, left_norms, right, right_norms, signal):
@@ -26,40 +27,52 @@
 
 def lower_inverse_kernel(a_ref, o_ref, s_ref, x_ref):
     half = a_ref.shape[0] // 2
-    lanes = lax.broadcasted_iota(jnp.int32, (half, half), 1)
-    rows = lax.broadcasted_iota(jnp.int32, (half, 1), 0)
     lane_row = lax.broadcasted_iota(jnp.int32, (1, half), 1)
-    eye = jnp.where(lax.broadcasted_iota(jnp.int32, (half, half), 0) == lanes, 1.0, 0.0)
+    eye = jnp.where(
+        lax.broadcasted_iota(jnp.int32, (half, half), 0)
+        == lax.broadcasted_iota(jnp.int32, (half, half), 1),
+        1.0,
+        0.0,
+    )
 
     def pick(values, index):
         return jnp.sum(jnp.where(lane_row == index, values, 0.0), axis=1, keepdims=True)
 
-    def step(j, carry):
-        k = 2 * j
-        s = s_ref[...]
-        x = x_ref[...]
-        row0 = s_ref[pl.ds(k, 1), :]
-        row1 = s_ref[pl.ds(k + 1, 1), :]
-        col0 = jnp.sum(jnp.where(lanes == k, s, 0.0), axis=1, keepdims=True)
-        col1 = jnp.sum(jnp.where(lanes == k + 1, s, 0.0), axis=1, keepdims=True)
-        root0 = jnp.sqrt(pick(row0, k))
-        cross = pick(row1, k) / root0
-        root1 = jnp.sqrt(pick(row1, k + 1) - cross * cross)
-        col0 = jnp.where(rows >= k, col0 / root0, 0.0)
-        row0 = jnp.where(lane_row >= k, row0 / root0, 0.0)
-        col1 = jnp.where(rows >= k + 1, (col1 - col0 * cross) / root1, 0.0)
-        row1 = jnp.where(lane_row >= k + 1, (row1 - cross * row0) / root1, 0.0)
-        s_ref[...] = s - col0 * row0 - col1 * row1
-        x0 = x_ref[pl.ds(k, 1), :] / root0
-        x1 = (x_ref[pl.ds(k + 1, 1), :] - cross * x0) / root1
-        rest = x - jnp.where(rows > k, col0, 0.0) * x0 - jnp.where(rows > k + 1, col1, 0.0) * x1
-        x_ref[...] = jnp.where(rows == k, x0, jnp.where(rows == k + 1, x1, rest))
-        return carry
+    def make_step(top):
+        count = half - top
+        lanes = lax.broadcasted_iota(jnp.int32, (count, half), 1)
+        rows = lax.broadcasted_iota(jnp.int32, (count, 1), 0) + top
+
+        def step(j, carry):
+            k = 2 * j
+            s = s_ref[top:, :]
+            x = x_ref[top:, :]
+            row0 = s_ref[pl.ds(k, 1), :]
+            row1 = s_ref[pl.ds(k + 1, 1), :]
+            col0 = jnp.sum(jnp.where(lanes == k, s, 0.0), axis=1, keepdims=True)
+            col1 = jnp.sum(jnp.where(lanes == k + 1, s, 0.0), axis=1, keepdims=True)
+            root0 = jnp.sqrt(pick(row0, k))
+            cross = pick(row1, k) / root0
+            root1 = jnp.sqrt(pick(row1, k + 1) - cross * cross)
+            col0 = jnp.where(rows >= k, col0 / root0, 0.0)
+            row0 = jnp.where(lane_row >= k, row0 / root0, 0.0)
+            col1 = jnp.where(rows >= k + 1, (col1 - col0 * cross) / root1, 0.0)
+            row1 = jnp.where(lane_row >= k + 1, (row1 - cross * row0) / root1, 0.0)
+            s_ref[top:, :] = s - col0 * row0 - col1 * row1
+            x0 = x_ref[pl.ds(k, 1), :] / root0
+            x1 = (x_ref[pl.ds(k + 1, 1), :] - cross * x0) / root1
+            rest = x - jnp.where(rows > k, col0, 0.0) * x0 - jnp.where(rows > k + 1, col1, 0.0) * x1
+            x_ref[top:, :] = jnp.where(rows == k, x0, jnp.where(rows == k + 1, x1, rest))
+            return carry
+
+        return step
 
     def base(block):
         s_ref[...] = block
         x_ref[...] = eye.astype(jnp.float32)
-        lax.fori_loop(0, half // 2, step, 0)
+        span = half // PHASES
+        for phase in range(PHASES):
+            lax.fori_loop(phase * span // 2, (phase + 1) * span // 2, make_step(phase * span), 0)
         return x_ref[...]
 
     first = base(a_ref[:half, :half])
@@ -107,7 +120,7 @@
 
 
 def panel_kernel(
-    consts_ref, pts_ref, pnorm_ref, pid_ref, scales_ref, cs_ref, cn_ref, own_cs_ref, own_cn_ref,
+    consts_ref, pts_ref, pid_ref, scales_ref, cs_ref, cn_ref, own_cs_ref, own_cn_ref,
     own_ids_ref, finv_ref, sinv_ref, mid_ref, own_panels_ref, sel_ref, out_ref,
 ):
     signal = consts_ref[0]
@@ -116,7 +129,7 @@
     scaled = (pts_ref[...].reshape(tile, FEAT) * scales_ref[...]).T
     high, middle, low = split_three(scaled)
     packed = jnp.concatenate([high, middle, high, low, high, middle], axis=0)
-    pnorm = pnorm_ref[...]
+    pnorm = jnp.sum(scaled * scaled, axis=0, keepdims=True)
     pid = pid_ref[...]
     cross = jnp.dot(cs_ref[...], packed, preferred_element_type=jnp.float32)
     values = signal * jnp.exp(-0.5 * (cn_ref[...] + pnorm - 2.0 * cross))
@@ -148,7 +161,7 @@
         out_ref[:, chunk, :] = result[:, chunk * lanes : (chunk + 1) * lanes]
 
 
-def panel_stage(consts, gathered, pnorm, pid, scales, cs, cn, own_cs, own_cn, own_ids, finv, sinv, mid, own_panels, sel):
+def panel_stage(consts, gathered, pid, scales, cs, cn, own_cs, own_cn, own_ids, finv, sinv, mid, own_panels, sel):
     col_count, row_count, block_rows, _ = gathered.shape
     tile = col_count * block_rows
     grid_rows = tile * row_count
@@ -164,12 +177,11 @@
             pl.BlockSpec(memory_space=pltpu.SMEM),
             pl.BlockSpec((col_count, 1, block_rows, FEAT), lambda i: (0, i, 0, 0)),
             pl.BlockSpec((1, tile), lambda i: (0, i)),
-            pl.BlockSpec((1, tile), lambda i: (0, i)),
         ]
         + [whole(a) for a in (scales, cs, cn, own_cs, own_cn, own_ids, finv, sinv, mid, own_panels, sel)],
         out_specs=pl.BlockSpec((out_rows, tile // 128, 128), lambda i: (0, i, 0)),
         out_shape=jax.ShapeDtypeStruct((out_rows, grid_rows // 128, 128), jnp.float32),
-    )(consts, gathered, pnorm, pid, scales, cs, cn, own_cs, own_cn, own_ids, finv, sinv, mid, own_panels, sel)
+    )(consts, gathered, pid, scales, cs, cn, own_cs, own_cn, own_ids, finv, sinv, mid, own_panels, sel)
 
 
 def ridge_where(row_ids, col_ids, jitter):
@@ -208,8 +220,6 @@
 
     center_scaled = centers * feature_scales
     center_norms = jnp.sum(center_scaled * center_scaled, axis=1)
-    gathered_scaled = gathered * feature_scales
-    point_norms = jnp.sum(gathered_scaled * gathered_scaled, axis=3).transpose(1, 0, 2).reshape(1, grid_rows)
 
     point_ids = (
         lax.broadcasted_iota(jnp.int32, (grid_rows // block_rows, block_rows), 0) * row_count
@@ -261,7 +271,6 @@
     finished = panel_stage(
         consts,
         gathered,
-        point_norms,
         point_ids,
         feature_scales.reshape(1, FEAT),
         pack_left(center_scaled[: 2 * PANEL]),

time: 162 us -> 151 us (0.932)
  Pallas kernels: 77.5 us -> 70.8 us
  other arithmetic: 11.9 us -> 8.61 us
    pallas_call x2, Pallas kernels: 47.1 us -> 40.3 us  [lower_inverse(): pl.pallas_call(lower_inverse_kernel, out_shape=jax.ShapeDtypeStruct((size...]
    reduce_sum x1 -> x0, other arithmetic: 3.34 us -> none  [on_device(): jnp.sum(gathered_scaled * gathered_scaled, axis=3).transpose(1, 0, 2)]
  transfers between devices with their start and end apart: 4 -> 4, of which waited for: 3 -> 3; matrix products, arithmetic and copies ran while one was open for 10% -> 10% of each run, Pallas kernels for 29% -> 27%
where the time goes in v7:
time: 151 us; the launch traced here: 150 us
  Pallas kernels  70.8 us (47%)
  waiting for transfers between devices  20.1 us (13%)
  starting transfers between devices  19.5 us (13%)
  between operations  15 us (10%)
  local copies, waits for them, and re-layouts  11.5 us (8%)
  other arithmetic  8.61 us (6%)
  matrix products  4.7 us (3%)
    pallas_call x2, Pallas kernels, lower_inverse(): pl.pallas_call(lower_inverse_kernel, out_shape=jax.ShapeDtypeStruct((size...  40.3 us
    pallas_call x1, Pallas kernels, panel_stage(): pl.pallas_call(panel_kernel, grid=(row_count,), in_specs=[pl.BlockSpec(me...  30.5 us
    all_to_all x2, waiting for transfers between devices, gather_by_all_to_all(): return lax.all_to_all(copies, axis_name, 0, 0, tiled=True)  14.9 us
    all_to_all x2, starting transfers between devices, gather_by_all_to_all(): return lax.all_to_all(copies, axis_name, 0, 0, tiled=True)  13.1 us
    all_to_all x1, starting transfers between devices, on_device(): moved = lax.all_to_all(blocks, 'row', 0, 0, tiled=True)  6.2 us
    all_to_all x1, waiting for transfers between devices, on_device(): moved = lax.all_to_all(blocks, 'row', 0, 0, tiled=True)  5.18 us
    unnamed x12, local copies, waits for them, and re-layouts  4.67 us
  transfers between devices with their start and end apart: 4, of which 3 were waited for; matrix products, arithmetic and copies ran while one was open for 10% of the time, Pallas kernels for 27%

profile of v7, /device:TPU:1, one launch (start us, length us, event | category | flops | bytes accessed | tf_op | source)
XLA Modules:
  0.0 150.2 jit_solution(17443642596418768312)
XLA Ops:
  6.5 1.0 copy.47
  7.6 0.8 reshape.147
  8.4 6.2 %all-to-all-start = ((f32[8,1,4096]{2,1,0:T(1,128)}), f32[8,1,4096]{2,1,0:T(1,128)S(1)}, u32[]{:S(2)}, u32[]{:S(2)}) async-start(f32[8,1,4096]{2,1,0:T(1,128)} %reshape.147), calls=%async_computation | async-start | bytes 262144 | tf_op jit(solution)/shard_map/all_to_all | solution.py:211
  14.6 0.1 iota_add_fusion.1
  14.7 5.2 %all-to-all-done = f32[8,1,4096]{2,1,0:T(1,128)S(1)} async-done(((f32[8,1,4096]{2,1,0:T(1,128)}), f32[8,1,4096]{2,1,0:T(1,128)S(1)}, u32[]{:S(2)}, u32[]{:S(2)}) %all-to-all-start) | async-done | bytes 131104 | tf_op jit(solution)/shard_map/all_to_all | solution.py:211
  19.9 0.5 broadcast.126
  20.4 0.9 reduce.2
  21.3 0.1 reshape.148
  21.4 0.0 copy-start
  21.5 1.0 reshape.149
  22.5 9.6 %all-to-all-start.1 = ((f32[16,1,4096]{2,1,0:T(1,128)}), f32[16,1,4096]{2,1,0:T(1,128)S(1)}, u32[]{:S(2)}, u32[]{:S(2)}) async-start(f32[16,1,4096]{2,1,0:T(1,128)} %reshape.149), calls=%async_computation.1 | async-start | bytes 524288 | tf_op jit(solution)/shard_map/all_to_all | solution.py:194
  32.2 0.1 reshape.125
  32.2 0.0 copy-start.2
  32.3 8.8 %all-to-all-done.1 = f32[16,1,4096]{2,1,0:T(1,128)S(1)} async-done(((f32[16,1,4096]{2,1,0:T(1,128)}), f32[16,1,4096]{2,1,0:T(1,128)S(1)}, u32[]{:S(2)}, u32[]{:S(2)}) %all-to-all-start.1) | async-done | bytes 262176 | tf_op jit(solution)/shard_map/all_to_all | solution.py:194
  41.0 1.2 reduce.3
  42.3 0.2 reshape.150
  42.5 0.1 broadcast_in_dim.66
  42.6 1.2 reshape.151
  43.8 3.5 %all-to-all-start.2 = ((f32[8,1,12288]{2,1,0:T(1,128)}), f32[8,1,12288]{2,1,0:T(1,128)S(1)}, u32[]{:S(2)}, u32[]{:S(2)}) async-start(f32[8,1,12288]{2,1,0:T(1,128)} %reshape.151), calls=%async_computation.2 | async-start | bytes 786432 | tf_op jit(solution)/shard_map/all_to_all | solution.py:194
  47.3 0.2 all-gather.3.cloned.1.call-start
  47.5 0.1 reshape.145.own_ids_ref
  47.6 0.0 copy-start.1
  49.0 0.1 fusion.22
  49.1 0.1 iota_add_fusion
  49.2 6.1 %all-to-all-done.2 = f32[8,1,12288]{2,1,0:T(1,128)S(1)} async-done(((f32[8,1,12288]{2,1,0:T(1,128)}), f32[8,1,12288]{2,1,0:T(1,128)S(1)}, u32[]{:S(2)}, u32[]{:S(2)}) %all-to-all-start.2) | async-done | bytes 393248 | tf_op jit(solution)/shard_map/all_to_all | solution.py:194
  55.3 1.5 %reduce.4 = f32[8,12288]{1,0:T(8,128)S(1)} reduce(f32[8,1,12288]{2,1,0:T(1,128)S(1)} %all-to-all-done.2, f32[]{:T(128)} %broadcast.126), dimensions={1}, to_apply=%all_to_all.11.reduce_sub_computation | reduce | bytes 786436 | tf_op jit(solution)/shard_map/all_to_all | solution.py:194
  56.8 0.3 reshape.152
  57.1 0.0 copy-done
  57.1 0.1 copy.48
  57.2 0.0 all-gather.3.cloned.1.call-update
  57.2 0.7 pad_maximum_fusion.2.consts_ref
  57.9 0.7 add.125.pid_ref
  58.6 0.7 select_convert_fusion.sel_ref
  59.3 0.0 copy-done.2
  59.3 0.3 multiply_reduce_fusion
  59.6 0.8 gather_fusion.1
  60.3 0.6 gather_fusion
  61.0 0.4 fusion.20
  61.3 0.1 copy.54
  61.5 0.1 copy.55
  61.6 0.8 fusion.13.a_ref
  62.5 20.2 %shard_map.46.finv_ref = f32[256,256]{1,0:T(8,128)} custom-call(f32[256,256]{1,0:T(8,128)} %fusion.13.a_ref), custom_call_target="tpu_custom_call" | custom-call | tf_op jit(solution)/shard_map/pallas_call | solution.py:98
  82.6 0.1 fusion.21
  82.7 1.0 fusion.4
  83.7 1.7 %convolution_convert_fusion = bf16[320,256]{1,0:T(8,128)(2,1)S(1)} fusion(f32[256,256]{1,0:T(8,128)} %shard_map.46.finv_ref, f32[320,512]{0,1:T(8,128)S(1)} %fusion.4), kind=kOutput, calls=%fused_computation.10 | convolution fusion | flops 251740160 | bytes 819200 | tf_op jit(solution)/shard_map/dot_general | solution.py:251
  85.5 0.7 slice.78.mid_ref
  86.1 0.1 copy.52
  86.2 0.9 copy.59.cn_ref
  87.1 0.2 convolution_subtract_fusion
  87.4 0.1 copy.58
  87.5 0.7 fusion.7.a_ref
  88.2 20.1 %shard_map.47.sinv_ref = f32[256,256]{1,0:T(8,128)} custom-call(f32[256,256]{1,0:T(8,128)} %fusion.7.a_ref), custom_call_target="tpu_custom_call" | custom-call | tf_op jit(solution)/shard_map/pallas_call | solution.py:98
  108.4 0.7 concatenate.19.own_cs_ref
  109.1 0.1 fusion.6
  109.2 1.1 concatenate.18.cs_ref
  110.2 1.3 convolution_convert_fusion.1
  111.6 0.6 pad_maximum_fusion.own_panels_ref
  112.2 0.0 copy-done.1
  112.2 0.6 and_select_fusion.own_cn_ref
  112.9 0.0 all-gather.3.cloned.1.call-done
  112.9 30.5 %shard_map.48 = f32[96,64,128]{2,1,0:T(8,128)} custom-call(f32[2]{0:T(128)} %pad_maximum_fusion.2.consts_ref, f32[16,8,64,64]{3,2,1,0:T(8,128)} %bitcast.37, s32[1,8192]{1,0:T(1,128)} %add.125.pid_ref, f32[1,64]{1,0:T(1,128)} %bitcast.43, bf16[512,384]{1,0:T(8,128)(2,1)} %concatenate.18.cs_ref, f32[512,1]{1,0:T(8,128)} %copy.59.cn_ref, ...), custom_call_target="tpu_custom_call" | custom-call | tf_op jit(solution)/shard_map/pallas_call | solution.py:173
  (18 shorter events, 0.2 us)
Async XLA Ops:
  8.4 11.5 %all-to-all-start = ((f32[8,1,4096]{2,1,0:T(1,128)}), f32[8,1,4096]{2,1,0:T(1,128)S(1)}, u32[]{:S(2)}, u32[]{:S(2)}) async-start(f32[8,1,4096]{2,1,0:T(1,128)} %reshape.147), calls=%async_computation | async-start | bytes 262144 | tf_op jit(solution)/shard_map/all_to_all | solution.py:211
  21.4 35.7 %copy-start = (f32[8,64,64]{2,1,0:T(8,128)}, f32[8,64,64]{2,1,0:T(8,128)S(1)}, u32[]{:S(2)}) copy-start(f32[8,64,64]{2,1,0:T(8,128)S(1)} %reshape.148) | copy-start | bytes 393220
  22.5 18.5 %all-to-all-start.1 = ((f32[16,1,4096]{2,1,0:T(1,128)}), f32[16,1,4096]{2,1,0:T(1,128)S(1)}, u32[]{:S(2)}, u32[]{:S(2)}) async-start(f32[16,1,4096]{2,1,0:T(1,128)} %reshape.149), calls=%async_computation.1 | async-start | bytes 524288 | tf_op jit(solution)/shard_map/all_to_all | solution.py:194
  32.2 27.0 %copy-start.2 = (f32[64]{0:T(128)S(1)}, f32[64]{0:T(128)}, u32[]{:S(2)}) copy-start(f32[64]{0:T(128)} %param.5) | copy-start | bytes 772
  43.8 11.4 %all-to-all-start.2 = ((f32[8,1,12288]{2,1,0:T(1,128)}), f32[8,1,12288]{2,1,0:T(1,128)S(1)}, u32[]{:S(2)}, u32[]{:S(2)}) async-start(f32[8,1,12288]{2,1,0:T(1,128)} %reshape.151), calls=%async_computation.2 | async-start | bytes 786432 | tf_op jit(solution)/shard_map/all_to_all | solution.py:194
  47.3 65.6 %all-gather.3.cloned.1.call-start = ((), (), s32[]{:S(2)}) async-start(), calls=%async_computation.3 | async-start | bytes 4456448 | tf_op jit(solution)/shard_map/all_gather | solution.py:218
  47.6 64.6 %copy-start.1 = (s32[64,1]{1,0:T(8,128)}, s32[64,1]{1,0:T(8,128)S(1)}, u32[]{:S(2)}) copy-start(s32[64,1]{1,0:T(8,128)S(1)} %reshape.145.own_ids_ref) | copy-start | bytes 772
Sparse Core Ops, SparseCore 0:
  57.3 53.0 all-gather.2

commit v8 on v7

--- a/solution.py
+++ b/solution.py
@@ -215,7 +215,7 @@
     centers = center_grid.transpose(1, 0, 2, 3).reshape(SLAB, FEAT)
 
     moved, centers = lax.optimization_barrier((moved, centers))
-    gathered = lax.all_gather(moved, "col", axis=0, tiled=False)
+    gathered = gather_by_all_to_all(moved, "col")
     grid_rows = gathered.shape[0] * gathered.shape[1] * block_rows
 
     center_scaled = centers * feature_scales

time: 151 us -> 159 us (1.053)
  between operations: 15 us -> 1.61 us
  local copies, waits for them, and re-layouts: 11.5 us -> 22.6 us
  other arithmetic: 8.61 us -> 16.1 us
  starting transfers between devices: 19.5 us -> 24.6 us
  waiting for transfers between devices: 20.1 us -> 18.3 us
    unnamed x12 -> x13, local copies, waits for them, and re-layouts: 4.67 us -> 12.1 us
    all_to_all x2 -> x3, other arithmetic: 2.77 us -> 10.2 us  [gather_by_all_to_all(): return lax.all_to_all(copies, axis_name, 0, 0, tiled=True)]
    all_to_all x2 -> x3, starting transfers between devices: 13.1 us -> 18.4 us  [gather_by_all_to_all(): return lax.all_to_all(copies, axis_name, 0, 0, tiled=True)]
    broadcast_in_dim x3 -> x4, local copies, waits for them, and re-layouts: 0.12 us -> 2.59 us  [gather_by_all_to_all(): copies = jnp.broadcast_to(piece[None], (count,) + piece.shape)]
    all_to_all x2 -> x3, waiting for transfers between devices: 14.9 us -> 13.5 us  [gather_by_all_to_all(): return lax.all_to_all(copies, axis_name, 0, 0, tiled=True)]
  transfers between devices with their start and end apart: 4 -> 4, of which waited for: 3 -> 3; matrix products, arithmetic and copies ran while one was open for 10% -> 7% of each run, Pallas kernels for 27% -> 13%
where the time goes in v8:
time: 159 us; the launch traced here: 158 us
  Pallas kernels  70.8 us (45%)
  starting transfers between devices  24.6 us (15%)
  local copies, waits for them, and re-layouts  22.6 us (14%)
  waiting for transfers between devices  18.3 us (12%)
  other arithmetic  16.1 us (10%)
  matrix products  3.74 us (2%)
  between operations  1.61 us (1%)
    pallas_call x2, Pallas kernels, lower_inverse(): pl.pallas_call(lower_inverse_kernel, out_shape=jax.ShapeDtypeStruct((size...  40.3 us
    pallas_call x1, Pallas kernels, panel_stage(): pl.pallas_call(panel_kernel, grid=(row_count,), in_specs=[pl.BlockSpec(me...  30.5 us
    all_to_all x3, starting transfers between devices, gather_by_all_to_all(): return lax.all_to_all(copies, axis_name, 0, 0, tiled=True)  18.4 us
    all_to_all x3, waiting for transfers between devices, gather_by_all_to_all(): return lax.all_to_all(copies, axis_name, 0, 0, tiled=True)  13.5 us
    unnamed x13, local copies, waits for them, and re-layouts  12.1 us
    all_to_all x3, other arithmetic, gather_by_all_to_all(): return lax.all_to_all(copies, axis_name, 0, 0, tiled=True)  10.2 us
    all_to_all x1, starting transfers between devices, on_device(): moved = lax.all_to_all(blocks, 'row', 0, 0, tiled=True)  6.2 us
    all_to_all x1, waiting for transfers between devices, on_device(): moved = lax.all_to_all(blocks, 'row', 0, 0, tiled=True)  4.84 us
  transfers between devices with their start and end apart: 4, of which 3 were waited for; matrix products, arithmetic and copies ran while one was open for 7% of the time, Pallas kernels for 13%

profile of v8, /device:TPU:1, one launch (start us, length us, event | category | flops | bytes accessed | tf_op | source)
XLA Modules:
  0.0 157.8 jit_solution(8912780995282797547)
XLA Ops:
  0.0 1.0 copy.65
  1.0 0.8 reshape.147
  1.9 6.2 %all-to-all-start = ((f32[8,1,4096]{2,1,0:T(1,128)}), f32[8,1,4096]{2,1,0:T(1,128)S(1)}, u32[]{:S(2)}, u32[]{:S(2)}) async-start(f32[8,1,4096]{2,1,0:T(1,128)} %reshape.147), calls=%async_computation | async-start | bytes 262144 | tf_op jit(solution)/shard_map/all_to_all | solution.py:211
  8.1 0.1 iota_add_fusion.1
  8.2 0.1 reshape.126
  8.3 0.1 reshape.145.own_ids_ref
  8.4 0.0 copy-start.1
  8.4 0.1 fusion.22
  8.5 4.8 %all-to-all-done = f32[8,1,4096]{2,1,0:T(1,128)S(1)} async-done(((f32[8,1,4096]{2,1,0:T(1,128)}), f32[8,1,4096]{2,1,0:T(1,128)S(1)}, u32[]{:S(2)}, u32[]{:S(2)}) %all-to-all-start) | async-done | bytes 131104 | tf_op jit(solution)/shard_map/all_to_all | solution.py:211
  13.3 0.6 broadcast.127
  13.9 1.0 reduce.2
  14.9 0.1 reshape.148
  15.1 1.0 reshape.149
  16.1 9.6 %all-to-all-start.1 = ((f32[16,1,4096]{2,1,0:T(1,128)}), f32[16,1,4096]{2,1,0:T(1,128)S(1)}, u32[]{:S(2)}, u32[]{:S(2)}) async-start(f32[16,1,4096]{2,1,0:T(1,128)} %reshape.149), calls=%async_computation.1 | async-start | bytes 524288 | tf_op jit(solution)/shard_map/all_to_all | solution.py:194
  27.0 0.1 iota_add_fusion
  27.1 7.5 %all-to-all-done.1 = f32[16,1,4096]{2,1,0:T(1,128)S(1)} async-done(((f32[16,1,4096]{2,1,0:T(1,128)}), f32[16,1,4096]{2,1,0:T(1,128)S(1)}, u32[]{:S(2)}, u32[]{:S(2)}) %all-to-all-start.1) | async-done | bytes 262176 | tf_op jit(solution)/shard_map/all_to_all | solution.py:194
  34.6 1.3 reduce.3
  35.9 0.2 reshape.150
  36.2 0.0 copy-start.2
  36.2 0.1 broadcast_in_dim.72
  36.3 1.2 reshape.151
  37.5 3.5 %all-to-all-start.2 = ((f32[8,1,12288]{2,1,0:T(1,128)}), f32[8,1,12288]{2,1,0:T(1,128)S(1)}, u32[]{:S(2)}, u32[]{:S(2)}) async-start(f32[8,1,12288]{2,1,0:T(1,128)} %reshape.151), calls=%async_computation.2 | async-start | bytes 786432 | tf_op jit(solution)/shard_map/all_to_all | solution.py:194
  41.0 0.6 pad_maximum_fusion.2.consts_ref
  41.6 0.7 add.125.pid_ref
  42.3 0.7 select_convert_fusion.sel_ref
  43.0 6.0 %all-to-all-done.2 = f32[8,1,12288]{2,1,0:T(1,128)S(1)} async-done(((f32[8,1,12288]{2,1,0:T(1,128)}), f32[8,1,12288]{2,1,0:T(1,128)S(1)}, u32[]{:S(2)}, u32[]{:S(2)}) %all-to-all-start.2) | async-done | bytes 393248 | tf_op jit(solution)/shard_map/all_to_all | solution.py:194
  48.9 1.6 %reduce.4 = f32[8,12288]{1,0:T(8,128)S(1)} reduce(f32[8,1,12288]{2,1,0:T(1,128)S(1)} %all-to-all-done.2, f32[]{:T(128)} %broadcast.127), dimensions={1}, to_apply=%all_to_all.14.reduce_sub_computation | reduce | bytes 786436 | tf_op jit(solution)/shard_map/all_to_all | solution.py:194
  50.6 0.3 reshape.152
  50.9 0.1 copy.48
  50.9 0.0 copy-done.2
  50.9 0.3 multiply_reduce_fusion
  51.3 0.8 gather_fusion.1
  52.0 0.6 gather_fusion
  52.7 0.4 fusion.20
  53.0 0.1 copy.54
  53.2 0.1 copy.55
  53.3 0.8 fusion.13.a_ref
  54.2 20.1 %shard_map.46.finv_ref = f32[256,256]{1,0:T(8,128)} custom-call(f32[256,256]{1,0:T(8,128)} %fusion.13.a_ref), custom_call_target="tpu_custom_call" | custom-call | tf_op jit(solution)/shard_map/pallas_call | solution.py:98
  74.3 2.5 %broadcast_in_dim.73 = f32[16,8,64,64]{3,2,1,0:T(8,128)} broadcast(f32[8,64,64]{2,1,0:T(8,128)S(1)} %reshape.148), dimensions={1,2,3} | broadcast | bytes 2228224 | tf_op jit(solution)/shard_map/broadcast_in_dim | solution.py:193
  76.8 5.5 %reshape.153 = f32[16,1,32768]{2,1,0:T(1,128)} reshape(f32[16,8,64,64]{3,2,1,0:T(8,128)} %broadcast_in_dim.73) | data formatting | bytes 4194304
  82.3 0.0 copy-start
  82.3 5.4 %all-to-all-start.3 = ((f32[16,1,32768]{2,1,0:T(1,128)}), f32[16,1,32768]{2,1,0:T(1,128)}, u32[]{:S(2)}, u32[]{:S(2)}) async-start(f32[16,1,32768]{2,1,0:T(1,128)} %reshape.153), calls=%async_computation.3 | async-start | bytes 4194304 | tf_op jit(solution)/shard_map/all_to_all | solution.py:194
  87.7 0.1 fusion.21
  87.7 1.0 fusion.4
  88.7 0.0 copy-done
  88.7 0.8 convolution_convert_fusion
  89.5 0.7 slice.78.mid_ref
  90.2 0.1 copy.52
  90.3 0.9 copy.59.cn_ref
  91.2 0.2 convolution_subtract_fusion
  91.5 0.1 copy.58
  91.6 0.8 fusion.7.a_ref
  92.4 20.1 %shard_map.47.sinv_ref = f32[256,256]{1,0:T(8,128)} custom-call(f32[256,256]{1,0:T(8,128)} %fusion.7.a_ref), custom_call_target="tpu_custom_call" | custom-call | tf_op jit(solution)/shard_map/pallas_call | solution.py:98
  112.5 0.7 concatenate.19.own_cs_ref
  113.2 0.1 fusion.6
  113.3 1.1 concatenate.18.cs_ref
  114.4 1.3 convolution_convert_fusion.1
  115.7 0.6 pad_maximum_fusion.own_panels_ref
  116.4 0.0 copy-done.1
  116.4 0.6 and_select_fusion.own_cn_ref
  117.0 0.0 all-to-all-done.3
  117.0 7.3 %reduce.5 = f32[16,32768]{1,0:T(8,128)S(1)} reduce(f32[16,1,32768]{2,1,0:T(1,128)} %all-to-all-done.3, f32[]{:T(128)} %broadcast.127), dimensions={1}, to_apply=%all_to_all.15.reduce_sub_computation | reduce | bytes 4194308 | tf_op jit(solution)/shard_map/all_to_all | solution.py:194
  124.3 3.0 %reshape.154.pts_ref = f32[16,8,64,64]{3,2,1,0:T(8,128)} reshape(f32[16,32768]{1,0:T(8,128)S(1)} %reduce.5) | data formatting | bytes 4194304
  127.3 30.5 %shard_map.48 = f32[96,64,128]{2,1,0:T(8,128)} custom-call(f32[2]{0:T(128)} %pad_maximum_fusion.2.consts_ref, f32[16,8,64,64]{3,2,1,0:T(8,128)} %reshape.154.pts_ref, s32[1,8192]{1,0:T(1,128)} %add.125.pid_ref, f32[1,64]{1,0:T(1,128)} %bitcast.41, bf16[512,384]{1,0:T(8,128)(2,1)} %concatenate.18.cs_ref, f32[512,1]{1,0:T(8,128)} %copy.59.cn_ref, ...), custom_call_target="tpu_custom_call" | custom-call | tf_op jit(solution)/shard_map/pallas_call | solution.py:173
  (18 shorter events, 0.2 us)
Async XLA Ops:
  1.9 11.5 %all-to-all-start = ((f32[8,1,4096]{2,1,0:T(1,128)}), f32[8,1,4096]{2,1,0:T(1,128)S(1)}, u32[]{:S(2)}, u32[]{:S(2)}) async-start(f32[8,1,4096]{2,1,0:T(1,128)} %reshape.147), calls=%async_computation | async-start | bytes 262144 | tf_op jit(solution)/shard_map/all_to_all | solution.py:211
  8.4 108.0 %copy-start.1 = (s32[64,1]{1,0:T(8,128)}, s32[64,1]{1,0:T(8,128)S(1)}, u32[]{:S(2)}) copy-start(s32[64,1]{1,0:T(8,128)S(1)} %reshape.145.own_ids_ref) | copy-start | bytes 772
  16.1 18.5 %all-to-all-start.1 = ((f32[16,1,4096]{2,1,0:T(1,128)}), f32[16,1,4096]{2,1,0:T(1,128)S(1)}, u32[]{:S(2)}, u32[]{:S(2)}) async-start(f32[16,1,4096]{2,1,0:T(1,128)} %reshape.149), calls=%async_computation.1 | async-start | bytes 524288 | tf_op jit(solution)/shard_map/all_to_all | solution.py:194
  36.2 14.8 %copy-start.2 = (f32[64]{0:T(128)S(1)}, f32[64]{0:T(128)}, u32[]{:S(2)}) copy-start(f32[64]{0:T(128)} %param.5) | copy-start | bytes 772
  37.5 11.4 %all-to-all-start.2 = ((f32[8,1,12288]{2,1,0:T(1,128)}), f32[8,1,12288]{2,1,0:T(1,128)S(1)}, u32[]{:S(2)}, u32[]{:S(2)}) async-start(f32[8,1,12288]{2,1,0:T(1,128)} %reshape.151), calls=%async_computation.2 | async-start | bytes 786432 | tf_op jit(solution)/shard_map/all_to_all | solution.py:194
  82.3 6.5 %copy-start = (f32[256,256]{1,0:T(8,128)S(1)}, f32[256,256]{1,0:T(8,128)}, u32[]{:S(2)}) copy-start(f32[256,256]{1,0:T(8,128)} %shard_map.46.finv_ref) | copy-start | bytes 786436
  82.3 34.7 %all-to-all-start.3 = ((f32[16,1,32768]{2,1,0:T(1,128)}), f32[16,1,32768]{2,1,0:T(1,128)}, u32[]{:S(2)}, u32[]{:S(2)}) async-start(f32[16,1,32768]{2,1,0:T(1,128)} %reshape.153), calls=%async_computation.3 | async-start | bytes 4194304 | tf_op jit(solution)/shard_map/all_to_all | solution.py:194

commit v9 on v7

--- a/solution.py
+++ b/solution.py
@@ -25,8 +25,8 @@
     )
 
 
-def lower_inverse_kernel(a_ref, o_ref, s_ref, x_ref):
-    half = a_ref.shape[0] // 2
+def lower_inverse_body(block, s_ref, x_ref):
+    half = block.shape[0] // 2
     lane_row = lax.broadcasted_iota(jnp.int32, (1, half), 1)
     eye = jnp.where(
         lax.broadcasted_iota(jnp.int32, (half, half), 0)
@@ -75,9 +75,9 @@
             lax.fori_loop(phase * span // 2, (phase + 1) * span // 2, make_step(phase * span), 0)
         return x_ref[...]
 
-    first = base(a_ref[:half, :half])
-    lower = _nt(a_ref[half:, :half], first)
-    schur = a_ref[half:, half:] - _nt(lower, lower)
+    first = base(block[:half, :half])
+    lower = _nt(block[half:, :half], first)
+    schur = block[half:, half:] - _nt(lower, lower)
     second = base((schur + schur.T) * 0.5)
     below = -jnp.dot(
         second,
@@ -85,21 +85,42 @@
         precision=HIGHEST,
         preferred_element_type=jnp.float32,
     )
-    o_ref[:half, :half] = first
-    o_ref[:half, half:] = jnp.zeros((half, half), jnp.float32)
-    o_ref[half:, :half] = below
-    o_ref[half:, half:] = second
-
-
-def lower_inverse(block):
-    size = block.shape[0]
-    half = size // 2
-    block = (block + block.T) * 0.5
+    top = jnp.concatenate([first, jnp.zeros((half, half), jnp.float32)], axis=1)
+    return jnp.concatenate([top, jnp.concatenate([below, second], axis=1)], axis=0)
+
+
+def factor_kernel(lead_ref, used_ref, finv_ref, sinv_ref, mid_ref, own_ref, s_ref, x_ref):
+    first_inverse = lower_inverse_body(lead_ref[...], s_ref, x_ref)
+    finv_ref[...] = first_inverse
+    used = used_ref[...]
+    panel = first_inverse.shape[0]
+    center_first = _nt(used[:, :panel], first_inverse).astype(jnp.bfloat16)
+    first_mid = center_first[:panel]
+    mid_ref[...] = first_mid
+    center_second = used[:, panel:] - lax.dot_general(
+        center_first, first_mid, (((1,), (1,)), ((), ())), preferred_element_type=jnp.float32
+    )
+    block = center_second[:panel]
+    second_inverse = lower_inverse_body((block + block.T) * 0.5, s_ref, x_ref)
+    sinv_ref[...] = second_inverse
+    second_own = _nt(center_second[panel:], second_inverse).astype(jnp.bfloat16)
+    own_ref[...] = jnp.concatenate([center_first[panel:], second_own], axis=1)
+
+
+def factor_centers(lead, used):
+    panel = lead.shape[0]
+    half = panel // 2
+    own_rows = used.shape[0] - panel
     return pl.pallas_call(
-        lower_inverse_kernel,
-        out_shape=jax.ShapeDtypeStruct((size, size), jnp.float32),
+        factor_kernel,
+        out_shape=(
+            jax.ShapeDtypeStruct((panel, panel), jnp.float32),
+            jax.ShapeDtypeStruct((panel, panel), jnp.float32),
+            jax.ShapeDtypeStruct((panel, panel), jnp.bfloat16),
+            jax.ShapeDtypeStruct((own_rows, 2 * panel), jnp.bfloat16),
+        ),
         scratch_shapes=[pltpu.VMEM((half, half), jnp.float32), pltpu.VMEM((half, half), jnp.float32)],
-    )(block)
+    )((lead + lead.T) * 0.5, used)
 
 
 def split_three(values):
@@ -241,25 +262,13 @@
     k11 = kernel_block(
         center_scaled[:PANEL], center_norms[:PANEL], center_scaled[:PANEL], center_norms[:PANEL], signal
     ) + ridge_where(lead_ids, lead_ids, jitter)
-    first_inverse = lower_inverse(k11)
     used_ids = jnp.concatenate([jnp.arange(PANEL, 2 * PANEL, dtype=jnp.int32), own_ids])
     used_scaled = jnp.concatenate([center_scaled[PANEL : 2 * PANEL], own_scaled])
     used_norms = jnp.concatenate([center_norms[PANEL : 2 * PANEL], own_norms])
     used_kernel = kernel_block(
         used_scaled, used_norms, center_scaled[: 2 * PANEL], center_norms[: 2 * PANEL], signal
     ) + ridge_where(used_ids, jnp.arange(2 * PANEL, dtype=jnp.int32), jitter)
-    center_first = jnp.dot(
-        used_kernel[:, :PANEL], first_inverse.T, precision=HIGHEST, preferred_element_type=jnp.float32
-    ).astype(jnp.bfloat16)
-    first_mid = center_first[:PANEL]
-    center_second = used_kernel[:, PANEL:] - jnp.dot(
-        center_first, first_mid.T, preferred_element_type=jnp.float32
-    )
-    second_inverse = lower_inverse(center_second[:PANEL])
-    second_own = jnp.dot(
-        center_second[PANEL:], second_inverse.T, precision=HIGHEST, preferred_element_type=jnp.float32
-    ).astype(jnp.bfloat16)
-    own_panels = jnp.concatenate([center_first[PANEL:], second_own], axis=1)
+    first_inverse, second_inverse, first_mid, own_panels = factor_centers(k11, used_kernel)
 
     select = jnp.where(
         lax.broadcasted_iota(jnp.int32, (BLK, PANEL), 1)

time: 151 us -> 147 us (0.974)
  blocking collectives: 0 us -> 29.6 us
  starting transfers between devices: 19.5 us -> 3.67 us
  waiting for transfers between devices: 20.1 us -> 8.6 us
  matrix products: 4.7 us -> 2.1 us
  local copies, waits for them, and re-layouts: 11.5 us -> 9.39 us
    all_to_all x0 -> x2, blocking collectives: none -> 29.6 us  [the longest x1 18.3 us: gather_by_all_to_all(): return lax.all_to_all(copies, axis_name, 0, 0, tiled=True)]
    all_to_all x2 -> x1, starting transfers between devices: 13.1 us -> 3.45 us  [gather_by_all_to_all(): return lax.all_to_all(copies, axis_name, 0, 0, tiled=True)]
    all_to_all x2 -> x1, waiting for transfers between devices: 14.9 us -> 7.72 us  [gather_by_all_to_all(): return lax.all_to_all(copies, axis_name, 0, 0, tiled=True)]
    all_to_all x1 -> x0, starting transfers between devices: 6.2 us -> none  [on_device(): moved = lax.all_to_all(blocks, 'row', 0, 0, tiled=True)]
    all_to_all x1 -> x0, waiting for transfers between devices: 5.18 us -> none  [on_device(): moved = lax.all_to_all(blocks, 'row', 0, 0, tiled=True)]
    dot_general x3 -> x0, matrix products: 3.33 us -> none  [the longest x1 1.74 us: on_device(): jnp.dot(used_kernel[:, :PANEL], first_inverse.T, precision=HIGHEST, prefe...]
    pallas_call x2 -> x1, Pallas kernels: 40.3 us -> 40.1 us  [factor_centers(): pl.pallas_call(factor_kernel, out_shape=(jax.ShapeDtypeStruct((panel, pan...]
  transfers between devices with their start and end apart: 4 -> 2, of which waited for: 3 -> 2; matrix products, arithmetic and copies ran while one was open for 10% -> 7% of each run, Pallas kernels for 27% -> 27%
where the time goes in v9:
time: 147 us; the launch traced here: 146 us
  Pallas kernels  70.6 us (48%)
  blocking collectives  29.6 us (20%)
  between operations  15 us (10%)
  local copies, waits for them, and re-layouts  9.39 us (6%)
  waiting for transfers between devices  8.6 us (6%)
  other arithmetic  7.22 us (5%)
  starting transfers between devices  3.67 us (2%)
  matrix products  2.1 us (1%)
    pallas_call x1, Pallas kernels, factor_centers(): pl.pallas_call(factor_kernel, out_shape=(jax.ShapeDtypeStruct((panel, pan...  40.1 us
    pallas_call x1, Pallas kernels, panel_stage(): pl.pallas_call(panel_kernel, grid=(row_count,), in_specs=[pl.BlockSpec(me...  30.5 us
    all_to_all x1, blocking collectives, gather_by_all_to_all(): return lax.all_to_all(copies, axis_name, 0, 0, tiled=True)  18.3 us
    all_to_all x1, blocking collectives, on_device(): moved = lax.all_to_all(blocks, 'row', 0, 0, tiled=True)  11.3 us
    all_to_all x1, waiting for transfers between devices, gather_by_all_to_all(): return lax.all_to_all(copies, axis_name, 0, 0, tiled=True)  7.72 us
    all_to_all x1, starting transfers between devices, gather_by_all_to_all(): return lax.all_to_all(copies, axis_name, 0, 0, tiled=True)  3.45 us
    unnamed x12, local copies, waits for them, and re-layouts  3.3 us
  transfers between devices with their start and end apart: 2, of which 2 were waited for; matrix products, arithmetic and copies ran while one was open for 7% of the time, Pallas kernels for 27%

profile of v9, /device:TPU:1, one launch (start us, length us, event | category | flops | bytes accessed | tf_op | source)
XLA Modules:
  0.0 146.1 jit_solution(9442492734901074679)
XLA Ops:
  6.5 1.0 copy.38
  7.6 0.2 reshape.147
  7.8 11.3 %all_to_all.15 = f32[8,1,4096]{2,1,0:T(1,128)S(1)} all-to-all(f32[8,1,4096]{2,1,0:T(1,128)S(1)} %reshape.147), channel_id=1, replica_groups=mesh['row'=8,'col'=16] {'row'}, dimensions={0} | all-to-all | bytes 262144 | tf_op jit(solution)/shard_map/all_to_all | solution.py:232
  19.0 0.5 broadcast.120
  19.6 0.9 reduce.2
  20.5 0.1 reshape.148
  20.6 0.0 copy-start
  20.7 0.3 reshape.149
  21.0 18.3 %all_to_all.16 = f32[16,1,4096]{2,1,0:T(1,128)S(1)} all-to-all(f32[16,1,4096]{2,1,0:T(1,128)S(1)} %reshape.149), channel_id=1, replica_groups=mesh['row'=8,'col'=16] {'col'}, dimensions={0} | all-to-all | bytes 524288 | tf_op jit(solution)/shard_map/all_to_all | solution.py:215
  39.3 0.0 copy-start.2
  39.3 1.3 reduce.3
  40.6 0.2 reshape.150
  40.8 0.1 broadcast_in_dim.66
  40.9 1.2 reshape.151
  42.1 3.5 %all-to-all-start.2 = ((f32[8,1,12288]{2,1,0:T(1,128)}), f32[8,1,12288]{2,1,0:T(1,128)S(1)}, u32[]{:S(2)}, u32[]{:S(2)}) async-start(f32[8,1,12288]{2,1,0:T(1,128)} %reshape.151), calls=%async_computation.2 | async-start | bytes 786432 | tf_op jit(solution)/shard_map/all_to_all | solution.py:215
  45.6 0.2 all-gather.3.cloned.1.call-start
  45.9 7.7 %all-to-all-done.2 = f32[8,1,12288]{2,1,0:T(1,128)S(1)} async-done(((f32[8,1,12288]{2,1,0:T(1,128)}), f32[8,1,12288]{2,1,0:T(1,128)S(1)}, u32[]{:S(2)}, u32[]{:S(2)}) %all-to-all-start.2) | async-done | bytes 393248 | tf_op jit(solution)/shard_map/all_to_all | solution.py:215
  53.6 1.6 %reduce.4 = f32[8,12288]{1,0:T(8,128)S(1)} reduce(f32[8,1,12288]{2,1,0:T(1,128)S(1)} %all-to-all-done.2, f32[]{:T(128)} %broadcast.120), dimensions={1}, to_apply=%all_to_all.11.reduce_sub_computation | reduce | bytes 786436 | tf_op jit(solution)/shard_map/all_to_all | solution.py:215
  55.1 0.3 reshape.152
  55.5 0.1 copy.39
  55.5 0.0 copy-done
  55.5 0.0 all-gather.3.cloned.1.call-update
  55.6 0.1 iota_add_fusion.1
  55.6 0.1 reshape.125
  55.7 0.1 reshape.145.own_ids_ref
  55.8 0.0 copy-start.1
  57.1 0.1 iota_add_fusion
  57.2 0.7 add.122.pid_ref
  57.9 0.6 pad_maximum_fusion.1.consts_ref
  58.6 0.1 fusion.19
  58.7 0.7 select_convert_fusion.sel_ref
  59.3 0.0 copy-done.2
  59.3 0.3 multiply_reduce_fusion
  59.6 0.8 gather_fusion.1
  60.4 0.6 gather_fusion
  61.0 0.1 copy.43
  61.1 0.9 copy.47.cn_ref
  62.0 0.4 fusion.17
  62.4 0.1 copy.45
  62.5 0.1 copy.46
  62.7 0.1 fusion.18
  62.8 1.7 %fusion.4.used_ref = f32[320,512]{1,0:T(8,128)} fusion(f32[]{:T(128)} %bitcast.29, s32[320]{0:T(512)S(1)} %pad_add_fusion, f32[512]{0:T(512)S(1)} %slice.47, f32[320]{0:T(512)S(1)} %pad_maximum_fusion, f32[]{:T(128)} %bitcast.27, f32[1536,64]{1,0:T(8,128)S(1)} %get-tuple-element.22, f32[64,64]{1,0:T(8,128)S(1)} %get-tuple-element.20, f32[256,64]{1,0:T(8,128)S(1)} %slice.51), kind=kOutput, calls=%fused_computation.7 | convolution fusion | flops 127160320 | bytes 1087496 | tf_op jit(solution)/shard_map/dot_general | solution.py:18
  64.5 0.8 fusion.11.lead_ref
  65.3 40.1 %shard_map.46 = (f32[256,256]{1,0:T(8,128)}, f32[256,256]{1,0:T(8,128)}, bf16[256,256]{1,0:T(8,128)(2,1)}, bf16[64,512]{1,0:T(8,128)(2,1)}) custom-call(f32[256,256]{1,0:T(8,128)} %fusion.11.lead_ref, f32[320,512]{1,0:T(8,128)} %fusion.4.used_ref), custom_call_target="tpu_custom_call" | custom-call | tf_op jit(solution)/shard_map/pallas_call | solution.py:114
  105.5 0.7 concatenate.16.own_cs_ref
  106.2 0.1 fusion.5
  106.3 1.1 concatenate.15.cs_ref
  107.3 0.0 copy-done.1
  107.3 0.6 and_select_fusion.own_cn_ref
  107.9 0.9 all-gather.3.cloned.1.call-done
  108.8 30.5 %shard_map.47 = f32[96,64,128]{2,1,0:T(8,128)} custom-call(f32[2]{0:T(128)} %pad_maximum_fusion.1.consts_ref, f32[16,8,64,64]{3,2,1,0:T(8,128)} %bitcast.30, s32[1,8192]{1,0:T(1,128)} %add.122.pid_ref, f32[1,64]{1,0:T(1,128)} %bitcast.36, bf16[512,384]{1,0:T(8,128)(2,1)} %concatenate.15.cs_ref, f32[512,1]{1,0:T(8,128)} %copy.47.cn_ref, ...), custom_call_target="tpu_custom_call" | custom-call | tf_op jit(solution)/shard_map/pallas_call | solution.py:194
  (16 shorter events, 0.1 us)
Async XLA Ops:
  20.6 34.9 %copy-start = (f32[8,64,64]{2,1,0:T(8,128)}, f32[8,64,64]{2,1,0:T(8,128)S(1)}, u32[]{:S(2)}) copy-start(f32[8,64,64]{2,1,0:T(8,128)S(1)} %reshape.148) | copy-start | bytes 393220
  39.3 20.0 %copy-start.2 = (f32[64]{0:T(128)S(1)}, f32[64]{0:T(128)}, u32[]{:S(2)}) copy-start(f32[64]{0:T(128)} %param.5) | copy-start | bytes 772
  42.1 11.4 %all-to-all-start.2 = ((f32[8,1,12288]{2,1,0:T(1,128)}), f32[8,1,12288]{2,1,0:T(1,128)S(1)}, u32[]{:S(2)}, u32[]{:S(2)}) async-start(f32[8,1,12288]{2,1,0:T(1,128)} %reshape.151), calls=%async_computation.2 | async-start | bytes 786432 | tf_op jit(solution)/shard_map/all_to_all | solution.py:215
  45.6 63.2 %all-gather.3.cloned.1.call-start = ((), (), s32[]{:S(2)}) async-start(), calls=%async_computation.3 | async-start | bytes 4456448 | tf_op jit(solution)/shard_map/all_gather | solution.py:239
  55.8 51.5 %copy-start.1 = (s32[64,1]{1,0:T(8,128)}, s32[64,1]{1,0:T(8,128)S(1)}, u32[]{:S(2)}) copy-start(s32[64,1]{1,0:T(8,128)S(1)} %reshape.145.own_ids_ref) | copy-start | bytes 772
Sparse Core Ops, SparseCore 0:
  55.7 53.0 all-gather.2

commit v10 on v9

--- a/solution.py
+++ b/solution.py
@@ -11,7 +11,7 @@
 BLK = 16
 
 HIGHEST = lax.Precision.HIGHEST
-PHASES = 4
+PHASES = 8
 
 
 def kernel_block(left, left_norms, right, right_norms, signal):
@@ -154,8 +154,10 @@
     pid = pid_ref[...]
     cross = jnp.dot(cs_ref[...], packed, preferred_element_type=jnp.float32)
     values = signal * jnp.exp(-0.5 * (cn_ref[...] + pnorm - 2.0 * cross))
-    lead = lax.broadcasted_iota(jnp.int32, values.shape, 0)
-    values = values + jnp.where(lead == pid, jitter, jnp.float32(0.0))
+    head = values[:, :128] + jnp.where(
+        lax.broadcasted_iota(jnp.int32, (values.shape[0], 128), 0) == pid[:, :128], jitter, jnp.float32(0.0)
+    )
+    values = jnp.concatenate([head, values[:, 128:]], axis=1)
     first = jnp.dot(
         finv_ref[...], values[:PANEL], precision=HIGHEST, preferred_element_type=jnp.float32
     ).astype(jnp.bfloat16)
@@ -165,7 +167,8 @@
     ).astype(jnp.bfloat16)
     own_cross = jnp.dot(own_cs_ref[...], packed, preferred_element_type=jnp.float32)
     own = signal * jnp.exp(-0.5 * (own_cn_ref[...] + pnorm - 2.0 * own_cross))
-    own = own + jnp.where(own_ids_ref[...] == pid, jitter, jnp.float32(0.0))
+    own_head = own[:, :256] + jnp.where(own_ids_ref[...] == pid[:, :256], jitter, jnp.float32(0.0))
+    own = jnp.concatenate([own_head, own[:, 256:]], axis=1)
     both = jnp.concatenate([first, second], axis=0)
     trailing = own - jnp.dot(own_panels_ref[...], both, preferred_element_type=jnp.float32)
     sel = sel_ref[...]

time: 147 us -> 146 us (level)
  Pallas kernels: 70.6 us -> 68.7 us
where the time goes in v10:
time: 146 us; the launch traced here: 145 us
  Pallas kernels  68.7 us (47%)
  blocking collectives  29.6 us (20%)
  between operations  15 us (10%)
  waiting for transfers between devices  9.57 us (7%)
  local copies, waits for them, and re-layouts  9.39 us (6%)
  other arithmetic  7.22 us (5%)
  starting transfers between devices  3.67 us (3%)
  matrix products  2.1 us (1%)
    pallas_call x1, Pallas kernels, factor_centers(): pl.pallas_call(factor_kernel, out_shape=(jax.ShapeDtypeStruct((panel, pan...  39.1 us
    pallas_call x1, Pallas kernels, panel_stage(): pl.pallas_call(panel_kernel, grid=(row_count,), in_specs=[pl.BlockSpec(me...  29.7 us
    all_to_all x1, blocking collectives, gather_by_all_to_all(): return lax.all_to_all(copies, axis_name, 0, 0, tiled=True)  18.3 us
    all_to_all x1, blocking collectives, on_device(): moved = lax.all_to_all(blocks, 'row', 0, 0, tiled=True)  11.3 us
    all_to_all x1, waiting for transfers between devices, gather_by_all_to_all(): return lax.all_to_all(copies, axis_name, 0, 0, tiled=True)  7.72 us
    all_to_all x1, starting transfers between devices, gather_by_all_to_all(): return lax.all_to_all(copies, axis_name, 0, 0, tiled=True)  3.45 us
    unnamed x12, local copies, waits for them, and re-layouts  3.3 us
  transfers between devices with their start and end apart: 2, of which 2 were waited for; matrix products, arithmetic and copies ran while one was open for 7% of the time, Pallas kernels for 27%

profile of v10, /device:TPU:1, one launch (start us, length us, event | category | flops | bytes accessed | tf_op | source)
XLA Modules:
  0.0 145.2 jit_solution(3279913643635164542)
XLA Ops:
  6.5 1.0 copy.38
  7.6 0.2 reshape.147
  7.8 11.3 %all_to_all.15 = f32[8,1,4096]{2,1,0:T(1,128)S(1)} all-to-all(f32[8,1,4096]{2,1,0:T(1,128)S(1)} %reshape.147), channel_id=1, replica_groups=mesh['row'=8,'col'=16] {'row'}, dimensions={0} | all-to-all | bytes 262144 | tf_op jit(solution)/shard_map/all_to_all | solution.py:235
  19.0 0.5 broadcast.120
  19.6 0.9 reduce.2
  20.5 0.1 reshape.148
  20.6 0.0 copy-start
  20.7 0.3 reshape.149
  21.0 18.3 %all_to_all.16 = f32[16,1,4096]{2,1,0:T(1,128)S(1)} all-to-all(f32[16,1,4096]{2,1,0:T(1,128)S(1)} %reshape.149), channel_id=1, replica_groups=mesh['row'=8,'col'=16] {'col'}, dimensions={0} | all-to-all | bytes 524288 | tf_op jit(solution)/shard_map/all_to_all | solution.py:218
  39.3 0.0 copy-start.2
  39.3 1.3 reduce.3
  40.6 0.2 reshape.150
  40.8 0.1 broadcast_in_dim.66
  40.9 1.2 reshape.151
  42.1 3.5 %all-to-all-start.2 = ((f32[8,1,12288]{2,1,0:T(1,128)}), f32[8,1,12288]{2,1,0:T(1,128)S(1)}, u32[]{:S(2)}, u32[]{:S(2)}) async-start(f32[8,1,12288]{2,1,0:T(1,128)} %reshape.151), calls=%async_computation.2 | async-start | bytes 786432 | tf_op jit(solution)/shard_map/all_to_all | solution.py:218
  45.6 0.2 all-gather.3.cloned.1.call-start
  45.9 7.7 %all-to-all-done.2 = f32[8,1,12288]{2,1,0:T(1,128)S(1)} async-done(((f32[8,1,12288]{2,1,0:T(1,128)}), f32[8,1,12288]{2,1,0:T(1,128)S(1)}, u32[]{:S(2)}, u32[]{:S(2)}) %all-to-all-start.2) | async-done | bytes 393248 | tf_op jit(solution)/shard_map/all_to_all | solution.py:218
  53.6 1.6 %reduce.4 = f32[8,12288]{1,0:T(8,128)S(1)} reduce(f32[8,1,12288]{2,1,0:T(1,128)S(1)} %all-to-all-done.2, f32[]{:T(128)} %broadcast.120), dimensions={1}, to_apply=%all_to_all.11.reduce_sub_computation | reduce | bytes 786436 | tf_op jit(solution)/shard_map/all_to_all | solution.py:218
  55.1 0.3 reshape.152
  55.5 0.1 copy.39
  55.5 0.0 copy-done
  55.5 0.0 all-gather.3.cloned.1.call-update
  55.6 0.1 iota_add_fusion.1
  55.6 0.1 reshape.125
  55.7 0.1 reshape.145.own_ids_ref
  55.8 0.0 copy-start.1
  57.1 0.1 iota_add_fusion
  57.2 0.7 add.122.pid_ref
  57.9 0.6 pad_maximum_fusion.1.consts_ref
  58.6 0.1 fusion.19
  58.7 0.7 select_convert_fusion.sel_ref
  59.3 0.0 copy-done.2
  59.3 0.3 multiply_reduce_fusion
  59.6 0.8 gather_fusion.1
  60.4 0.6 gather_fusion
  61.0 0.1 copy.43
  61.1 0.9 copy.47.cn_ref
  62.0 0.4 fusion.17
  62.4 0.1 copy.45
  62.5 0.1 copy.46
  62.7 0.1 fusion.18
  62.8 1.7 %fusion.4.used_ref = f32[320,512]{1,0:T(8,128)} fusion(f32[]{:T(128)} %bitcast.29, s32[320]{0:T(512)S(1)} %pad_add_fusion, f32[512]{0:T(512)S(1)} %slice.47, f32[320]{0:T(512)S(1)} %pad_maximum_fusion, f32[]{:T(128)} %bitcast.27, f32[1536,64]{1,0:T(8,128)S(1)} %get-tuple-element.22, f32[64,64]{1,0:T(8,128)S(1)} %get-tuple-element.20, f32[256,64]{1,0:T(8,128)S(1)} %slice.51), kind=kOutput, calls=%fused_computation.7 | convolution fusion | flops 127160320 | bytes 1087496 | tf_op jit(solution)/shard_map/dot_general | solution.py:18
  64.5 0.8 fusion.11.lead_ref
  65.3 39.1 %shard_map.46 = (f32[256,256]{1,0:T(8,128)}, f32[256,256]{1,0:T(8,128)}, bf16[256,256]{1,0:T(8,128)(2,1)}, bf16[64,512]{1,0:T(8,128)(2,1)}) custom-call(f32[256,256]{1,0:T(8,128)} %fusion.11.lead_ref, f32[320,512]{1,0:T(8,128)} %fusion.4.used_ref), custom_call_target="tpu_custom_call" | custom-call | tf_op jit(solution)/shard_map/pallas_call | solution.py:114
  104.4 0.7 concatenate.16.own_cs_ref
  105.1 0.1 fusion.5
  105.2 1.1 concatenate.15.cs_ref
  106.2 0.0 copy-done.1
  106.2 0.6 and_select_fusion.own_cn_ref
  106.9 1.8 %all-gather.3.cloned.1.call-done = f32[128,64,64]{2,1,0:T(8,128)} async-done(((f32[8,64,64]{2,1,0:T(8,128)}), f32[128,64,64]{2,1,0:T(8,128)}) %all-gather.3.cloned.1.call-update) | async-done | bytes 2097168 | tf_op jit(solution)/shard_map/all_gather | solution.py:242
  108.7 29.7 %shard_map.47 = f32[96,64,128]{2,1,0:T(8,128)} custom-call(f32[2]{0:T(128)} %pad_maximum_fusion.1.consts_ref, f32[16,8,64,64]{3,2,1,0:T(8,128)} %bitcast.30, s32[1,8192]{1,0:T(1,128)} %add.122.pid_ref, f32[1,64]{1,0:T(1,128)} %bitcast.36, bf16[512,384]{1,0:T(8,128)(2,1)} %concatenate.15.cs_ref, f32[512,1]{1,0:T(8,128)} %copy.47.cn_ref, ...), custom_call_target="tpu_custom_call" | custom-call | tf_op jit(solution)/shard_map/pallas_call | solution.py:197
  (16 shorter events, 0.1 us)
Async XLA Ops:
  20.6 34.9 %copy-start = (f32[8,64,64]{2,1,0:T(8,128)}, f32[8,64,64]{2,1,0:T(8,128)S(1)}, u32[]{:S(2)}) copy-start(f32[8,64,64]{2,1,0:T(8,128)S(1)} %reshape.148) | copy-start | bytes 393220
  39.3 20.0 %copy-start.2 = (f32[64]{0:T(128)S(1)}, f32[64]{0:T(128)}, u32[]{:S(2)}) copy-start(f32[64]{0:T(128)} %param.5) | copy-start | bytes 772
  42.1 11.4 %all-to-all-start.2 = ((f32[8,1,12288]{2,1,0:T(1,128)}), f32[8,1,12288]{2,1,0:T(1,128)S(1)}, u32[]{:S(2)}, u32[]{:S(2)}) async-start(f32[8,1,12288]{2,1,0:T(1,128)} %reshape.151), calls=%async_computation.2 | async-start | bytes 786432 | tf_op jit(solution)/shard_map/all_to_all | solution.py:218
  45.6 63.1 %all-gather.3.cloned.1.call-start = ((), (), s32[]{:S(2)}) async-start(), calls=%async_computation.3 | async-start | bytes 4456448 | tf_op jit(solution)/shard_map/all_gather | solution.py:242
  55.8 50.4 %copy-start.1 = (s32[64,1]{1,0:T(8,128)}, s32[64,1]{1,0:T(8,128)S(1)}, u32[]{:S(2)}) copy-start(s32[64,1]{1,0:T(8,128)S(1)} %reshape.145.own_ids_ref) | copy-start | bytes 772
Sparse Core Ops, SparseCore 0:
  55.7 52.9 all-gather.2

commit v11 on v10

--- a/solution.py
+++ b/solution.py
@@ -147,7 +147,7 @@
     signal = consts_ref[0]
     jitter = consts_ref[1]
     tile = pts_ref.shape[0] * pts_ref.shape[2]
-    scaled = (pts_ref[...].reshape(tile, FEAT) * scales_ref[...]).T
+    scaled = pts_ref[...].reshape(tile, pts_ref.shape[3]).T[:FEAT] * scales_ref[...]
     high, middle, low = split_three(scaled)
     packed = jnp.concatenate([high, middle, high, low, high, middle], axis=0)
     pnorm = jnp.sum(scaled * scaled, axis=0, keepdims=True)
@@ -199,7 +199,7 @@
         grid=(row_count,),
         in_specs=[
             pl.BlockSpec(memory_space=pltpu.SMEM),
-            pl.BlockSpec((col_count, 1, block_rows, FEAT), lambda i: (0, i, 0, 0)),
+            pl.BlockSpec((col_count, 1, block_rows, gathered.shape[3]), lambda i: (0, i, 0, 0)),
             pl.BlockSpec((1, tile), lambda i: (0, i)),
         ]
         + [whole(a) for a in (scales, cs, cn, own_cs, own_cn, own_ids, finv, sinv, mid, own_panels, sel)],
@@ -239,7 +239,11 @@
     centers = center_grid.transpose(1, 0, 2, 3).reshape(SLAB, FEAT)
 
     moved, centers = lax.optimization_barrier((moved, centers))
-    gathered = lax.all_gather(moved, "col", axis=0, tiled=False)
+    padded = jnp.pad(moved, ((0, 0), (0, 0), (0, 128 - FEAT))).reshape(1, -1)
+    copies = jnp.broadcast_to(padded, (col_count, padded.shape[1]))
+    gathered = lax.all_to_all(copies, "col", 0, 0, tiled=True).reshape(
+        col_count, row_count, block_rows, 128
+    )
     grid_rows = gathered.shape[0] * gathered.shape[1] * block_rows
 
     center_scaled = centers * feature_scales
@@ -284,7 +288,7 @@
         consts,
         gathered,
         point_ids,
-        feature_scales.reshape(1, FEAT),
+        feature_scales.reshape(FEAT, 1),
         pack_left(center_scaled[: 2 * PANEL]),
         center_norms[: 2 * PANEL].reshape(-1, 1),
         pack_left(own_scaled),

time: 146 us -> 147 us (level)
  the two profiles are of different devices: /device:TPU:1 before, /device:TPU:97 now
where the time goes in v11:
time: 147 us; the launch traced here: 146 us
  Pallas kernels  68.8 us (47%)
  blocking collectives  25.2 us (17%)
  local copies, waits for them, and re-layouts  15.4 us (10%)
  waiting for transfers between devices  13.5 us (9%)
  starting transfers between devices  12.3 us (8%)
  other arithmetic  7.34 us (5%)
  matrix products  2.1 us (1%)
  between operations  1.55 us (1%)
    pallas_call x1, Pallas kernels, factor_centers(): pl.pallas_call(factor_kernel, out_shape=(jax.ShapeDtypeStruct((panel, pan...  39.1 us
    pallas_call x1, Pallas kernels, panel_stage(): pl.pallas_call(panel_kernel, grid=(row_count,), in_specs=[pl.BlockSpec(me...  29.7 us
    all_to_all x1, blocking collectives, gather_by_all_to_all(): return lax.all_to_all(copies, axis_name, 0, 0, tiled=True)  15.6 us
    all_to_all x1, blocking collectives, on_device(): moved = lax.all_to_all(blocks, 'row', 0, 0, tiled=True)  9.54 us
    all_to_all x1, starting transfers between devices, on_device(): lax.all_to_all(copies, 'col', 0, 0, tiled=True)  8.28 us
    all_to_all x1, waiting for transfers between devices, gather_by_all_to_all(): return lax.all_to_all(copies, axis_name, 0, 0, tiled=True)  7.75 us
    all_to_all x1, waiting for transfers between devices, on_device(): lax.all_to_all(copies, 'col', 0, 0, tiled=True)  5.73 us
    broadcast_in_dim x1, local copies, waits for them, and re-layouts, on_device(): copies = jnp.broadcast_to(padded, (col_count, padded.shape[1]))  5.2 us
  transfers between devices with their start and end apart: 2, of which 2 were waited for; matrix products, arithmetic and copies ran while one was open for 8% of the time, Pallas kernels for 27%

profile of v11, /device:TPU:97, one launch (start us, length us, event | category | flops | bytes accessed | tf_op | source)
XLA Modules:
  0.0 146.2 jit_solution(8989609588475833643)
XLA Ops:
  0.0 1.0 copy.41
  1.0 0.2 reshape.160
  1.2 9.5 %all_to_all.21 = f32[8,1,4096]{2,1,0:T(1,128)S(1)} all-to-all(f32[8,1,4096]{2,1,0:T(1,128)S(1)} %reshape.160), channel_id=1, replica_groups=mesh['row'=8,'col'=16] {'row'}, dimensions={0} | all-to-all | bytes 262144 | tf_op jit(solution)/shard_map/all_to_all | solution.py:235
  10.8 0.6 broadcast.125
  11.4 1.0 reduce.2
  12.4 0.1 reshape.161
  12.5 0.3 reshape.162
  12.9 15.6 %all_to_all.22 = f32[16,1,4096]{2,1,0:T(1,128)S(1)} all-to-all(f32[16,1,4096]{2,1,0:T(1,128)S(1)} %reshape.162), channel_id=1, replica_groups=mesh['row'=8,'col'=16] {'col'}, dimensions={0} | all-to-all | bytes 524288 | tf_op jit(solution)/shard_map/all_to_all | solution.py:218
  28.5 1.3 reduce.3
  29.8 0.2 reshape.163
  30.0 0.1 broadcast_in_dim.73
  30.1 1.2 reshape.164
  31.4 4.1 %all-to-all-start.2 = ((f32[8,1,12288]{2,1,0:T(1,128)}), f32[8,1,12288]{2,1,0:T(1,128)S(1)}, u32[]{:S(2)}, u32[]{:S(2)}) async-start(f32[8,1,12288]{2,1,0:T(1,128)} %reshape.164), calls=%async_computation.2 | async-start | bytes 786432 | tf_op jit(solution)/shard_map/all_to_all | solution.py:218
  35.4 7.7 %all-to-all-done.2 = f32[8,1,12288]{2,1,0:T(1,128)S(1)} async-done(((f32[8,1,12288]{2,1,0:T(1,128)}), f32[8,1,12288]{2,1,0:T(1,128)S(1)}, u32[]{:S(2)}, u32[]{:S(2)}) %all-to-all-start.2) | async-done | bytes 393248 | tf_op jit(solution)/shard_map/all_to_all | solution.py:218
  43.2 1.6 %reduce.4 = f32[8,12288]{1,0:T(8,128)S(1)} reduce(f32[8,1,12288]{2,1,0:T(1,128)S(1)} %all-to-all-done.2, f32[]{:T(128)} %broadcast.125), dimensions={1}, to_apply=%all_to_all.15.reduce_sub_computation | reduce | bytes 786436 | tf_op jit(solution)/shard_map/all_to_all | solution.py:218
  44.8 0.3 reshape.165
  45.1 0.1 copy.42
  45.2 5.2 %broadcast_in_dim.75 = f32[16,1,65536]{2,1,0:T(1,128)} broadcast(f32[65536]{0:T(1024)S(1)} %bitcast.33), dimensions={2} | broadcast | bytes 4456448 | tf_op jit(solution)/shard_map/broadcast_in_dim | solution.py:243
  50.4 0.0 copy-start.1
  50.4 8.3 %all-to-all-start.3 = ((f32[16,1,65536]{2,1,0:T(1,128)}), f32[16,1,65536]{2,1,0:T(1,128)}, u32[]{:S(2)}, u32[]{:S(2)}) async-start(f32[16,1,65536]{2,1,0:T(1,128)} %broadcast_in_dim.75), calls=%async_computation.3 | async-start | bytes 8388608 | tf_op jit(solution)/shard_map/all_to_all | solution.py:244
  58.7 0.1 iota_add_fusion.1
  58.8 0.1 reshape.158.own_ids_ref
  58.9 0.0 copy-start
  58.9 0.1 reshape.139
  60.3 0.1 iota_add_fusion
  60.4 0.7 add.124.pid_ref
  61.1 0.0 copy-done.1
  61.1 0.7 copy.50.scales_ref
  61.8 0.6 pad_maximum_fusion.1.consts_ref
  62.4 0.1 fusion.19
  62.5 0.7 select_convert_fusion.sel_ref
  63.2 0.3 multiply_reduce_fusion
  63.5 0.8 gather_fusion.1
  64.2 0.6 gather_fusion
  64.8 0.9 copy.51.cn_ref
  65.7 0.1 copy.46
  65.8 0.4 fusion.17
  66.2 0.1 copy.49
  66.3 0.1 copy.48
  66.5 0.1 fusion.18
  66.6 1.7 %fusion.4.used_ref = f32[320,512]{1,0:T(8,128)} fusion(f32[]{:T(128)} %bitcast.30, s32[320]{0:T(512)S(1)} %pad_add_fusion, f32[512]{0:T(512)S(1)} %slice.47, f32[320]{0:T(512)S(1)} %pad_maximum_fusion, f32[]{:T(128)} %bitcast.28, f32[1536,64]{1,0:T(8,128)S(1)} %get-tuple-element.22, f32[64,64]{1,0:T(8,128)S(1)} %get-tuple-element.20, f32[256,64]{1,0:T(8,128)S(1)} %slice.51), kind=kOutput, calls=%fused_computation.7 | convolution fusion | flops 127160320 | bytes 1087496 | tf_op jit(solution)/shard_map/dot_general | solution.py:18
  68.3 0.8 fusion.11.lead_ref
  69.1 39.1 %shard_map.46 = (f32[256,256]{1,0:T(8,128)}, f32[256,256]{1,0:T(8,128)}, bf16[256,256]{1,0:T(8,128)(2,1)}, bf16[64,512]{1,0:T(8,128)(2,1)}) custom-call(f32[256,256]{1,0:T(8,128)} %fusion.11.lead_ref, f32[320,512]{1,0:T(8,128)} %fusion.4.used_ref), custom_call_target="tpu_custom_call" | custom-call | tf_op jit(solution)/shard_map/pallas_call | solution.py:114
  108.2 0.1 fusion.5
  108.3 1.1 concatenate.15.cs_ref
  109.4 0.7 concatenate.16.own_cs_ref
  110.1 0.0 copy-done
  110.1 0.6 and_select_fusion.own_cn_ref
  110.7 5.7 %all-to-all-done.3 = f32[16,1,65536]{2,1,0:T(1,128)} async-done(((f32[16,1,65536]{2,1,0:T(1,128)}), f32[16,1,65536]{2,1,0:T(1,128)}, u32[]{:S(2)}, u32[]{:S(2)}) %all-to-all-start.3) | async-done | bytes 4194336 | tf_op jit(solution)/shard_map/all_to_all | solution.py:244
  116.5 29.7 %shard_map.47 = f32[96,64,128]{2,1,0:T(8,128)} custom-call(f32[2]{0:T(128)} %pad_maximum_fusion.1.consts_ref, f32[16,8,64,128]{3,2,1,0:T(8,128)} %bitcast.5.pts_ref, s32[1,8192]{1,0:T(1,128)} %add.124.pid_ref, f32[64,1]{1,0:T(8,128)} %copy.50.scales_ref, bf16[512,384]{1,0:T(8,128)(2,1)} %concatenate.15.cs_ref, f32[512,1]{1,0:T(8,128)} %copy.51.cn_ref, ...), custom_call_target="tpu_custom_call" | custom-call | tf_op jit(solution)/shard_map/pallas_call | solution.py:197
  (17 shorter events, 0.2 us)
Async XLA Ops:
  31.4 11.8 %all-to-all-start.2 = ((f32[8,1,12288]{2,1,0:T(1,128)}), f32[8,1,12288]{2,1,0:T(1,128)S(1)}, u32[]{:S(2)}, u32[]{:S(2)}) async-start(f32[8,1,12288]{2,1,0:T(1,128)} %reshape.164), calls=%async_computation.2 | async-start | bytes 786432 | tf_op jit(solution)/shard_map/all_to_all | solution.py:218
  50.4 10.7 %copy-start.1 = (f32[64]{0:T(128)S(1)}, f32[64]{0:T(128)}, u32[]{:S(2)}) copy-start(f32[64]{0:T(128)} %param.5) | copy-start | bytes 772
  50.4 66.0 %all-to-all-start.3 = ((f32[16,1,65536]{2,1,0:T(1,128)}), f32[16,1,65536]{2,1,0:T(1,128)}, u32[]{:S(2)}, u32[]{:S(2)}) async-start(f32[16,1,65536]{2,1,0:T(1,128)} %broadcast_in_dim.75), calls=%async_computation.3 | async-start | bytes 8388608 | tf_op jit(solution)/shard_map/all_to_all | solution.py:244
  58.9 51.2 %copy-start = (s32[64,1]{1,0:T(8,128)}, s32[64,1]{1,0:T(8,128)S(1)}, u32[]{:S(2)}) copy-start(s32[64,1]{1,0:T(8,128)S(1)} %reshape.158.own_ids_ref) | copy-start | bytes 772

commit v12 on v10

--- a/solution.py
+++ b/solution.py
@@ -146,8 +146,10 @@
 ):
     signal = consts_ref[0]
     jitter = consts_ref[1]
-    tile = pts_ref.shape[0] * pts_ref.shape[2]
-    scaled = (pts_ref[...].reshape(tile, FEAT) * scales_ref[...]).T
+    points = jnp.concatenate(
+        [pts_ref[:, part].reshape(-1, FEAT) for part in range(pts_ref.shape[1])], axis=0
+    )
+    scaled = (points * scales_ref[...]).T
     high, middle, low = split_three(scaled)
     packed = jnp.concatenate([high, middle, high, low, high, middle], axis=0)
     pnorm = jnp.sum(scaled * scaled, axis=0, keepdims=True)
@@ -187,8 +189,9 @@
 
 def panel_stage(consts, gathered, pid, scales, cs, cn, own_cs, own_cn, own_ids, finv, sinv, mid, own_panels, sel):
     col_count, row_count, block_rows, _ = gathered.shape
-    tile = col_count * block_rows
-    grid_rows = tile * row_count
+    parts = 2
+    tile = col_count * block_rows * parts
+    grid_rows = col_count * block_rows * row_count
     out_rows = 2 * BLK + own_cs.shape[0]
 
     def whole(array):
@@ -196,10 +199,10 @@
 
     return pl.pallas_call(
         panel_kernel,
-        grid=(row_count,),
+        grid=(row_count // parts,),
         in_specs=[
             pl.BlockSpec(memory_space=pltpu.SMEM),
-            pl.BlockSpec((col_count, 1, block_rows, FEAT), lambda i: (0, i, 0, 0)),
+            pl.BlockSpec((col_count, parts, block_rows, FEAT), lambda i: (0, i, 0, 0)),
             pl.BlockSpec((1, tile), lambda i: (0, i)),
         ]
         + [whole(a) for a in (scales, cs, cn, own_cs, own_cn, own_ids, finv, sinv, mid, own_panels, sel)],

time: 146 us -> 144 us (0.986)
  Pallas kernels: 68.7 us -> 67.1 us
    pallas_call x1, Pallas kernels: 29.7 us -> 27.9 us  [panel_stage(): pl.pallas_call(panel_kernel, grid=(row_count // parts,), in_specs=[pl.Blo...]
  transfers between devices with their start and end apart: 2 -> 2, of which waited for: 2 -> 2; matrix products, arithmetic and copies ran while one was open for 7% -> 8% of each run, Pallas kernels for 27% -> 27%
where the time goes in v12:
time: 144 us; the launch traced here: 143 us
  Pallas kernels  67.1 us (47%)
  blocking collectives  29.6 us (21%)
  between operations  15 us (10%)
  waiting for transfers between devices  9.62 us (7%)
  local copies, waits for them, and re-layouts  9.39 us (7%)
  other arithmetic  7.22 us (5%)
  starting transfers between devices  3.49 us (2%)
  matrix products  2.1 us (1%)
    pallas_call x1, Pallas kernels, factor_centers(): pl.pallas_call(factor_kernel, out_shape=(jax.ShapeDtypeStruct((panel, pan...  39.2 us
    pallas_call x1, Pallas kernels, panel_stage(): pl.pallas_call(panel_kernel, grid=(row_count // parts,), in_specs=[pl.Blo...  27.9 us
    all_to_all x1, blocking collectives, gather_by_all_to_all(): return lax.all_to_all(copies, axis_name, 0, 0, tiled=True)  18.3 us
    all_to_all x1, blocking collectives, on_device(): moved = lax.all_to_all(blocks, 'row', 0, 0, tiled=True)  11.3 us
    all_to_all x1, waiting for transfers between devices, gather_by_all_to_all(): return lax.all_to_all(copies, axis_name, 0, 0, tiled=True)  7.9 us
    all_to_all x1, starting transfers between devices, gather_by_all_to_all(): return lax.all_to_all(copies, axis_name, 0, 0, tiled=True)  3.45 us
    unnamed x12, local copies, waits for them, and re-layouts  3.3 us
  transfers between devices with their start and end apart: 2, of which 2 were waited for; matrix products, arithmetic and copies ran while one was open for 8% of the time, Pallas kernels for 27%

profile of v12, /device:TPU:1, one launch (start us, length us, event | category | flops | bytes accessed | tf_op | source)
XLA Modules:
  0.0 143.5 jit_solution(9624035333074545997)
XLA Ops:
  6.5 1.0 copy.38
  7.6 0.2 reshape.147
  7.8 11.3 %all_to_all.15 = f32[8,1,4096]{2,1,0:T(1,128)S(1)} all-to-all(f32[8,1,4096]{2,1,0:T(1,128)S(1)} %reshape.147), channel_id=1, replica_groups=mesh['row'=8,'col'=16] {'row'}, dimensions={0} | all-to-all | bytes 262144 | tf_op jit(solution)/shard_map/all_to_all | solution.py:238
  19.0 0.5 broadcast.120
  19.6 0.9 reduce.2
  20.5 0.1 reshape.148
  20.6 0.0 copy-start
  20.7 0.3 reshape.149
  21.0 18.3 %all_to_all.16 = f32[16,1,4096]{2,1,0:T(1,128)S(1)} all-to-all(f32[16,1,4096]{2,1,0:T(1,128)S(1)} %reshape.149), channel_id=1, replica_groups=mesh['row'=8,'col'=16] {'col'}, dimensions={0} | all-to-all | bytes 524288 | tf_op jit(solution)/shard_map/all_to_all | solution.py:221
  39.3 0.0 copy-start.2
  39.3 1.3 reduce.3
  40.6 0.2 reshape.150
  40.8 0.1 broadcast_in_dim.66
  40.9 1.2 reshape.151
  42.1 3.5 %all-to-all-start.2 = ((f32[8,1,12288]{2,1,0:T(1,128)}), f32[8,1,12288]{2,1,0:T(1,128)S(1)}, u32[]{:S(2)}, u32[]{:S(2)}) async-start(f32[8,1,12288]{2,1,0:T(1,128)} %reshape.151), calls=%async_computation.2 | async-start | bytes 786432 | tf_op jit(solution)/shard_map/all_to_all | solution.py:221
  45.6 0.0 all-gather.3.cloned.1.call-start
  45.7 7.9 %all-to-all-done.2 = f32[8,1,12288]{2,1,0:T(1,128)S(1)} async-done(((f32[8,1,12288]{2,1,0:T(1,128)}), f32[8,1,12288]{2,1,0:T(1,128)S(1)}, u32[]{:S(2)}, u32[]{:S(2)}) %all-to-all-start.2) | async-done | bytes 393248 | tf_op jit(solution)/shard_map/all_to_all | solution.py:221
  53.6 1.6 %reduce.4 = f32[8,12288]{1,0:T(8,128)S(1)} reduce(f32[8,1,12288]{2,1,0:T(1,128)S(1)} %all-to-all-done.2, f32[]{:T(128)} %broadcast.120), dimensions={1}, to_apply=%all_to_all.11.reduce_sub_computation | reduce | bytes 786436 | tf_op jit(solution)/shard_map/all_to_all | solution.py:221
  55.1 0.3 reshape.152
  55.5 0.1 copy.39
  55.5 0.0 copy-done
  55.5 0.0 all-gather.3.cloned.1.call-update
  55.6 0.1 iota_add_fusion.1
  55.6 0.1 reshape.125
  55.7 0.1 reshape.145.own_ids_ref
  55.8 0.0 copy-start.1
  57.1 0.1 iota_add_fusion
  57.2 0.7 add.122.pid_ref
  57.9 0.6 pad_maximum_fusion.1.consts_ref
  58.6 0.1 fusion.19
  58.7 0.7 select_convert_fusion.sel_ref
  59.3 0.0 copy-done.2
  59.3 0.3 multiply_reduce_fusion
  59.6 0.8 gather_fusion.1
  60.4 0.6 gather_fusion
  61.0 0.1 copy.43
  61.1 0.9 copy.47.cn_ref
  62.0 0.4 fusion.17
  62.4 0.1 copy.45
  62.5 0.1 copy.46
  62.7 0.1 fusion.18
  62.8 1.7 %fusion.4.used_ref = f32[320,512]{1,0:T(8,128)} fusion(f32[]{:T(128)} %bitcast.29, s32[320]{0:T(512)S(1)} %pad_add_fusion, f32[512]{0:T(512)S(1)} %slice.47, f32[320]{0:T(512)S(1)} %pad_maximum_fusion, f32[]{:T(128)} %bitcast.27, f32[1536,64]{1,0:T(8,128)S(1)} %get-tuple-element.22, f32[64,64]{1,0:T(8,128)S(1)} %get-tuple-element.20, f32[256,64]{1,0:T(8,128)S(1)} %slice.51), kind=kOutput, calls=%fused_computation.7 | convolution fusion | flops 127160320 | bytes 1087496 | tf_op jit(solution)/shard_map/dot_general | solution.py:18
  64.5 0.8 fusion.11.lead_ref
  65.3 39.2 %shard_map.46 = (f32[256,256]{1,0:T(8,128)}, f32[256,256]{1,0:T(8,128)}, bf16[256,256]{1,0:T(8,128)(2,1)}, bf16[64,512]{1,0:T(8,128)(2,1)}) custom-call(f32[256,256]{1,0:T(8,128)} %fusion.11.lead_ref, f32[320,512]{1,0:T(8,128)} %fusion.4.used_ref), custom_call_target="tpu_custom_call" | custom-call | tf_op jit(solution)/shard_map/pallas_call | solution.py:114
  104.6 0.7 concatenate.16.own_cs_ref
  105.3 0.1 fusion.5
  105.4 1.1 concatenate.15.cs_ref
  106.4 0.0 copy-done.1
  106.4 0.6 and_select_fusion.own_cn_ref
  107.0 1.7 %all-gather.3.cloned.1.call-done = f32[128,64,64]{2,1,0:T(8,128)} async-done(((f32[8,64,64]{2,1,0:T(8,128)}), f32[128,64,64]{2,1,0:T(8,128)}) %all-gather.3.cloned.1.call-update) | async-done | bytes 2097168 | tf_op jit(solution)/shard_map/all_gather | solution.py:245
  108.8 27.9 %shard_map.47 = f32[96,64,128]{2,1,0:T(8,128)} custom-call(f32[2]{0:T(128)} %pad_maximum_fusion.1.consts_ref, f32[16,8,64,64]{3,2,1,0:T(8,128)} %bitcast.30, s32[1,8192]{1,0:T(1,128)} %add.122.pid_ref, f32[1,64]{1,0:T(1,128)} %bitcast.36, bf16[512,384]{1,0:T(8,128)(2,1)} %concatenate.15.cs_ref, f32[512,1]{1,0:T(8,128)} %copy.47.cn_ref, ...), custom_call_target="tpu_custom_call" | custom-call | tf_op jit(solution)/shard_map/pallas_call | solution.py:200
  (16 shorter events, 0.1 us)
Async XLA Ops:
  20.6 34.9 %copy-start = (f32[8,64,64]{2,1,0:T(8,128)}, f32[8,64,64]{2,1,0:T(8,128)S(1)}, u32[]{:S(2)}) copy-start(f32[8,64,64]{2,1,0:T(8,128)S(1)} %reshape.148) | copy-start | bytes 393220
  39.3 20.0 %copy-start.2 = (f32[64]{0:T(128)S(1)}, f32[64]{0:T(128)}, u32[]{:S(2)}) copy-start(f32[64]{0:T(128)} %param.5) | copy-start | bytes 772
  42.1 11.4 %all-to-all-start.2 = ((f32[8,1,12288]{2,1,0:T(1,128)}), f32[8,1,12288]{2,1,0:T(1,128)S(1)}, u32[]{:S(2)}, u32[]{:S(2)}) async-start(f32[8,1,12288]{2,1,0:T(1,128)} %reshape.151), calls=%async_computation.2 | async-start | bytes 786432 | tf_op jit(solution)/shard_map/all_to_all | solution.py:221
  45.6 63.1 %all-gather.3.cloned.1.call-start = ((), (), s32[]{:S(2)}) async-start(), calls=%async_computation.3 | async-start | bytes 4456448 | tf_op jit(solution)/shard_map/all_gather | solution.py:245
  55.8 50.6 %copy-start.1 = (s32[64,1]{1,0:T(8,128)}, s32[64,1]{1,0:T(8,128)S(1)}, u32[]{:S(2)}) copy-start(s32[64,1]{1,0:T(8,128)S(1)} %reshape.145.own_ids_ref) | copy-start | bytes 772
Sparse Core Ops, SparseCore 0:
  55.7 53.0 all-gather.2

commit v13 on v12

--- a/solution.py
+++ b/solution.py
@@ -189,7 +189,7 @@
 
 def panel_stage(consts, gathered, pid, scales, cs, cn, own_cs, own_cn, own_ids, finv, sinv, mid, own_panels, sel):
     col_count, row_count, block_rows, _ = gathered.shape
-    parts = 2
+    parts = 4
     tile = col_count * block_rows * parts
     grid_rows = col_count * block_rows * row_count
     out_rows = 2 * BLK + own_cs.shape[0]

time: 144 us -> 144 us (level)
  no operation moved by 1% of the time
where the time goes in v13:
time: 144 us
  Pallas kernels  67.3 us (47%)
  blocking collectives  29.6 us (21%)
  between operations  15 us (10%)
  waiting for transfers between devices  9.75 us (7%)
  local copies, waits for them, and re-layouts  9.39 us (7%)
  other arithmetic  7.22 us (5%)
  starting transfers between devices  3.49 us (2%)
  matrix products  2.1 us (1%)
    pallas_call x1, Pallas kernels, factor_centers(): pl.pallas_call(factor_kernel, out_shape=(jax.ShapeDtypeStruct((panel, pan...  39.1 us
    pallas_call x1, Pallas kernels, panel_stage(): pl.pallas_call(panel_kernel, grid=(row_count // parts,), in_specs=[pl.Blo...  28.2 us
    all_to_all x1, blocking collectives, gather_by_all_to_all(): return lax.all_to_all(copies, axis_name, 0, 0, tiled=True)  18.3 us
    all_to_all x1, blocking collectives, on_device(): moved = lax.all_to_all(blocks, 'row', 0, 0, tiled=True)  11.3 us
    all_to_all x1, waiting for transfers between devices, gather_by_all_to_all(): return lax.all_to_all(copies, axis_name, 0, 0, tiled=True)  7.9 us
    all_to_all x1, starting transfers between devices, gather_by_all_to_all(): return lax.all_to_all(copies, axis_name, 0, 0, tiled=True)  3.45 us
    unnamed x12, local copies, waits for them, and re-layouts  3.3 us
  transfers between devices with their start and end apart: 2, of which 2 were waited for; matrix products, arithmetic and copies ran while one was open for 8% of the time, Pallas kernels for 27%

profile of v13, /device:TPU:1, one launch (start us, length us, event | category | flops | bytes accessed | tf_op | source)
XLA Modules:
  0.0 143.8 jit_solution(1829005024715985584)
XLA Ops:
  6.5 1.0 copy.38
  7.6 0.2 reshape.147
  7.8 11.3 %all_to_all.15 = f32[8,1,4096]{2,1,0:T(1,128)S(1)} all-to-all(f32[8,1,4096]{2,1,0:T(1,128)S(1)} %reshape.147), channel_id=1, replica_groups=mesh['row'=8,'col'=16] {'row'}, dimensions={0} | all-to-all | bytes 262144 | tf_op jit(solution)/shard_map/all_to_all | solution.py:238
  19.0 0.5 broadcast.120
  19.6 0.9 reduce.2
  20.5 0.1 reshape.148
  20.6 0.0 copy-start
  20.7 0.3 reshape.149
  21.0 18.3 %all_to_all.16 = f32[16,1,4096]{2,1,0:T(1,128)S(1)} all-to-all(f32[16,1,4096]{2,1,0:T(1,128)S(1)} %reshape.149), channel_id=1, replica_groups=mesh['row'=8,'col'=16] {'col'}, dimensions={0} | all-to-all | bytes 524288 | tf_op jit(solution)/shard_map/all_to_all | solution.py:221
  39.3 0.0 copy-start.2
  39.3 1.3 reduce.3
  40.6 0.2 reshape.150
  40.8 0.1 broadcast_in_dim.66
  40.9 1.2 reshape.151
  42.1 3.5 %all-to-all-start.2 = ((f32[8,1,12288]{2,1,0:T(1,128)}), f32[8,1,12288]{2,1,0:T(1,128)S(1)}, u32[]{:S(2)}, u32[]{:S(2)}) async-start(f32[8,1,12288]{2,1,0:T(1,128)} %reshape.151), calls=%async_computation.2 | async-start | bytes 786432 | tf_op jit(solution)/shard_map/all_to_all | solution.py:221
  45.6 0.0 all-gather.3.cloned.1.call-start
  45.7 7.9 %all-to-all-done.2 = f32[8,1,12288]{2,1,0:T(1,128)S(1)} async-done(((f32[8,1,12288]{2,1,0:T(1,128)}), f32[8,1,12288]{2,1,0:T(1,128)S(1)}, u32[]{:S(2)}, u32[]{:S(2)}) %all-to-all-start.2) | async-done | bytes 393248 | tf_op jit(solution)/shard_map/all_to_all | solution.py:221
  53.6 1.6 %reduce.4 = f32[8,12288]{1,0:T(8,128)S(1)} reduce(f32[8,1,12288]{2,1,0:T(1,128)S(1)} %all-to-all-done.2, f32[]{:T(128)} %broadcast.120), dimensions={1}, to_apply=%all_to_all.11.reduce_sub_computation | reduce | bytes 786436 | tf_op jit(solution)/shard_map/all_to_all | solution.py:221
  55.1 0.3 reshape.152
  55.5 0.1 copy.39
  55.5 0.0 copy-done
  55.5 0.0 all-gather.3.cloned.1.call-update
  55.6 0.1 iota_add_fusion.1
  55.6 0.1 reshape.125
  55.7 0.1 reshape.145.own_ids_ref
  55.8 0.0 copy-start.1
  57.1 0.1 iota_add_fusion
  57.2 0.7 add.122.pid_ref
  57.9 0.6 pad_maximum_fusion.1.consts_ref
  58.6 0.1 fusion.19
  58.7 0.7 select_convert_fusion.sel_ref
  59.3 0.0 copy-done.2
  59.3 0.3 multiply_reduce_fusion
  59.6 0.8 gather_fusion.1
  60.4 0.6 gather_fusion
  61.0 0.1 copy.43
  61.1 0.9 copy.47.cn_ref
  62.0 0.4 fusion.17
  62.4 0.1 copy.45
  62.5 0.1 copy.46
  62.7 0.1 fusion.18
  62.8 1.7 %fusion.4.used_ref = f32[320,512]{1,0:T(8,128)} fusion(f32[]{:T(128)} %bitcast.29, s32[320]{0:T(512)S(1)} %pad_add_fusion, f32[512]{0:T(512)S(1)} %slice.47, f32[320]{0:T(512)S(1)} %pad_maximum_fusion, f32[]{:T(128)} %bitcast.27, f32[1536,64]{1,0:T(8,128)S(1)} %get-tuple-element.22, f32[64,64]{1,0:T(8,128)S(1)} %get-tuple-element.20, f32[256,64]{1,0:T(8,128)S(1)} %slice.51), kind=kOutput, calls=%fused_computation.7 | convolution fusion | flops 127160320 | bytes 1087496 | tf_op jit(solution)/shard_map/dot_general | solution.py:18
  64.5 0.8 fusion.11.lead_ref
  65.3 39.1 %shard_map.46 = (f32[256,256]{1,0:T(8,128)}, f32[256,256]{1,0:T(8,128)}, bf16[256,256]{1,0:T(8,128)(2,1)}, bf16[64,512]{1,0:T(8,128)(2,1)}) custom-call(f32[256,256]{1,0:T(8,128)} %fusion.11.lead_ref, f32[320,512]{1,0:T(8,128)} %fusion.4.used_ref), custom_call_target="tpu_custom_call" | custom-call | tf_op jit(solution)/shard_map/pallas_call | solution.py:114
  104.4 0.7 concatenate.16.own_cs_ref
  105.1 0.1 fusion.5
  105.2 1.1 concatenate.15.cs_ref
  106.2 0.0 copy-done.1
  106.2 0.6 and_select_fusion.own_cn_ref
  106.9 1.8 %all-gather.3.cloned.1.call-done = f32[128,64,64]{2,1,0:T(8,128)} async-done(((f32[8,64,64]{2,1,0:T(8,128)}), f32[128,64,64]{2,1,0:T(8,128)}) %all-gather.3.cloned.1.call-update) | async-done | bytes 2097168 | tf_op jit(solution)/shard_map/all_gather | solution.py:245
  108.7 28.2 %shard_map.47 = f32[96,64,128]{2,1,0:T(8,128)} custom-call(f32[2]{0:T(128)} %pad_maximum_fusion.1.consts_ref, f32[16,8,64,64]{3,2,1,0:T(8,128)} %bitcast.30, s32[1,8192]{1,0:T(1,128)} %add.122.pid_ref, f32[1,64]{1,0:T(1,128)} %bitcast.36, bf16[512,384]{1,0:T(8,128)(2,1)} %concatenate.15.cs_ref, f32[512,1]{1,0:T(8,128)} %copy.47.cn_ref, ...), custom_call_target="tpu_custom_call" | custom-call | tf_op jit(solution)/shard_map/pallas_call | solution.py:200
  (16 shorter events, 0.1 us)
Async XLA Ops:
  20.6 34.9 %copy-start = (f32[8,64,64]{2,1,0:T(8,128)}, f32[8,64,64]{2,1,0:T(8,128)S(1)}, u32[]{:S(2)}) copy-start(f32[8,64,64]{2,1,0:T(8,128)S(1)} %reshape.148) | copy-start | bytes 393220
  39.3 20.0 %copy-start.2 = (f32[64]{0:T(128)S(1)}, f32[64]{0:T(128)}, u32[]{:S(2)}) copy-start(f32[64]{0:T(128)} %param.5) | copy-start | bytes 772
  42.1 11.4 %all-to-all-start.2 = ((f32[8,1,12288]{2,1,0:T(1,128)}), f32[8,1,12288]{2,1,0:T(1,128)S(1)}, u32[]{:S(2)}, u32[]{:S(2)}) async-start(f32[8,1,12288]{2,1,0:T(1,128)} %reshape.151), calls=%async_computation.2 | async-start | bytes 786432 | tf_op jit(solution)/shard_map/all_to_all | solution.py:221
  45.6 63.1 %all-gather.3.cloned.1.call-start = ((), (), s32[]{:S(2)}) async-start(), calls=%async_computation.3 | async-start | bytes 4456448 | tf_op jit(solution)/shard_map/all_gather | solution.py:245
  55.8 50.4 %copy-start.1 = (s32[64,1]{1,0:T(8,128)}, s32[64,1]{1,0:T(8,128)S(1)}, u32[]{:S(2)}) copy-start(s32[64,1]{1,0:T(8,128)S(1)} %reshape.145.own_ids_ref) | copy-start | bytes 772
Sparse Core Ops, SparseCore 0:
  55.7 52.9 all-gather.2

commit v14 on v12

--- a/solution.py
+++ b/solution.py
@@ -237,8 +237,13 @@
     blocks = points.reshape(row_count, block_rows, FEAT)
     moved = lax.all_to_all(blocks, "row", 0, 0, tiled=True)
 
-    first_slot = gather_by_all_to_all(moved[0], "col")[:center_sources]
-    center_grid = gather_by_all_to_all(first_slot, "row")
+    flat_slot = moved[0].reshape(1, -1)
+    first_slot = lax.all_to_all(
+        jnp.broadcast_to(flat_slot, (col_count, flat_slot.shape[1])), "col", 0, 0, tiled=True
+    )[:center_sources].reshape(1, -1)
+    center_grid = lax.all_to_all(
+        jnp.broadcast_to(first_slot, (row_count, first_slot.shape[1])), "row", 0, 0, tiled=True
+    ).reshape(row_count, center_sources, block_rows, FEAT)
     centers = center_grid.transpose(1, 0, 2, 3).reshape(SLAB, FEAT)
 
     moved, centers = lax.optimization_barrier((moved, centers))

time: 144 us -> 141 us (0.979)
  other arithmetic: 7.22 us -> 5.4 us
    unnamed x12 -> x8, local copies, waits for them, and re-layouts: 3.3 us -> 1.23 us
    all_to_all x2 -> x1, other arithmetic: 2.82 us -> 0.93 us  [on_device(): lax.all_to_all(jnp.broadcast_to(first_slot, (row_count, first_slot.shape[...]
  transfers between devices with their start and end apart: 2 -> 2, of which waited for: 2 -> 2; matrix products, arithmetic and copies ran while one was open for 8% -> 8% of each run, Pallas kernels for 27% -> 28%
where the time goes in v14:
time: 141 us
  Pallas kernels  67.1 us (48%)
  blocking collectives  29.6 us (21%)
  between operations  14.9 us (11%)
  waiting for transfers between devices  9.57 us (7%)
  local copies, waits for them, and re-layouts  8.7 us (6%)
  other arithmetic  5.4 us (4%)
  starting transfers between devices  3.49 us (2%)
  matrix products  2.1 us (1%)
    pallas_call x1, Pallas kernels, factor_centers(): pl.pallas_call(factor_kernel, out_shape=(jax.ShapeDtypeStruct((panel, pan...  39.3 us
    pallas_call x1, Pallas kernels, panel_stage(): pl.pallas_call(panel_kernel, grid=(row_count // parts,), in_specs=[pl.Blo...  27.8 us
    all_to_all x1, blocking collectives, on_device(): lax.all_to_all(jnp.broadcast_to(flat_slot, (col_count, flat_slot.shape[1]...  18.3 us
    all_to_all x1, blocking collectives, on_device(): moved = lax.all_to_all(blocks, 'row', 0, 0, tiled=True)  11.3 us
    all_to_all x1, waiting for transfers between devices, on_device(): lax.all_to_all(jnp.broadcast_to(first_slot, (row_count, first_slot.shape[...  7.9 us
    all_to_all x1, starting transfers between devices, on_device(): lax.all_to_all(jnp.broadcast_to(first_slot, (row_count, first_slot.shape[...  3.45 us
  transfers between devices with their start and end apart: 2, of which 2 were waited for; matrix products, arithmetic and copies ran while one was open for 8% of the time, Pallas kernels for 28%

profile of v14, /device:TPU:1, one launch (start us, length us, event | category | flops | bytes accessed | tf_op | source)
XLA Modules:
  0.0 140.9 jit_solution(8899004556331714000)
XLA Ops:
  6.5 0.0 copy-start.2
  6.5 1.0 copy.39
  7.6 0.2 reshape.171
  7.8 11.3 %all_to_all.17 = f32[8,1,4096]{2,1,0:T(1,128)S(1)} all-to-all(f32[8,1,4096]{2,1,0:T(1,128)S(1)} %reshape.171), channel_id=1, replica_groups=mesh['row'=8,'col'=16] {'row'}, dimensions={0} | all-to-all | bytes 262144 | tf_op jit(solution)/shard_map/all_to_all | solution.py:238
  19.0 0.5 broadcast.126
  19.5 1.0 reduce.3
  20.5 0.1 reshape.172
  20.6 0.0 copy-start
  20.6 0.1 broadcast_in_dim.65
  20.7 0.2 broadcast_in_dim.66
  20.9 18.3 %all_to_all.18 = f32[16,1,4096]{2,1,0:T(1,128)S(1)} all-to-all(f32[16,1,4096]{2,1,0:T(1,128)S(1)} %broadcast_in_dim.66), channel_id=1, replica_groups=mesh['row'=8,'col'=16] {'col'}, dimensions={0} | all-to-all | bytes 524288 | tf_op jit(solution)/shard_map/all_to_all | solution.py:241
  39.2 0.9 broadcast_in_dim.68
  40.2 3.5 %all-to-all-start.2 = ((f32[8,1,12288]{2,1,0:T(1,128)}), f32[8,1,12288]{2,1,0:T(1,128)S(1)}, u32[]{:S(2)}, u32[]{:S(2)}) async-start(f32[8,1,12288]{2,1,0:T(1,128)} %broadcast_in_dim.68), calls=%async_computation.2 | async-start | bytes 786432 | tf_op jit(solution)/shard_map/all_to_all | solution.py:244
  43.6 0.0 all-gather.3.cloned.1.call-start
  43.7 7.9 %all-to-all-done.2 = f32[8,1,12288]{2,1,0:T(1,128)S(1)} async-done(((f32[8,1,12288]{2,1,0:T(1,128)}), f32[8,1,12288]{2,1,0:T(1,128)S(1)}, u32[]{:S(2)}, u32[]{:S(2)}) %all-to-all-start.2) | async-done | bytes 393248 | tf_op jit(solution)/shard_map/all_to_all | solution.py:244
  51.6 0.9 reduce
  52.5 0.3 reshape.144
  52.8 0.1 copy.40
  52.9 0.0 copy-done
  52.9 0.0 all-gather.3.cloned.1.call-update
  52.9 0.1 iota_add_fusion.1
  53.0 0.1 reshape.148
  53.1 0.1 reshape.168.own_ids_ref
  53.2 0.0 copy-start.1
  54.5 0.1 iota_add_fusion
  54.6 0.7 add.122.pid_ref
  55.3 0.7 pad_maximum_fusion.1.consts_ref
  56.0 0.1 fusion.19
  56.1 0.7 select_convert_fusion.sel_ref
  56.8 0.0 copy-done.2
  56.8 0.3 multiply_reduce_fusion
  57.1 0.8 gather_fusion.1
  57.9 0.6 gather_fusion
  58.5 0.1 copy.44
  58.6 0.9 copy.48.cn_ref
  59.5 0.4 fusion.17
  59.8 0.1 copy.46
  60.0 0.1 copy.47
  60.1 0.1 fusion.18
  60.2 1.7 %fusion.4.used_ref = f32[320,512]{1,0:T(8,128)} fusion(f32[]{:T(128)} %bitcast.28, s32[320]{0:T(512)S(1)} %pad_add_fusion, f32[512]{0:T(512)S(1)} %slice.48, f32[320]{0:T(512)S(1)} %pad_maximum_fusion, f32[]{:T(128)} %bitcast.26, f32[1536,64]{1,0:T(8,128)S(1)} %get-tuple-element.22, f32[64,64]{1,0:T(8,128)S(1)} %get-tuple-element.20, f32[256,64]{1,0:T(8,128)S(1)} %slice.52), kind=kOutput, calls=%fused_computation.7 | convolution fusion | flops 127160320 | bytes 1087496 | tf_op jit(solution)/shard_map/dot_general | solution.py:18
  61.9 0.8 fusion.11.lead_ref
  62.8 39.3 %shard_map.46 = (f32[256,256]{1,0:T(8,128)}, f32[256,256]{1,0:T(8,128)}, bf16[256,256]{1,0:T(8,128)(2,1)}, bf16[64,512]{1,0:T(8,128)(2,1)}) custom-call(f32[256,256]{1,0:T(8,128)} %fusion.11.lead_ref, f32[320,512]{1,0:T(8,128)} %fusion.4.used_ref), custom_call_target="tpu_custom_call" | custom-call | tf_op jit(solution)/shard_map/pallas_call | solution.py:114
  102.1 0.7 concatenate.16.own_cs_ref
  102.8 0.1 fusion.5
  102.9 1.1 concatenate.15.cs_ref
  103.9 0.0 copy-done.1
  103.9 0.6 and_select_fusion.own_cn_ref
  104.5 1.7 %all-gather.3.cloned.1.call-done = f32[128,64,64]{2,1,0:T(8,128)} async-done(((f32[8,64,64]{2,1,0:T(8,128)}), f32[128,64,64]{2,1,0:T(8,128)}) %all-gather.3.cloned.1.call-update) | async-done | bytes 2097168 | tf_op jit(solution)/shard_map/all_gather | solution.py:250
  106.2 27.8 %shard_map.47 = f32[96,64,128]{2,1,0:T(8,128)} custom-call(f32[2]{0:T(128)} %pad_maximum_fusion.1.consts_ref, f32[16,8,64,64]{3,2,1,0:T(8,128)} %bitcast.29, s32[1,8192]{1,0:T(1,128)} %add.122.pid_ref, f32[1,64]{1,0:T(1,128)} %bitcast.36, bf16[512,384]{1,0:T(8,128)(2,1)} %concatenate.15.cs_ref, f32[512,1]{1,0:T(8,128)} %copy.48.cn_ref, ...), custom_call_target="tpu_custom_call" | custom-call | tf_op jit(solution)/shard_map/pallas_call | solution.py:200
  (15 shorter events, 0.1 us)
Async XLA Ops:
  6.5 50.3 %copy-start.2 = (f32[64]{0:T(128)S(1)}, f32[64]{0:T(128)}, u32[]{:S(2)}) copy-start(f32[64]{0:T(128)} %param.5) | copy-start | bytes 772
  20.6 32.3 %copy-start = (f32[8,64,64]{2,1,0:T(8,128)}, f32[8,64,64]{2,1,0:T(8,128)S(1)}, u32[]{:S(2)}) copy-start(f32[8,64,64]{2,1,0:T(8,128)S(1)} %reshape.172) | copy-start | bytes 393220
  40.2 11.4 %all-to-all-start.2 = ((f32[8,1,12288]{2,1,0:T(1,128)}), f32[8,1,12288]{2,1,0:T(1,128)S(1)}, u32[]{:S(2)}, u32[]{:S(2)}) async-start(f32[8,1,12288]{2,1,0:T(1,128)} %broadcast_in_dim.68), calls=%async_computation.2 | async-start | bytes 786432 | tf_op jit(solution)/shard_map/all_to_all | solution.py:244
  43.6 62.5 %all-gather.3.cloned.1.call-start = ((), (), s32[]{:S(2)}) async-start(), calls=%async_computation.3 | async-start | bytes 4456448 | tf_op jit(solution)/shard_map/all_gather | solution.py:250
  53.2 50.7 %copy-start.1 = (s32[64,1]{1,0:T(8,128)}, s32[64,1]{1,0:T(8,128)S(1)}, u32[]{:S(2)}) copy-start(s32[64,1]{1,0:T(8,128)S(1)} %reshape.168.own_ids_ref) | copy-start | bytes 772
Sparse Core Ops, SparseCore 0:
  53.1 53.0 all-gather.2

commit v15 on v14

--- a/solution.py
+++ b/solution.py
@@ -237,6 +237,19 @@
     blocks = points.reshape(row_count, block_rows, FEAT)
     moved = lax.all_to_all(blocks, "row", 0, 0, tiled=True)
 
+    point_count = rows_one * col_count
+    point_ids = (
+        lax.broadcasted_iota(jnp.int32, (point_count // block_rows, block_rows), 0) * row_count
+        + row
+    ) * block_rows + lax.broadcasted_iota(jnp.int32, (point_count // block_rows, block_rows), 1)
+    point_ids = point_ids.reshape(1, point_count)
+    select = jnp.where(
+        lax.broadcasted_iota(jnp.int32, (BLK, PANEL), 1)
+        == column * BLK + lax.broadcasted_iota(jnp.int32, (BLK, PANEL), 0),
+        1.0,
+        0.0,
+    ).astype(jnp.bfloat16)
+    consts = jnp.stack([signal, jitter])
     flat_slot = moved[0].reshape(1, -1)
     first_slot = lax.all_to_all(
         jnp.broadcast_to(flat_slot, (col_count, flat_slot.shape[1])), "col", 0, 0, tiled=True
@@ -244,6 +257,9 @@
     center_grid = lax.all_to_all(
         jnp.broadcast_to(first_slot, (row_count, first_slot.shape[1])), "row", 0, 0, tiled=True
     ).reshape(row_count, center_sources, block_rows, FEAT)
+    point_ids, select, consts, center_grid = lax.optimization_barrier(
+        (point_ids, select, consts, center_grid)
+    )
     centers = center_grid.transpose(1, 0, 2, 3).reshape(SLAB, FEAT)
 
     moved, centers = lax.optimization_barrier((moved, centers))
@@ -253,11 +269,6 @@
     center_scaled = centers * feature_scales
     center_norms = jnp.sum(center_scaled * center_scaled, axis=1)
 
-    point_ids = (
-        lax.broadcasted_iota(jnp.int32, (grid_rows // block_rows, block_rows), 0) * row_count
-        + row
-    ) * block_rows + lax.broadcasted_iota(jnp.int32, (grid_rows // block_rows, block_rows), 1)
-    point_ids = point_ids.reshape(1, grid_rows)
 
     own_ids = (
         (
@@ -281,13 +292,6 @@
     ) + ridge_where(used_ids, jnp.arange(2 * PANEL, dtype=jnp.int32), jitter)
     first_inverse, second_inverse, first_mid, own_panels = factor_centers(k11, used_kernel)
 
-    select = jnp.where(
-        lax.broadcasted_iota(jnp.int32, (BLK, PANEL), 1)
-        == column * BLK + lax.broadcasted_iota(jnp.int32, (BLK, PANEL), 0),
-        1.0,
-        0.0,
-    ).astype(jnp.bfloat16)
-    consts = jnp.stack([signal, jitter])
     finished = panel_stage(
         consts,
         gathered,

time: 141 us -> 143 us (1.014)
  blocking collectives: 29.6 us -> 0 us
  starting transfers between devices: 3.49 us -> 19.3 us
  waiting for transfers between devices: 9.57 us -> 23.8 us
    all_to_all x2 -> x0, blocking collectives: 29.6 us -> none  [the longest x1 18.3 us: on_device(): lax.all_to_all(jnp.broadcast_to(flat_slot, (col_count, flat_slot.shape[1]...]
    all_to_all x0 -> x2, starting transfers between devices: none -> 15.8 us  [the longest x1 9.61 us: on_device(): lax.all_to_all(jnp.broadcast_to(flat_slot, (col_count, flat_slot.shape[1]...]
    all_to_all x0 -> x2, waiting for transfers between devices: none -> 14.1 us  [the longest x1 8.81 us: on_device(): lax.all_to_all(jnp.broadcast_to(flat_slot, (col_count, flat_slot.shape[1]...]
    all_gather x1, waiting for transfers between devices: 1.66 us -> 5.1 us  [on_device(): gathered = lax.all_gather(moved, 'col', axis=0, tiled=False)]
    all_to_all x1, waiting for transfers between devices: 7.9 us -> 4.66 us  [on_device(): lax.all_to_all(jnp.broadcast_to(first_slot, (row_count, first_slot.shape[...]
  transfers between devices with their start and end apart: 2 -> 4, of which waited for: 2 -> 4; matrix products, arithmetic and copies ran while one was open for 8% -> 8% of each run, Pallas kernels for 28% -> 28%
where the time goes in v15:
time: 143 us
  Pallas kernels  67.1 us (47%)
  waiting for transfers between devices  23.8 us (17%)
  starting transfers between devices  19.3 us (13%)
  between operations  14.9 us (10%)
  local copies, waits for them, and re-layouts  10.1 us (7%)
  other arithmetic  5.32 us (4%)
  matrix products  2.1 us (1%)
    pallas_call x1, Pallas kernels, factor_centers(): pl.pallas_call(factor_kernel, out_shape=(jax.ShapeDtypeStruct((panel, pan...  39.3 us
    pallas_call x1, Pallas kernels, panel_stage(): pl.pallas_call(panel_kernel, grid=(row_count // parts,), in_specs=[pl.Blo...  27.9 us
    all_to_all x1, starting transfers between devices, on_device(): lax.all_to_all(jnp.broadcast_to(flat_slot, (col_count, flat_slot.shape[1]...  9.61 us
    all_to_all x1, waiting for transfers between devices, on_device(): lax.all_to_all(jnp.broadcast_to(flat_slot, (col_count, flat_slot.shape[1]...  8.81 us
    all_to_all x1, starting transfers between devices, on_device(): moved = lax.all_to_all(blocks, 'row', 0, 0, tiled=True)  6.2 us
    all_to_all x1, waiting for transfers between devices, on_device(): moved = lax.all_to_all(blocks, 'row', 0, 0, tiled=True)  5.26 us
    all_gather x1, waiting for transfers between devices, on_device(): gathered = lax.all_gather(moved, 'col', axis=0, tiled=False)  5.1 us
    all_to_all x1, waiting for transfers between devices, on_device(): lax.all_to_all(jnp.broadcast_to(first_slot, (row_count, first_slot.shape[...  4.66 us
  transfers between devices with their start and end apart: 4, of which 4 were waited for; matrix products, arithmetic and copies ran while one was open for 8% of the time, Pallas kernels for 28%

profile of v15, /device:TPU:1, one launch (start us, length us, event | category | flops | bytes accessed | tf_op | source)
XLA Modules:
  0.0 142.7 jit_solution(11963803521732830874)
XLA Ops:
  6.5 0.0 copy-start.2
  6.5 1.0 copy.39
  7.6 0.8 reshape.171
  8.4 6.2 %all-to-all-start = ((f32[8,1,4096]{2,1,0:T(1,128)}), f32[8,1,4096]{2,1,0:T(1,128)S(1)}, u32[]{:S(2)}, u32[]{:S(2)}) async-start(f32[8,1,4096]{2,1,0:T(1,128)} %reshape.171), calls=%async_computation | async-start | bytes 262144 | tf_op jit(solution)/shard_map/all_to_all | solution.py:238
  14.6 5.3 %all-to-all-done = f32[8,1,4096]{2,1,0:T(1,128)S(1)} async-done(((f32[8,1,4096]{2,1,0:T(1,128)}), f32[8,1,4096]{2,1,0:T(1,128)S(1)}, u32[]{:S(2)}, u32[]{:S(2)}) %all-to-all-start) | async-done | bytes 131104 | tf_op jit(solution)/shard_map/all_to_all | solution.py:238
  19.9 0.5 broadcast.126
  20.4 1.0 reduce.3
  21.4 0.1 reshape.172
  21.5 0.0 copy-start
  21.5 0.1 broadcast_in_dim.67
  21.6 0.9 broadcast_in_dim.68
  22.5 9.6 %all-to-all-start.1 = ((f32[16,1,4096]{2,1,0:T(1,128)}), f32[16,1,4096]{2,1,0:T(1,128)S(1)}, u32[]{:S(2)}, u32[]{:S(2)}) async-start(f32[16,1,4096]{2,1,0:T(1,128)} %broadcast_in_dim.68), calls=%async_computation.1 | async-start | bytes 524288 | tf_op jit(solution)/shard_map/all_to_all | solution.py:254
  32.1 0.1 iota_add_fusion
  32.2 8.8 %all-to-all-done.1 = f32[16,1,4096]{2,1,0:T(1,128)S(1)} async-done(((f32[16,1,4096]{2,1,0:T(1,128)}), f32[16,1,4096]{2,1,0:T(1,128)S(1)}, u32[]{:S(2)}, u32[]{:S(2)}) %all-to-all-start.1) | async-done | bytes 262176 | tf_op jit(solution)/shard_map/all_to_all | solution.py:254
  41.0 0.9 broadcast_in_dim.70
  41.9 3.5 %all-to-all-start.2 = ((f32[8,1,12288]{2,1,0:T(1,128)}), f32[8,1,12288]{2,1,0:T(1,128)S(1)}, u32[]{:S(2)}, u32[]{:S(2)}) async-start(f32[8,1,12288]{2,1,0:T(1,128)} %broadcast_in_dim.70), calls=%async_computation.2 | async-start | bytes 786432 | tf_op jit(solution)/shard_map/all_to_all | solution.py:257
  45.4 0.0 all-gather.3.cloned.1.call-start
  46.7 0.7 add.122.pid_ref
  47.4 0.6 pad_maximum_fusion.1.consts_ref
  48.0 0.7 select_convert_fusion.sel_ref
  48.7 4.7 %all-to-all-done.2 = f32[8,1,12288]{2,1,0:T(1,128)S(1)} async-done(((f32[8,1,12288]{2,1,0:T(1,128)}), f32[8,1,12288]{2,1,0:T(1,128)S(1)}, u32[]{:S(2)}, u32[]{:S(2)}) %all-to-all-start.2) | async-done | bytes 393248 | tf_op jit(solution)/shard_map/all_to_all | solution.py:257
  53.4 0.9 reduce
  54.3 0.3 reshape.144
  54.6 0.1 copy.40
  54.7 0.0 copy-done
  54.7 0.0 all-gather.3.cloned.1.call-update
  54.7 0.1 iota_add_fusion.1
  54.8 0.1 reshape.148
  54.9 0.1 reshape.168.own_ids_ref
  55.0 0.0 copy-start.1
  55.0 0.1 fusion.19
  55.1 0.0 copy-done.2
  55.1 0.3 multiply_reduce_fusion
  55.4 0.8 gather_fusion.1
  56.2 0.6 gather_fusion
  56.8 0.1 copy.44
  56.9 0.9 copy.48.cn_ref
  57.8 0.4 fusion.17
  58.2 0.1 copy.46
  58.3 0.1 copy.47
  58.5 0.1 fusion.18
  58.6 1.7 %fusion.4.used_ref = f32[320,512]{1,0:T(8,128)} fusion(f32[]{:T(128)} %bitcast.28, s32[320]{0:T(512)S(1)} %pad_add_fusion, f32[512]{0:T(512)S(1)} %slice.48, f32[320]{0:T(512)S(1)} %pad_maximum_fusion, f32[]{:T(128)} %bitcast.26, f32[1536,64]{1,0:T(8,128)S(1)} %get-tuple-element.30, f32[64,64]{1,0:T(8,128)S(1)} %get-tuple-element.28, f32[256,64]{1,0:T(8,128)S(1)} %slice.52), kind=kOutput, calls=%fused_computation.7 | convolution fusion | flops 127160320 | bytes 1087496 | tf_op jit(solution)/shard_map/dot_general | solution.py:18
  60.3 0.8 fusion.11.lead_ref
  61.1 39.3 %shard_map.46 = (f32[256,256]{1,0:T(8,128)}, f32[256,256]{1,0:T(8,128)}, bf16[256,256]{1,0:T(8,128)(2,1)}, bf16[64,512]{1,0:T(8,128)(2,1)}) custom-call(f32[256,256]{1,0:T(8,128)} %fusion.11.lead_ref, f32[320,512]{1,0:T(8,128)} %fusion.4.used_ref), custom_call_target="tpu_custom_call" | custom-call | tf_op jit(solution)/shard_map/pallas_call | solution.py:114
  100.4 0.7 concatenate.16.own_cs_ref
  101.1 0.1 fusion.5
  101.2 1.1 concatenate.15.cs_ref
  102.2 0.0 copy-done.1
  102.2 0.6 and_select_fusion.own_cn_ref
  102.9 5.1 %all-gather.3.cloned.1.call-done = f32[128,64,64]{2,1,0:T(8,128)} async-done(((f32[8,64,64]{2,1,0:T(8,128)}), f32[128,64,64]{2,1,0:T(8,128)}) %all-gather.3.cloned.1.call-update) | async-done | bytes 2097168 | tf_op jit(solution)/shard_map/all_gather | solution.py:266
  108.0 27.9 %shard_map.47 = f32[96,64,128]{2,1,0:T(8,128)} custom-call(f32[2]{0:T(128)} %pad_maximum_fusion.1.consts_ref, f32[16,8,64,64]{3,2,1,0:T(8,128)} %bitcast.29, s32[1,8192]{1,0:T(1,128)} %add.122.pid_ref, f32[1,64]{1,0:T(1,128)} %bitcast.36, bf16[512,384]{1,0:T(8,128)(2,1)} %concatenate.15.cs_ref, f32[512,1]{1,0:T(8,128)} %copy.48.cn_ref, ...), custom_call_target="tpu_custom_call" | custom-call | tf_op jit(solution)/shard_map/pallas_call | solution.py:200
  (15 shorter events, 0.1 us)
Async XLA Ops:
  6.5 48.6 %copy-start.2 = (f32[64]{0:T(128)S(1)}, f32[64]{0:T(128)}, u32[]{:S(2)}) copy-start(f32[64]{0:T(128)} %param.5) | copy-start | bytes 772
  8.4 11.5 %all-to-all-start = ((f32[8,1,4096]{2,1,0:T(1,128)}), f32[8,1,4096]{2,1,0:T(1,128)S(1)}, u32[]{:S(2)}, u32[]{:S(2)}) async-start(f32[8,1,4096]{2,1,0:T(1,128)} %reshape.171), calls=%async_computation | async-start | bytes 262144 | tf_op jit(solution)/shard_map/all_to_all | solution.py:238
  21.5 33.2 %copy-start = (f32[8,64,64]{2,1,0:T(8,128)}, f32[8,64,64]{2,1,0:T(8,128)S(1)}, u32[]{:S(2)}) copy-start(f32[8,64,64]{2,1,0:T(8,128)S(1)} %reshape.172) | copy-start | bytes 393220
  22.5 18.5 %all-to-all-start.1 = ((f32[16,1,4096]{2,1,0:T(1,128)}), f32[16,1,4096]{2,1,0:T(1,128)S(1)}, u32[]{:S(2)}, u32[]{:S(2)}) async-start(f32[16,1,4096]{2,1,0:T(1,128)} %broadcast_in_dim.68), calls=%async_computation.1 | async-start | bytes 524288 | tf_op jit(solution)/shard_map/all_to_all | solution.py:254
  41.9 11.4 %all-to-all-start.2 = ((f32[8,1,12288]{2,1,0:T(1,128)}), f32[8,1,12288]{2,1,0:T(1,128)S(1)}, u32[]{:S(2)}, u32[]{:S(2)}) async-start(f32[8,1,12288]{2,1,0:T(1,128)} %broadcast_in_dim.70), calls=%async_computation.2 | async-start | bytes 786432 | tf_op jit(solution)/shard_map/all_to_all | solution.py:257
  45.4 62.6 %all-gather.3.cloned.1.call-start = ((), (), s32[]{:S(2)}) async-start(), calls=%async_computation.3 | async-start | bytes 4456448 | tf_op jit(solution)/shard_map/all_gather | solution.py:266
  55.0 47.3 %copy-start.1 = (s32[64,1]{1,0:T(8,128)}, s32[64,1]{1,0:T(8,128)S(1)}, u32[]{:S(2)}) copy-start(s32[64,1]{1,0:T(8,128)S(1)} %reshape.168.own_ids_ref) | copy-start | bytes 772
Sparse Core Ops, SparseCore 0:
  54.8 53.0 all-gather.2

commit v16 on v14

--- a/solution.py
+++ b/solution.py
@@ -234,10 +234,11 @@
     signal = amplitude[0]
     jitter = ridge[0]
 
-    blocks = points.reshape(row_count, block_rows, FEAT)
-    moved = lax.all_to_all(blocks, "row", 0, 0, tiled=True)
-
-    flat_slot = moved[0].reshape(1, -1)
+    blocks = points.reshape(row_count, block_rows * FEAT)
+    moved_flat = lax.all_to_all(blocks, "row", 0, 0, tiled=True)
+    moved = moved_flat.reshape(row_count, block_rows, FEAT)
+
+    flat_slot = moved_flat[:1]
     first_slot = lax.all_to_all(
         jnp.broadcast_to(flat_slot, (col_count, flat_slot.shape[1])), "col", 0, 0, tiled=True
     )[:center_sources].reshape(1, -1)

time: 141 us -> 140 us (level)
  transfers between devices with their start and end apart: 2 -> 2, of which waited for: 2 -> 2; matrix products, arithmetic and copies ran while one was open for 8% -> 9% of each run, Pallas kernels for 28% -> 28%
where the time goes in v16:
time: 140 us; the launch traced here: 139 us
  Pallas kernels  67.1 us (48%)
  blocking collectives  29.6 us (21%)
  between operations  14.9 us (11%)
  local copies, waits for them, and re-layouts  8.83 us (6%)
  waiting for transfers between devices  8.54 us (6%)
  other arithmetic  4.68 us (3%)
  starting transfers between devices  3.49 us (2%)
  matrix products  2.1 us (2%)
    pallas_call x1, Pallas kernels, factor_centers(): pl.pallas_call(factor_kernel, out_shape=(jax.ShapeDtypeStruct((panel, pan...  39.2 us
    pallas_call x1, Pallas kernels, panel_stage(): pl.pallas_call(panel_kernel, grid=(row_count // parts,), in_specs=[pl.Blo...  27.8 us
    all_to_all x1, blocking collectives, on_device(): lax.all_to_all(jnp.broadcast_to(flat_slot, (col_count, flat_slot.shape[1]...  18.3 us
    all_to_all x1, blocking collectives, on_device(): moved_flat = lax.all_to_all(blocks, 'row', 0, 0, tiled=True)  11.3 us
    all_to_all x1, waiting for transfers between devices, on_device(): lax.all_to_all(jnp.broadcast_to(first_slot, (row_count, first_slot.shape[...  6.77 us
    all_to_all x1, starting transfers between devices, on_device(): lax.all_to_all(jnp.broadcast_to(first_slot, (row_count, first_slot.shape[...  3.45 us
  transfers between devices with their start and end apart: 2, of which 2 were waited for; matrix products, arithmetic and copies ran while one was open for 9% of the time, Pallas kernels for 28%

profile of v16, /device:TPU:1, one launch (start us, length us, event | category | flops | bytes accessed | tf_op | source)
XLA Modules:
  0.0 139.2 jit_solution(7165911556500179771)
XLA Ops:
  6.5 0.0 copy-start.1
  6.5 1.0 copy.39
  7.6 0.2 all_to_all.18
  7.8 11.3 %all_to_all.22 = f32[8,1,4096]{2,1,0:T(1,128)S(1)} all-to-all(f32[8,1,4096]{2,1,0:T(1,128)S(1)} %all_to_all.18), channel_id=1, replica_groups=mesh['row'=8,'col'=16] {'row'}, dimensions={0} | all-to-all | bytes 262144 | tf_op jit(solution)/shard_map/all_to_all | solution.py:238
  19.0 0.2 broadcast_in_dim.63
  19.2 18.3 %all_to_all.23 = f32[16,1,4096]{2,1,0:T(1,128)S(1)} all-to-all(f32[16,1,4096]{2,1,0:T(1,128)S(1)} %broadcast_in_dim.63), channel_id=1, replica_groups=mesh['row'=8,'col'=16] {'col'}, dimensions={0} | all-to-all | bytes 524288 | tf_op jit(solution)/shard_map/all_to_all | solution.py:242
  37.6 0.9 broadcast_in_dim.65
  38.5 3.5 %all-to-all-start.2 = ((f32[8,1,12288]{2,1,0:T(1,128)}), f32[8,1,12288]{2,1,0:T(1,128)S(1)}, u32[]{:S(2)}, u32[]{:S(2)}) async-start(f32[8,1,12288]{2,1,0:T(1,128)} %broadcast_in_dim.65), calls=%async_computation.2 | async-start | bytes 786432 | tf_op jit(solution)/shard_map/all_to_all | solution.py:245
  42.0 0.0 all-gather.3.cloned.1.call-start
  42.0 0.3 reduce
  42.3 0.8 reshape.148
  43.2 6.8 %all-to-all-done.2 = f32[8,1,12288]{2,1,0:T(1,128)S(1)} async-done(((f32[8,1,12288]{2,1,0:T(1,128)}), f32[8,1,12288]{2,1,0:T(1,128)S(1)}, u32[]{:S(2)}, u32[]{:S(2)}) %all-to-all-start.2) | async-done | bytes 393248 | tf_op jit(solution)/shard_map/all_to_all | solution.py:245
  49.9 0.9 reduce.1
  50.9 0.3 reshape.149
  51.2 0.1 copy.41
  51.2 0.0 all-gather.3.cloned.1.call-update
  51.3 0.1 iota_add_fusion.1
  51.3 0.1 reshape.153
  51.4 0.1 reshape.173.own_ids_ref
  51.5 0.0 copy-start
  52.9 0.1 iota_add_fusion
  52.9 0.7 add.122.pid_ref
  53.7 0.6 pad_maximum_fusion.1.consts_ref
  54.2 0.1 fusion.19
  54.4 0.7 select_convert_fusion.sel_ref
  55.0 0.0 copy-done.1
  55.0 0.3 multiply_reduce_fusion
  55.3 0.8 gather_fusion.1
  56.1 0.6 gather_fusion
  56.7 0.1 copy.45
  56.8 0.9 copy.49.cn_ref
  57.7 0.4 fusion.17
  58.1 0.1 copy.47
  58.2 0.1 copy.48
  58.4 0.1 fusion.18
  58.5 1.7 %fusion.4.used_ref = f32[320,512]{1,0:T(8,128)} fusion(f32[]{:T(128)} %bitcast.28, s32[320]{0:T(512)S(1)} %pad_add_fusion, f32[512]{0:T(512)S(1)} %slice.52, f32[320]{0:T(512)S(1)} %pad_maximum_fusion, f32[]{:T(128)} %bitcast.26, f32[1536,64]{1,0:T(8,128)S(1)} %get-tuple-element.22, f32[64,64]{1,0:T(8,128)S(1)} %get-tuple-element.20, f32[256,64]{1,0:T(8,128)S(1)} %slice.56), kind=kOutput, calls=%fused_computation.7 | convolution fusion | flops 127160320 | bytes 1087496 | tf_op jit(solution)/shard_map/dot_general | solution.py:18
  60.2 0.8 fusion.11.lead_ref
  61.0 39.2 %shard_map.46 = (f32[256,256]{1,0:T(8,128)}, f32[256,256]{1,0:T(8,128)}, bf16[256,256]{1,0:T(8,128)(2,1)}, bf16[64,512]{1,0:T(8,128)(2,1)}) custom-call(f32[256,256]{1,0:T(8,128)} %fusion.11.lead_ref, f32[320,512]{1,0:T(8,128)} %fusion.4.used_ref), custom_call_target="tpu_custom_call" | custom-call | tf_op jit(solution)/shard_map/pallas_call | solution.py:114
  100.3 0.7 concatenate.16.own_cs_ref
  101.0 0.1 fusion.5
  101.1 1.1 concatenate.15.cs_ref
  102.1 0.0 copy-done
  102.1 0.6 and_select_fusion.own_cn_ref
  102.7 1.8 %all-gather.3.cloned.1.call-done = f32[128,64,64]{2,1,0:T(8,128)} async-done(((f32[8,64,64]{2,1,0:T(8,128)}), f32[128,64,64]{2,1,0:T(8,128)}) %all-gather.3.cloned.1.call-update) | async-done | bytes 2097168 | tf_op jit(solution)/shard_map/all_gather | solution.py:251
  104.5 27.8 %shard_map.47 = f32[96,64,128]{2,1,0:T(8,128)} custom-call(f32[2]{0:T(128)} %pad_maximum_fusion.1.consts_ref, f32[16,8,64,64]{3,2,1,0:T(8,128)} %bitcast.29, s32[1,8192]{1,0:T(1,128)} %add.122.pid_ref, f32[1,64]{1,0:T(1,128)} %bitcast.36, bf16[512,384]{1,0:T(8,128)(2,1)} %concatenate.15.cs_ref, f32[512,1]{1,0:T(8,128)} %copy.49.cn_ref, ...), custom_call_target="tpu_custom_call" | custom-call | tf_op jit(solution)/shard_map/pallas_call | solution.py:200
  (15 shorter events, 0.1 us)
Async XLA Ops:
  6.5 48.5 %copy-start.1 = (f32[64]{0:T(128)S(1)}, f32[64]{0:T(128)}, u32[]{:S(2)}) copy-start(f32[64]{0:T(128)} %param.5) | copy-start | bytes 772
  38.5 11.4 %all-to-all-start.2 = ((f32[8,1,12288]{2,1,0:T(1,128)}), f32[8,1,12288]{2,1,0:T(1,128)S(1)}, u32[]{:S(2)}, u32[]{:S(2)}) async-start(f32[8,1,12288]{2,1,0:T(1,128)} %broadcast_in_dim.65), calls=%async_computation.2 | async-start | bytes 786432 | tf_op jit(solution)/shard_map/all_to_all | solution.py:245
  42.0 62.5 %all-gather.3.cloned.1.call-start = ((), (), s32[]{:S(2)}) async-start(), calls=%async_computation.3 | async-start | bytes 4456448 | tf_op jit(solution)/shard_map/all_gather | solution.py:251
  51.5 50.6 %copy-start = (s32[64,1]{1,0:T(8,128)}, s32[64,1]{1,0:T(8,128)S(1)}, u32[]{:S(2)}) copy-start(s32[64,1]{1,0:T(8,128)S(1)} %reshape.173.own_ids_ref) | copy-start | bytes 772
Sparse Core Ops, SparseCore 0:
  51.4 53.0 all-gather.2

commit v17 on v16

--- a/solution.py
+++ b/solution.py
@@ -11,7 +11,7 @@
 BLK = 16
 
 HIGHEST = lax.Precision.HIGHEST
-PHASES = 8
+PHASES = 16
 
 
 def kernel_block(left, left_norms, right, right_norms, signal):

time: 140 us -> 140 us (level)
  no operation moved by 1% of the time
where the time goes in v17:
time: 140 us; the launch traced here: 139 us
  Pallas kernels  66.5 us (48%)
  blocking collectives  29.6 us (21%)
  between operations  14.9 us (11%)
  waiting for transfers between devices  9.31 us (7%)
  local copies, waits for them, and re-layouts  8.83 us (6%)
  other arithmetic  4.68 us (3%)
  starting transfers between devices  3.49 us (2%)
  matrix products  2.1 us (2%)
    pallas_call x1, Pallas kernels, factor_centers(): pl.pallas_call(factor_kernel, out_shape=(jax.ShapeDtypeStruct((panel, pan...  38.7 us
    pallas_call x1, Pallas kernels, panel_stage(): pl.pallas_call(panel_kernel, grid=(row_count // parts,), in_specs=[pl.Blo...  27.8 us
    all_to_all x1, blocking collectives, on_device(): lax.all_to_all(jnp.broadcast_to(flat_slot, (col_count, flat_slot.shape[1]...  18.3 us
    all_to_all x1, blocking collectives, on_device(): moved_flat = lax.all_to_all(blocks, 'row', 0, 0, tiled=True)  11.3 us
    all_to_all x1, waiting for transfers between devices, on_device(): lax.all_to_all(jnp.broadcast_to(first_slot, (row_count, first_slot.shape[...  6.77 us
    all_to_all x1, starting transfers between devices, on_device(): lax.all_to_all(jnp.broadcast_to(first_slot, (row_count, first_slot.shape[...  3.45 us
  transfers between devices with their start and end apart: 2, of which 2 were waited for; matrix products, arithmetic and copies ran while one was open for 9% of the time, Pallas kernels for 28%

profile of v17, /device:TPU:1, one launch (start us, length us, event | category | flops | bytes accessed | tf_op | source)
XLA Modules:
  0.0 139.4 jit_solution(11209261275483243605)
XLA Ops:
  6.5 0.0 copy-start.1
  6.5 1.0 copy.39
  7.6 0.2 all_to_all.18
  7.8 11.3 %all_to_all.22 = f32[8,1,4096]{2,1,0:T(1,128)S(1)} all-to-all(f32[8,1,4096]{2,1,0:T(1,128)S(1)} %all_to_all.18), channel_id=1, replica_groups=mesh['row'=8,'col'=16] {'row'}, dimensions={0} | all-to-all | bytes 262144 | tf_op jit(solution)/shard_map/all_to_all | solution.py:238
  19.0 0.2 broadcast_in_dim.63
  19.2 18.3 %all_to_all.23 = f32[16,1,4096]{2,1,0:T(1,128)S(1)} all-to-all(f32[16,1,4096]{2,1,0:T(1,128)S(1)} %broadcast_in_dim.63), channel_id=1, replica_groups=mesh['row'=8,'col'=16] {'col'}, dimensions={0} | all-to-all | bytes 524288 | tf_op jit(solution)/shard_map/all_to_all | solution.py:242
  37.6 0.9 broadcast_in_dim.65
  38.5 3.5 %all-to-all-start.2 = ((f32[8,1,12288]{2,1,0:T(1,128)}), f32[8,1,12288]{2,1,0:T(1,128)S(1)}, u32[]{:S(2)}, u32[]{:S(2)}) async-start(f32[8,1,12288]{2,1,0:T(1,128)} %broadcast_in_dim.65), calls=%async_computation.2 | async-start | bytes 786432 | tf_op jit(solution)/shard_map/all_to_all | solution.py:245
  42.0 0.0 all-gather.3.cloned.1.call-start
  42.0 0.3 reduce
  42.3 0.8 reshape.148
  43.2 6.8 %all-to-all-done.2 = f32[8,1,12288]{2,1,0:T(1,128)S(1)} async-done(((f32[8,1,12288]{2,1,0:T(1,128)}), f32[8,1,12288]{2,1,0:T(1,128)S(1)}, u32[]{:S(2)}, u32[]{:S(2)}) %all-to-all-start.2) | async-done | bytes 393248 | tf_op jit(solution)/shard_map/all_to_all | solution.py:245
  49.9 0.9 reduce.1
  50.9 0.3 reshape.149
  51.2 0.1 copy.41
  51.2 0.0 all-gather.3.cloned.1.call-update
  51.3 0.1 iota_add_fusion.1
  51.3 0.1 reshape.153
  51.4 0.1 reshape.173.own_ids_ref
  51.5 0.0 copy-start
  52.9 0.1 iota_add_fusion
  52.9 0.7 add.122.pid_ref
  53.7 0.6 pad_maximum_fusion.1.consts_ref
  54.2 0.1 fusion.19
  54.4 0.7 select_convert_fusion.sel_ref
  55.0 0.0 copy-done.1
  55.0 0.3 multiply_reduce_fusion
  55.3 0.8 gather_fusion.1
  56.1 0.6 gather_fusion
  56.7 0.1 copy.45
  56.8 0.9 copy.49.cn_ref
  57.7 0.4 fusion.17
  58.1 0.1 copy.47
  58.2 0.1 copy.48
  58.4 0.1 fusion.18
  58.5 1.7 %fusion.4.used_ref = f32[320,512]{1,0:T(8,128)} fusion(f32[]{:T(128)} %bitcast.28, s32[320]{0:T(512)S(1)} %pad_add_fusion, f32[512]{0:T(512)S(1)} %slice.52, f32[320]{0:T(512)S(1)} %pad_maximum_fusion, f32[]{:T(128)} %bitcast.26, f32[1536,64]{1,0:T(8,128)S(1)} %get-tuple-element.22, f32[64,64]{1,0:T(8,128)S(1)} %get-tuple-element.20, f32[256,64]{1,0:T(8,128)S(1)} %slice.56), kind=kOutput, calls=%fused_computation.7 | convolution fusion | flops 127160320 | bytes 1087496 | tf_op jit(solution)/shard_map/dot_general | solution.py:18
  60.2 0.8 fusion.11.lead_ref
  61.0 38.7 %shard_map.46 = (f32[256,256]{1,0:T(8,128)}, f32[256,256]{1,0:T(8,128)}, bf16[256,256]{1,0:T(8,128)(2,1)}, bf16[64,512]{1,0:T(8,128)(2,1)}) custom-call(f32[256,256]{1,0:T(8,128)} %fusion.11.lead_ref, f32[320,512]{1,0:T(8,128)} %fusion.4.used_ref), custom_call_target="tpu_custom_call" | custom-call | tf_op jit(solution)/shard_map/pallas_call | solution.py:114
  99.7 0.7 concatenate.16.own_cs_ref
  100.4 0.1 fusion.5
  100.5 1.1 concatenate.15.cs_ref
  101.5 0.0 copy-done
  101.5 0.6 and_select_fusion.own_cn_ref
  102.2 2.5 %all-gather.3.cloned.1.call-done = f32[128,64,64]{2,1,0:T(8,128)} async-done(((f32[8,64,64]{2,1,0:T(8,128)}), f32[128,64,64]{2,1,0:T(8,128)}) %all-gather.3.cloned.1.call-update) | async-done | bytes 2097168 | tf_op jit(solution)/shard_map/all_gather | solution.py:251
  104.7 27.8 %shard_map.47 = f32[96,64,128]{2,1,0:T(8,128)} custom-call(f32[2]{0:T(128)} %pad_maximum_fusion.1.consts_ref, f32[16,8,64,64]{3,2,1,0:T(8,128)} %bitcast.29, s32[1,8192]{1,0:T(1,128)} %add.122.pid_ref, f32[1,64]{1,0:T(1,128)} %bitcast.36, bf16[512,384]{1,0:T(8,128)(2,1)} %concatenate.15.cs_ref, f32[512,1]{1,0:T(8,128)} %copy.49.cn_ref, ...), custom_call_target="tpu_custom_call" | custom-call | tf_op jit(solution)/shard_map/pallas_call | solution.py:200
  (15 shorter events, 0.1 us)
Async XLA Ops:
  6.5 48.5 %copy-start.1 = (f32[64]{0:T(128)S(1)}, f32[64]{0:T(128)}, u32[]{:S(2)}) copy-start(f32[64]{0:T(128)} %param.5) | copy-start | bytes 772
  38.5 11.4 %all-to-all-start.2 = ((f32[8,1,12288]{2,1,0:T(1,128)}), f32[8,1,12288]{2,1,0:T(1,128)S(1)}, u32[]{:S(2)}, u32[]{:S(2)}) async-start(f32[8,1,12288]{2,1,0:T(1,128)} %broadcast_in_dim.65), calls=%async_computation.2 | async-start | bytes 786432 | tf_op jit(solution)/shard_map/all_to_all | solution.py:245
  42.0 62.7 %all-gather.3.cloned.1.call-start = ((), (), s32[]{:S(2)}) async-start(), calls=%async_computation.3 | async-start | bytes 4456448 | tf_op jit(solution)/shard_map/all_gather | solution.py:251
  51.5 50.0 %copy-start = (s32[64,1]{1,0:T(8,128)}, s32[64,1]{1,0:T(8,128)S(1)}, u32[]{:S(2)}) copy-start(s32[64,1]{1,0:T(8,128)S(1)} %reshape.173.own_ids_ref) | copy-start | bytes 772
Sparse Core Ops, SparseCore 0:
  51.4 53.2 all-gather.2

commit v18 on v16

--- a/solution.py
+++ b/solution.py
@@ -89,11 +89,12 @@
     return jnp.concatenate([top, jnp.concatenate([below, second], axis=1)], axis=0)
 
 
-def factor_kernel(lead_ref, used_ref, finv_ref, sinv_ref, mid_ref, own_ref, s_ref, x_ref):
-    first_inverse = lower_inverse_body(lead_ref[...], s_ref, x_ref)
+def factor_kernel(block_ref, finv_ref, sinv_ref, mid_ref, own_ref, s_ref, x_ref):
+    panel = finv_ref.shape[0]
+    lead = block_ref[:panel, :panel]
+    first_inverse = lower_inverse_body((lead + lead.T) * 0.5, s_ref, x_ref)
     finv_ref[...] = first_inverse
-    used = used_ref[...]
-    panel = first_inverse.shape[0]
+    used = block_ref[panel:, :]
     center_first = _nt(used[:, :panel], first_inverse).astype(jnp.bfloat16)
     first_mid = center_first[:panel]
     mid_ref[...] = first_mid
@@ -107,10 +108,10 @@
     own_ref[...] = jnp.concatenate([center_first[panel:], second_own], axis=1)
 
 
-def factor_centers(lead, used):
-    panel = lead.shape[0]
+def factor_centers(block):
+    panel = block.shape[1] // 2
     half = panel // 2
-    own_rows = used.shape[0] - panel
+    own_rows = block.shape[0] - 2 * panel
     return pl.pallas_call(
         factor_kernel,
         out_shape=(
@@ -120,7 +121,7 @@
             jax.ShapeDtypeStruct((own_rows, 2 * panel), jnp.bfloat16),
         ),
         scratch_shapes=[pltpu.VMEM((half, half), jnp.float32), pltpu.VMEM((half, half), jnp.float32)],
-    )((lead + lead.T) * 0.5, used)
+    )(block)
 
 
 def split_three(values):
@@ -270,17 +271,13 @@
     own_scaled = jnp.take(center_scaled, own_ids, axis=0)
     own_norms = jnp.take(center_norms, own_ids, axis=0)
 
-    lead_ids = jnp.arange(PANEL, dtype=jnp.int32)
-    k11 = kernel_block(
-        center_scaled[:PANEL], center_norms[:PANEL], center_scaled[:PANEL], center_norms[:PANEL], signal
-    ) + ridge_where(lead_ids, lead_ids, jitter)
-    used_ids = jnp.concatenate([jnp.arange(PANEL, 2 * PANEL, dtype=jnp.int32), own_ids])
-    used_scaled = jnp.concatenate([center_scaled[PANEL : 2 * PANEL], own_scaled])
-    used_norms = jnp.concatenate([center_norms[PANEL : 2 * PANEL], own_norms])
+    used_ids = jnp.concatenate([jnp.arange(2 * PANEL, dtype=jnp.int32), own_ids])
+    used_scaled = jnp.concatenate([center_scaled[: 2 * PANEL], own_scaled])
+    used_norms = jnp.concatenate([center_norms[: 2 * PANEL], own_norms])
     used_kernel = kernel_block(
         used_scaled, used_norms, center_scaled[: 2 * PANEL], center_norms[: 2 * PANEL], signal
     ) + ridge_where(used_ids, jnp.arange(2 * PANEL, dtype=jnp.int32), jitter)
-    first_inverse, second_inverse, first_mid, own_panels = factor_centers(k11, used_kernel)
+    first_inverse, second_inverse, first_mid, own_panels = factor_centers(used_kernel)
 
     select = jnp.where(
         lax.broadcasted_iota(jnp.int32, (BLK, PANEL), 1)

time: 140 us -> 139 us (level)
  transfers between devices with their start and end apart: 2 -> 2, of which waited for: 2 -> 2; matrix products, arithmetic and copies ran while one was open for 9% -> 8% of each run, Pallas kernels for 28% -> 28%
where the time goes in v18:
time: 139 us
  Pallas kernels  67.3 us (48%)
  blocking collectives  29.6 us (21%)
  between operations  14.9 us (11%)
  waiting for transfers between devices  9.02 us (6%)
  local copies, waits for them, and re-layouts  8.55 us (6%)
  other arithmetic  3.87 us (3%)
  starting transfers between devices  3.49 us (3%)
  matrix products  2.47 us (2%)
    pallas_call x1, Pallas kernels, factor_centers(): pl.pallas_call(factor_kernel, out_shape=(jax.ShapeDtypeStruct((panel, pan...  39.4 us
    pallas_call x1, Pallas kernels, panel_stage(): pl.pallas_call(panel_kernel, grid=(row_count // parts,), in_specs=[pl.Blo...  27.9 us
    all_to_all x1, blocking collectives, on_device(): lax.all_to_all(jnp.broadcast_to(flat_slot, (col_count, flat_slot.shape[1]...  18.3 us
    all_to_all x1, blocking collectives, on_device(): moved_flat = lax.all_to_all(blocks, 'row', 0, 0, tiled=True)  11.3 us
    all_to_all x1, waiting for transfers between devices, on_device(): lax.all_to_all(jnp.broadcast_to(first_slot, (row_count, first_slot.shape[...  6.77 us
    all_to_all x1, starting transfers between devices, on_device(): lax.all_to_all(jnp.broadcast_to(first_slot, (row_count, first_slot.shape[...  3.45 us
  transfers between devices with their start and end apart: 2, of which 2 were waited for; matrix products, arithmetic and copies ran while one was open for 8% of the time, Pallas kernels for 28%

profile of v18, /device:TPU:1, one launch (start us, length us, event | category | flops | bytes accessed | tf_op | source)
XLA Modules:
  0.0 139.1 jit_solution(6709575651200738908)
XLA Ops:
  6.5 1.0 copy.30
  7.6 0.2 all_to_all.18
  7.8 11.3 %all_to_all.22 = f32[8,1,4096]{2,1,0:T(1,128)S(1)} all-to-all(f32[8,1,4096]{2,1,0:T(1,128)S(1)} %all_to_all.18), channel_id=1, replica_groups=mesh['row'=8,'col'=16] {'row'}, dimensions={0} | all-to-all | bytes 262144 | tf_op jit(solution)/shard_map/all_to_all | solution.py:239
  19.0 0.2 broadcast_in_dim.51
  19.2 18.3 %all_to_all.23 = f32[16,1,4096]{2,1,0:T(1,128)S(1)} all-to-all(f32[16,1,4096]{2,1,0:T(1,128)S(1)} %broadcast_in_dim.51), channel_id=1, replica_groups=mesh['row'=8,'col'=16] {'col'}, dimensions={0} | all-to-all | bytes 524288 | tf_op jit(solution)/shard_map/all_to_all | solution.py:243
  37.5 0.9 broadcast_in_dim.53
  38.5 3.5 %all-to-all-start.2 = ((f32[8,1,12288]{2,1,0:T(1,128)}), f32[8,1,12288]{2,1,0:T(1,128)S(1)}, u32[]{:S(2)}, u32[]{:S(2)}) async-start(f32[8,1,12288]{2,1,0:T(1,128)} %broadcast_in_dim.53), calls=%async_computation.2 | async-start | bytes 786432 | tf_op jit(solution)/shard_map/all_to_all | solution.py:246
  41.9 0.0 all-gather.3.cloned.1.call-start
  42.0 0.3 reduce
  42.3 0.8 reshape.146
  43.1 6.8 %all-to-all-done.2 = f32[8,1,12288]{2,1,0:T(1,128)S(1)} async-done(((f32[8,1,12288]{2,1,0:T(1,128)}), f32[8,1,12288]{2,1,0:T(1,128)S(1)}, u32[]{:S(2)}, u32[]{:S(2)}) %all-to-all-start.2) | async-done | bytes 393248 | tf_op jit(solution)/shard_map/all_to_all | solution.py:246
  49.9 0.9 reduce.1
  50.8 0.3 reshape.147
  51.2 0.0 copy-start.1
  51.2 0.1 copy.32
  51.2 0.0 all-gather.3.cloned.1.call-update
  51.3 0.1 iota_add_fusion.1
  51.4 0.1 reshape.151
  51.5 0.1 reshape.171.own_ids_ref
  51.5 0.0 copy-start
  52.9 0.1 iota_add_fusion
  53.0 0.7 add.93.pid_ref
  53.7 0.6 pad_maximum_fusion.1.consts_ref
  54.3 0.1 fusion.10
  54.4 0.7 select_convert_fusion.sel_ref
  55.1 0.0 copy-done.1
  55.1 0.3 multiply_reduce_fusion
  55.4 0.8 gather_fusion.1
  56.2 0.6 gather_fusion
  56.8 0.1 copy.36
  56.8 0.9 copy.37.cn_ref
  57.7 0.1 fusion.9
  57.8 0.1 fusion.12
  57.9 2.5 %fusion.4.block_ref = f32[576,512]{1,0:T(8,128)} fusion(f32[512,64]{1,0:T(8,128)S(1)} %get-tuple-element.23, f32[]{:T(128)} %bitcast.13, s32[576]{0:T(1024)S(1)} %pad_add_fusion, f32[512]{0:T(512)S(1)} %slice.36, f32[576]{0:T(1024)S(1)} %pad_maximum_fusion, f32[]{:T(128)} %bitcast.12, f32[64,64]{1,0:T(8,128)S(1)} %get-tuple-element.20), kind=kOutput, calls=%fused_computation.7 | convolution fusion | flops 228888576 | bytes 1333768 | tf_op jit(solution)/shard_map/dot_general | solution.py:18
  60.4 39.4 %shard_map.46 = (f32[256,256]{1,0:T(8,128)}, f32[256,256]{1,0:T(8,128)}, bf16[256,256]{1,0:T(8,128)(2,1)}, bf16[64,512]{1,0:T(8,128)(2,1)}) custom-call(f32[576,512]{1,0:T(8,128)} %fusion.4.block_ref), custom_call_target="tpu_custom_call" | custom-call | tf_op jit(solution)/shard_map/pallas_call | solution.py:115
  99.8 0.7 concatenate.16.own_cs_ref
  100.5 1.0 concatenate.15.cs_ref
  101.6 0.0 copy-done
  101.6 0.6 and_select_fusion.own_cn_ref
  102.2 2.2 %all-gather.3.cloned.1.call-done = f32[128,64,64]{2,1,0:T(8,128)} async-done(((f32[8,64,64]{2,1,0:T(8,128)}), f32[128,64,64]{2,1,0:T(8,128)}) %all-gather.3.cloned.1.call-update) | async-done | bytes 2097168 | tf_op jit(solution)/shard_map/all_gather | solution.py:252
  104.4 27.9 %shard_map.47 = f32[96,64,128]{2,1,0:T(8,128)} custom-call(f32[2]{0:T(128)} %pad_maximum_fusion.1.consts_ref, f32[16,8,64,64]{3,2,1,0:T(8,128)} %bitcast.14, s32[1,8192]{1,0:T(1,128)} %add.93.pid_ref, f32[1,64]{1,0:T(1,128)} %bitcast.21, bf16[512,384]{1,0:T(8,128)(2,1)} %concatenate.15.cs_ref, f32[512,1]{1,0:T(8,128)} %copy.37.cn_ref, ...), custom_call_target="tpu_custom_call" | custom-call | tf_op jit(solution)/shard_map/pallas_call | solution.py:201
  (13 shorter events, 0.1 us)
Async XLA Ops:
  38.5 11.4 %all-to-all-start.2 = ((f32[8,1,12288]{2,1,0:T(1,128)}), f32[8,1,12288]{2,1,0:T(1,128)S(1)}, u32[]{:S(2)}, u32[]{:S(2)}) async-start(f32[8,1,12288]{2,1,0:T(1,128)} %broadcast_in_dim.53), calls=%async_computation.2 | async-start | bytes 786432 | tf_op jit(solution)/shard_map/all_to_all | solution.py:246
  41.9 62.5 %all-gather.3.cloned.1.call-start = ((), (), s32[]{:S(2)}) async-start(), calls=%async_computation.3 | async-start | bytes 4456448 | tf_op jit(solution)/shard_map/all_gather | solution.py:252
  51.2 3.9 %copy-start.1 = (f32[64]{0:T(128)S(1)}, f32[64]{0:T(128)}, u32[]{:S(2)}) copy-start(f32[64]{0:T(128)} %param.5) | copy-start | bytes 772
  51.5 50.1 %copy-start = (s32[64,1]{1,0:T(8,128)}, s32[64,1]{1,0:T(8,128)S(1)}, u32[]{:S(2)}) copy-start(s32[64,1]{1,0:T(8,128)S(1)} %reshape.171.own_ids_ref) | copy-start | bytes 772
Sparse Core Ops, SparseCore 0:
  51.4 53.0 all-gather.2
